TPU v7x, 512 devices: a whole 4x4x16 slice. The times are simulated.
512 devices in a mesh: patch: 8 (over y, core), au: 4 (over z_lo), vert: 16 (over x, z_hi).
Axes of the slice: x: 4, y: 4, z: 16 (z_hi: 4, z_lo: 4; z = z_hi * 4 + z_lo), core: 2. Of those that a mesh axis runs over, the one named last changes fastest.
Arguments:
- fields: bfloat16 [8, 8, 32, 256, 512], P('patch', None, None, 'vert', 'au'), may hold values from -6 to 6
- coef_u: float32 [3, 512], P(None, 'au'), may hold values from 0.1 to 0.3
- coef_v: float32 [3, 256], P(None, 'vert'), may hold values from 0.1 to 0.3
- coef_w: float32 [3, 32], replicated, may hold values from 0.1 to 0.3
- orient: int32 [8, 2], replicated, may hold values from 0 to 1
- link: int32 [8], replicated, may hold values from 1 to 4
Outputs:
- design: float32 [8, 4, 32, 64], P('patch', None, 'vert', 'au')
All inputs are finite; a program needn't handle non-finite values.
Results may differ from a plain program's by a relative error of at most 0.0003.
Values may be sent and summed in bfloat16 or wider, within the bound.
No kernel may reach another device: no remote copies, remote signals or barrier semaphores. Data moves between devices by JAX's collectives and lax.ppermute only.
A program may use at most 128 MiB of HBM per device.

v0:
```python
import jax
import jax.numpy as jnp
from jax import lax
from jax.sharding import PartitionSpec as P

RATIO = 8


def with_halo(block, sides, width):
    for axis, dim in sides:
        count = lax.axis_size(axis)
        forward = [(i, i + 1) for i in range(count - 1)]
        backward = [(target, source) for source, target in forward]
        low = lax.ppermute(
            lax.slice_in_dim(block, block.shape[dim] - width, None, axis=dim), axis, forward
        )
        high = lax.ppermute(lax.slice_in_dim(block, 0, width, axis=dim), axis, backward)
        block = jnp.concatenate([low, block, high], axis=dim)
    return block


def from_behind(block, axis, distance):
    devices = range(lax.axis_size(axis))
    route = [((i - distance) % len(devices), i) for i in devices]
    return lax.ppermute(block, axis, route)


def field_density(extended, width, reach, layers_w, rows_v, rows_u):
    padded = jnp.pad(extended, ((0, 0), (2, 2), (0, 0), (0, 0)))
    channels = extended.shape[0]
    anchor = (0, 2, width - reach, width - reach)
    extent = (channels, layers_w, rows_v + 2 * reach, rows_u + 2 * reach)

    def shifted(direction, offset):
        corner_at = list(anchor)
        corner_at[direction] = corner_at[direction] + offset
        limit_at = tuple((b + s for b, s in zip(corner_at, extent)))
        return lax.slice(padded, tuple(corner_at), limit_at).astype(jnp.float32)

    centre = shifted(1, 0)
    product_sum = jnp.zeros(extent[1:], jnp.float32)
    div_flow = jnp.zeros(extent[1:], jnp.float32)
    div_adjoint = jnp.zeros(extent[1:], jnp.float32)
    for direction in (1, 2, 3):
        slopes = (
            8.0 * (shifted(direction, 1) - shifted(direction, -1))
            - (shifted(direction, 2) - shifted(direction, -2))
        ) / 12.0
        component = 3 - direction
        for k in range(3):
            product_sum = product_sum + slopes[k] * slopes[4 + k]
        div_flow = div_flow + slopes[component]
        div_adjoint = div_adjoint + slopes[4 + component]
    return product_sum - centre[3] * div_adjoint - centre[7] * div_flow


def blur(widened):
    padded = jnp.pad(widened, ((1, 1), (0, 0), (0, 0)))
    along_w = (padded[:-2] + 4.0 * padded[1:-1] + padded[2:]) / 6.0
    along_v = (along_w[:, :-2] + 4.0 * along_w[:, 1:-1] + along_w[:, 2:]) / 6.0
    return (along_v[:, :, :-2] + 4.0 * along_v[:, :, 1:-1] + along_v[:, :, 2:]) / 6.0


def band_matrix(coef_in, columns, offset):
    row_count = coef_in.shape[1]
    target = (jnp.arange(row_count) // RATIO)[:, None] + offset
    column = jnp.arange(columns)[None, :]
    result = jnp.zeros((row_count, columns), jnp.float32)
    for d in range(3):
        result = result + jnp.where(column == target + (d - 1), coef_in[d][:, None], 0.0)
    return result


def fold_vert(partial_value):
    widened = with_halo(partial_value, (("vert", 1),), 2)
    interior = widened[:, 4:-4]
    interior = interior.at[:, :2].add(widened[:, :2])
    return interior.at[:, -2:].add(widened[:, -2:])


def fold_first(partial_value):
    widened = with_halo(partial_value, (("au", 2),), 2)
    interior = widened[:, :, 4:-4]
    interior = interior.at[:, :, :2].add(widened[:, :, :2])
    return interior.at[:, :, -2:].add(widened[:, :, -2:])


def shards(fields, coef_u, coef_v, coef_w, orient, link):
    highest = lax.Precision.HIGHEST
    stacked = fields[0]
    layers_w = stacked.shape[1]
    rows_v = stacked.shape[2]
    rows_u = stacked.shape[3]
    columns_v = rows_v // RATIO + 4
    columns_u = rows_u // RATIO + 4
    extended = with_halo(stacked, (("au", 3), ("vert", 2)), 2)
    density = field_density(extended, 2, 0, layers_w, rows_v, rows_u)
    widened = with_halo(density, (("au", 2), ("vert", 1)), 1)
    smooth = blur(widened)
    mat_v = band_matrix(coef_v, columns_v, 2)
    mat_u = band_matrix(coef_u, columns_u, 2)
    mat_w = band_matrix(coef_w, layers_w // RATIO, 0)
    reduced = jnp.einsum("wvu,wa->avu", smooth, mat_w, precision=highest)
    reduced = fold_vert(jnp.einsum("avu,vb->abu", reduced, mat_v, precision=highest))
    reduced = fold_first(jnp.einsum("abu,uc->abc", reduced, mat_u, precision=highest))
    patch_index = lax.axis_index("patch")
    patches = lax.axis_size("patch")
    layers_d = reduced.shape[0]
    out_index = jnp.where(orient[patch_index, 0] == 1, 0, layers_d - 1).astype(jnp.int32)
    in_index = jnp.where(orient[patch_index, 1] == 1, layers_d - 1, 0).astype(jnp.int32)
    layer_ids = jnp.arange(layers_d)
    out_mask = (layer_ids == out_index).astype(jnp.float32)[:, None, None]
    in_mask = (layer_ids == in_index).astype(jnp.float32)[:, None, None]
    out_face = jnp.sum(out_mask * reduced, axis=0)
    in_face = jnp.sum(in_mask * reduced, axis=0)
    gate_here = link[patch_index].astype(jnp.float32)
    gate_before = link[(patch_index + patches - 1) % patches].astype(jnp.float32)
    from_before = from_behind(out_face * gate_here, "patch", 1)
    from_after = from_behind(in_face * gate_before, "patch", -1)
    design = reduced + in_mask * from_before[None] + out_mask * from_after[None]
    return design[None]


def solution(mesh):
    placed = (P("patch", None, None, "vert", "au"), P(None, "au"), P(None, "vert"), P(), P(), P())
    return jax.shard_map(
        shards,
        mesh=mesh,
        in_specs=placed,
        out_specs=P("patch", None, "vert", "au"),
        check_vma=False,
    )
```

profile of v0, /device:TPU:6, one launch (start us, length us, event | category | flops | bytes accessed | tf_op | source)
XLA Modules:
  0.0 160.9 jit_solution(8669139225313745885)
XLA Ops:
  0.0 6.0 %copy.43 = bf16[1,8,32,16,128]{2,3,4,1,0:T(8,128)(2,1)} copy(bf16[1,8,32,16,128]{4,3,2,1,0:T(8,128)(2,1)} %param.18) | data formatting | bytes 2097152 | tf_op args[0]
  6.0 1.0 fusion.80
  7.0 4.0 %collective-permute-start = (bf16[8,32,16,2]{1,2,3,0:T(8,128)(2,1)S(1)}, bf16[8,32,16,2]{1,2,3,0:T(8,128)(2,1)S(1)}, u32[]{:S(2)}, u32[]{:S(2)}) collective-permute-start(bf16[8,32,16,2]{1,2,3,0:T(8,128)(2,1)S(1)} %get-tuple-element.76), channel_id=1, source_target_pairs={{0,16},{16,32},{32,48},{1,17},{17,33},{33,49},{2,18},{18,34},{34,5... | collective-permute-start | bytes 49160 | tf_op jit(solution)/shard_map/ppermute | solution.py:14
  11.0 1.3 collective-permute-start.1
  12.3 6.2 %bitcast_convert_fusion = f32[8,32,16,128]{1,2,3,0:T(8,128)} fusion(bf16[1,8,32,16,128]{2,3,4,1,0:T(8,128)(2,1)} %copy.43), kind=kLoop, calls=%fused_computation.159 | loop fusion | flops 524288 | bytes 3145728 | tf_op jit(solution)/shard_map/convert_element_type | solution.py:38
  18.6 1.3 pad_maximum_fusion.5
  19.9 0.5 copy.44
  20.5 9.1 %collective-permute-start.2 = (bf16[8,32,2,132]{3,1,2,0:T(8,128)(2,1)S(1)}, bf16[8,32,2,132]{3,1,2,0:T(8,128)(2,1)S(1)}, u32[]{:S(2)}, u32[]{:S(2)}) collective-permute-start(bf16[8,32,2,132]{3,1,2,0:T(8,128)(2,1)S(1)} %copy.44), channel_id=1, source_target_pairs={{0,1},{1,2},{2,3},{3,4},{4,5},{5,6},{6,7},{7,8},{8,9},{9,10},{10,1... | collective-permute-start | bytes 405512 | tf_op jit(solution)/shard_map/ppermute | solution.py:14
  29.6 0.5 copy.45
  30.1 4.9 %collective-permute-start.3 = (bf16[8,32,2,132]{3,1,2,0:T(8,128)(2,1)S(1)}, bf16[8,32,2,132]{3,1,2,0:T(8,128)(2,1)S(1)}, u32[]{:S(2)}, u32[]{:S(2)}) collective-permute-start(bf16[8,32,2,132]{3,1,2,0:T(8,128)(2,1)S(1)} %copy.45), channel_id=1, source_target_pairs={{1,0},{2,1},{3,2},{4,3},{5,4},{6,5},{7,6},{8,7},{9,8},{10,9},{11,1... | collective-permute-start | bytes 405512 | tf_op jit(solution)/shard_map/ppermute | solution.py:17
  35.1 0.7 constant_dynamic-slice_fusion.1
  37.0 1.9 %collective-permute-done.2 = bf16[8,32,2,132]{3,1,2,0:T(8,128)(2,1)S(1)} collective-permute-done((bf16[8,32,2,132]{3,1,2,0:T(8,128)(2,1)S(1)}, bf16[8,32,2,132]{3,1,2,0:T(8,128)(2,1)S(1)}, u32[]{:S(2)}, u32[]{:S(2)}) %collective-permute-start.2) | collective-permute-done | bytes 135200 | tf_op jit(solution)/shard_map/ppermute | solution.py:14
  38.9 0.6 copy.46
  39.5 9.7 %collective-permute-done.3 = bf16[8,32,2,132]{3,1,2,0:T(8,128)(2,1)S(1)} collective-permute-done((bf16[8,32,2,132]{3,1,2,0:T(8,128)(2,1)S(1)}, bf16[8,32,2,132]{3,1,2,0:T(8,128)(2,1)S(1)}, u32[]{:S(2)}, u32[]{:S(2)}) %collective-permute-start.3) | collective-permute-done | bytes 135200 | tf_op jit(solution)/shard_map/ppermute | solution.py:17
  49.2 0.6 copy.47
  49.8 7.5 %pad_maximum_fusion = (bf16[8,32,18,132]{1,2,3,0:T(8,128)(2,1)S(1)}, bf16[8,32,18,132]{1,2,3,0:T(8,128)(2,1)S(1)}) fusion(bf16[8,32,2,132]{1,2,3,0:T(2,128)(2,1)S(1)} %copy.47, bf16[8,32,16,2]{1,2,3,0:T(8,128)(2,1)S(1)} %collective-permute-done.1, bf16[8,32,16,128]{1,2,3,0:T(8,128)(2,1)} %bitcast.41, bf16[8,32,16,2]{1,2,3,0:T(8,128)(2,1)S(1)} %collective-permute-done, ...), kind=kLoop, calls=%fused_computation.13 | loop fusion | flops 9732096 | bytes 3784704 | tf_op jit(solution)/shard_map/concatenate | solution.py:18
  57.3 6.5 %subtract_multiply_fusion.1 = f32[8,32,16,128]{1,2,3,0:T(8,128)} fusion(bf16[8,32,18,132]{1,2,3,0:T(8,128)(2,1)S(1)} %get-tuple-element.72, bf16[8,32,18,132]{1,2,3,0:T(8,128)(2,1)S(1)} %get-tuple-element.71), kind=kLoop, calls=%fused_computation.4 | loop fusion | flops 4718592 | bytes 6291456 | tf_op jit(solution)/shard_map/div | solution.py:45
  63.8 11.5 %select_maximum_fusion = bf16[8,36,20,132]{1,2,3,0:T(8,128)(2,1)S(1)} fusion(bf16[8,32,2,132]{1,2,3,0:T(2,128)(2,1)S(1)} %copy.47, bf16[8,32,2,132]{1,2,3,0:T(2,128)(2,1)S(1)} %copy.46, bf16[8,32,16,2]{1,2,3,0:T(8,128)(2,1)S(1)} %collective-permute-done.1, bf16[8,32,16,128]{1,2,3,0:T(8,128)(2,1)S(1)} %bitcast.43, ...), kind=kLoop, calls=%fused_computation.6 | loop fusion | flops 13685760 | bytes 2872320 | tf_op jit(solution)/shard_map/concatenate | solution.py:18
  75.4 10.9 %subtract_multiply_fusion = (f32[8,32,16,128]{1,2,3,0:T(8,128)}, f32[8,32,16,128]{1,2,3,0:T(8,128)}) fusion(bf16[8,32,16,2]{1,2,3,0:T(8,128)(2,1)S(1)} %collective-permute-done, bf16[8,32,16,128]{1,2,3,0:T(8,128)(2,1)S(1)} %bitcast.44, bf16[8,32,16,2]{1,2,3,0:T(8,128)(2,1)S(1)} %collective-permute-done.1, bf16[8,36,20,132]{1,2,3,0:T(8,128)(2,1)S(1)} %select_maximum_fusion), kind=kLoop, calls=%fused_computation.3 | loop fusion | flops 11534336 | bytes 9469952 | tf_op jit(solution)/shard_map/div | solution.py:45
  86.3 5.9 %fusion.9 = f32[32,16,128]{0,1,2:T(8,128)S(1)} fusion(f32[8,32,16,128]{1,2,3,0:T(8,128)} %bitcast_convert_fusion, f32[8,32,16,128]{1,2,3,0:T(8,128)} %get-tuple-element.98, f32[8,32,16,128]{1,2,3,0:T(8,128)S(1)} %bitcast.46, f32[8,32,16,128]{1,2,3,0:T(8,128)} %get-tuple-element.99), kind=kLoop, calls=%fused_computation.27 | loop fusion | flops 1638400 | bytes 5505024 | tf_op jit(solution)/shard_map/sub | solution.py:54
  92.2 16.2 %collective-permute-start.4 = (f32[32,16,1]{0,1,2:T(8,128)S(1)}, f32[32,16,1]{0,1,2:T(8,128)S(1)}, u32[]{:S(2)}, u32[]{:S(2)}) collective-permute-start(f32[32,16,1]{0,1,2:T(8,128)S(1)} %get-tuple-element.79), channel_id=1, source_target_pairs={{0,16},{16,32},{32,48},{1,17},{17,33},{33,49},{2,18},{18,34},{34,5... | collective-permute-start | bytes 6152 | tf_op jit(solution)/shard_map/ppermute | solution.py:14
  108.4 1.3 collective-permute-start.5
  109.8 4.2 %collective-permute-done.5 = f32[32,16,1]{0,1,2:T(8,128)S(1)} collective-permute-done((f32[32,16,1]{0,1,2:T(8,128)S(1)}, f32[32,16,1]{0,1,2:T(8,128)S(1)}, u32[]{:S(2)}, u32[]{:S(2)}) %collective-permute-start.5) | collective-permute-done | bytes 2080 | tf_op jit(solution)/shard_map/ppermute | solution.py:17
  114.1 0.1 fusion.81
  114.2 7.1 %collective-permute-start.6 = (f32[32,1,130]{0,1,2:T(1,128)S(1)}, f32[32,1,130]{0,1,2:T(1,128)S(1)}, u32[]{:S(2)}, u32[]{:S(2)}) collective-permute-start(f32[32,1,130]{0,1,2:T(1,128)S(1)} %get-tuple-element.77), channel_id=1, source_target_pairs={{0,1},{1,2},{2,3},{3,4},{4,5},{5,6},{6,7},{7,8},{8,9},{9,10},{10,1... | collective-permute-start | bytes 49928 | tf_op jit(solution)/shard_map/ppermute | solution.py:14
  121.3 3.5 %collective-permute-start.7 = (f32[32,1,130]{0,1,2:T(1,128)S(1)}, f32[32,1,130]{0,1,2:T(1,128)S(1)}, u32[]{:S(2)}, u32[]{:S(2)}) collective-permute-start(f32[32,1,130]{0,1,2:T(1,128)S(1)} %get-tuple-element.78), channel_id=1, source_target_pairs={{1,0},{2,1},{3,2},{4,3},{5,4},{6,5},{7,6},{8,7},{9,8},{10,9},{11,1... | collective-permute-start | bytes 49928 | tf_op jit(solution)/shard_map/ppermute | solution.py:17
  124.8 0.6 copy.51
  125.4 1.0 collective-permute-done.6
  126.5 6.9 %collective-permute-done.7 = f32[32,1,130]{0,1,2:T(1,128)S(1)} collective-permute-done((f32[32,1,130]{0,1,2:T(1,128)S(1)}, f32[32,1,130]{0,1,2:T(1,128)S(1)}, u32[]{:S(2)}, u32[]{:S(2)}) %collective-permute-start.7) | collective-permute-done | bytes 16672 | tf_op jit(solution)/shard_map/ppermute | solution.py:17
  133.6 0.2 fusion.21
  133.8 0.1 fusion.22
  133.8 0.4 fusion.25
  134.3 0.1 convolution_bitcast_fusion
  134.4 2.0 %collective-permute-start.8 = (f32[4,2,128]{2,1,0:T(2,128)S(1)}, f32[4,2,128]{2,1,0:T(2,128)S(1)}, u32[]{:S(2)}, u32[]{:S(2)}) collective-permute-start(f32[4,2,128]{2,1,0:T(2,128)S(1)} %get-tuple-element.81), channel_id=1, source_target_pairs={{0,1},{1,2},{2,3},{3,4},{4,5},{5,6},{6,7},{7,8},{8,9},{9,10},{10,1... | collective-permute-start | bytes 12296 | tf_op jit(solution)/shard_map/ppermute | solution.py:14
  136.5 8.6 %collective-permute-start.9 = (f32[4,2,128]{2,1,0:T(2,128)S(1)}, f32[4,2,128]{2,1,0:T(2,128)S(1)}, u32[]{:S(2)}, u32[]{:S(2)}) collective-permute-start(f32[4,2,128]{2,1,0:T(2,128)S(1)} %get-tuple-element.82), channel_id=1, source_target_pairs={{1,0},{2,1},{3,2},{4,3},{5,4},{6,5},{7,6},{8,7},{9,8},{10,9},{11,1... | collective-permute-start | bytes 12296 | tf_op jit(solution)/shard_map/ppermute | solution.py:17
  145.1 0.7 fusion.85
  147.1 0.2 fusion.33
  147.3 0.1 fusion.84
  147.5 2.5 %collective-permute-start.10 = (f32[4,2,2]{2,0,1:T(4,128)S(1)}, f32[4,2,2]{2,0,1:T(4,128)S(1)}, u32[]{:S(2)}, u32[]{:S(2)}) collective-permute-start(f32[4,2,2]{2,0,1:T(4,128)S(1)} %get-tuple-element.84), channel_id=1, source_target_pairs={{0,16},{16,32},{32,48},{1,17},{17,33},{33,49},{2,18},{18,34},{34,5... | collective-permute-start | bytes 200 | tf_op jit(solution)/shard_map/ppermute | solution.py:14
  149.9 1.3 collective-permute-start.11
  151.2 0.1 slice_add_fusion.3
  151.3 0.1 scatter-add.6
  151.4 4.0 %collective-permute-done.11 = f32[4,2,2]{2,0,1:T(4,128)S(1)} collective-permute-done((f32[4,2,2]{2,0,1:T(4,128)S(1)}, f32[4,2,2]{2,0,1:T(4,128)S(1)}, u32[]{:S(2)}, u32[]{:S(2)}) %collective-permute-start.11) | collective-permute-done | bytes 96 | tf_op jit(solution)/shard_map/ppermute | solution.py:17
  155.5 0.3 scatter-add.9
  155.8 0.1 multiply_reduce_fusion.1
  156.0 2.9 %collective-permute-start.13 = (f32[2,16]{1,0:T(2,128)S(1)}, f32[2,16]{1,0:T(2,128)S(1)}, u32[]{:S(2)}, u32[]{:S(2)}) collective-permute-start(f32[2,16]{1,0:T(2,128)S(1)} %broadcast_multiply_fusion), channel_id=1, source_target_pairs={{64,0},{128,64},{192,128},{256,192},{320,256},{384,320},{448,384},... | collective-permute-start | bytes 392 | tf_op jit(solution)/shard_map/ppermute | solution.py:25
  158.9 1.2 collective-permute-done.12
  160.3 0.6 copy.61
  (49 shorter events, 0.7 us)
Async XLA Ops:
  6.0 12.5 %copy-start.3 = (f32[3,32]{1,0:T(4,128)S(1)}, f32[3,32]{1,0:T(4,128)}, u32[]{:S(2)}) copy-start(f32[3,32]{1,0:T(4,128)} %param.21) | copy-start | bytes 1156
  6.0 12.6 %copy-start.4 = (f32[3,16]{1,0:T(4,128)S(1)}, f32[3,16]{1,0:T(4,128)}, u32[]{:S(2)}) copy-start(f32[3,16]{1,0:T(4,128)} %param.20) | copy-start | bytes 580
  6.0 12.6 %copy-start.5 = (f32[3,128]{1,0:T(4,128)S(1)}, f32[3,128]{1,0:T(4,128)}, u32[]{:S(2)}) copy-start(f32[3,128]{1,0:T(4,128)} %param.19) | copy-start | bytes 4612
  6.0 12.6 %copy-start = (bf16[1,8,32,16,128]{2,3,4,1,0:T(8,128)(2,1)S(1)}, bf16[1,8,32,16,128]{2,3,4,1,0:T(8,128)(2,1)}, u32[]{:S(2)}) copy-start(bf16[1,8,32,16,128]{2,3,4,1,0:T(8,128)(2,1)} %copy.43) | copy-start | bytes 3145732
  7.0 11.6 %collective-permute-start = (bf16[8,32,16,2]{1,2,3,0:T(8,128)(2,1)S(1)}, bf16[8,32,16,2]{1,2,3,0:T(8,128)(2,1)S(1)}, u32[]{:S(2)}, u32[]{:S(2)}) collective-permute-start(bf16[8,32,16,2]{1,2,3,0:T(8,128)(2,1)S(1)} %get-tuple-element.76), channel_id=1, source_target_pairs={{0,16},{16,32},{32,48},{1,17},{17,33},{33,49},{2,18},{18,34},{34,5... | collective-permute-start | bytes 49160 | tf_op jit(solution)/shard_map/ppermute | solution.py:14
  11.0 7.6 %collective-permute-start.1 = (bf16[8,32,16,2]{1,2,3,0:T(8,128)(2,1)S(1)}, bf16[8,32,16,2]{1,2,3,0:T(8,128)(2,1)S(1)}, u32[]{:S(2)}, u32[]{:S(2)}) collective-permute-start(bf16[8,32,16,2]{1,2,3,0:T(8,128)(2,1)S(1)} %get-tuple-element.75), channel_id=1, source_target_pairs={{16,0},{32,16},{48,32},{17,1},{33,17},{49,33},{18,2},{34,18},{50,3... | collective-permute-start | bytes 49160 | tf_op jit(solution)/shard_map/ppermute | solution.py:17
  18.5 16.6 %copy-start.6 = (s32[8,2]{0,1:T(2,128)S(1)}, s32[8,2]{0,1:T(2,128)}, u32[]{:S(2)}) copy-start(s32[8,2]{0,1:T(2,128)} %param.22) | copy-start | bytes 196
  20.5 18.4 %collective-permute-start.2 = (bf16[8,32,2,132]{3,1,2,0:T(8,128)(2,1)S(1)}, bf16[8,32,2,132]{3,1,2,0:T(8,128)(2,1)S(1)}, u32[]{:S(2)}, u32[]{:S(2)}) collective-permute-start(bf16[8,32,2,132]{3,1,2,0:T(8,128)(2,1)S(1)} %copy.44), channel_id=1, source_target_pairs={{0,1},{1,2},{2,3},{3,4},{4,5},{5,6},{6,7},{7,8},{8,9},{9,10},{10,1... | collective-permute-start | bytes 405512 | tf_op jit(solution)/shard_map/ppermute | solution.py:14
  30.1 19.1 %collective-permute-start.3 = (bf16[8,32,2,132]{3,1,2,0:T(8,128)(2,1)S(1)}, bf16[8,32,2,132]{3,1,2,0:T(8,128)(2,1)S(1)}, u32[]{:S(2)}, u32[]{:S(2)}) collective-permute-start(bf16[8,32,2,132]{3,1,2,0:T(8,128)(2,1)S(1)} %copy.45), channel_id=1, source_target_pairs={{1,0},{2,1},{3,2},{4,3},{5,4},{6,5},{7,6},{8,7},{9,8},{10,9},{11,1... | collective-permute-start | bytes 405512 | tf_op jit(solution)/shard_map/ppermute | solution.py:17
  57.3 6.5 %copy-start.1 = (bf16[1,8,32,16,128]{2,3,4,1,0:T(8,128)(2,1)S(1)}, bf16[1,8,32,16,128]{2,3,4,1,0:T(8,128)(2,1)}, u32[]{:S(2)}) copy-start(bf16[1,8,32,16,128]{2,3,4,1,0:T(8,128)(2,1)} %copy.43) | copy-start | bytes 3145732
  63.8 22.5 %slice-start = ((s8[8388608]{0:T(1024)(128)(4,1)}), s8[4194304]{0:T(1024)(128)(4,1)S(1)}, s32[]{:S(2)}) async-start(s8[8388608]{0:T(1024)(128)(4,1)} %bitcast.45), calls=%async_computation | async-start | bytes 8388608
  75.4 11.0 %slice-start.1 = ((s8[8388608]{0:T(1024)(128)(4,1)}), s8[4194304]{0:T(1024)(128)(4,1)S(1)}, s32[]{:S(2)}) async-start(s8[8388608]{0:T(1024)(128)(4,1)} %bitcast.45), calls=%async_computation.1 | async-start | bytes 8388608
  92.2 52.9 %copy-start.2 = (s32[8]{0:T(128)S(1)}, s32[8]{0:T(128)}, u32[]{:S(2)}) copy-start(s32[8]{0:T(128)} %param.23) | copy-start | bytes 100
  92.2 17.6 %collective-permute-start.4 = (f32[32,16,1]{0,1,2:T(8,128)S(1)}, f32[32,16,1]{0,1,2:T(8,128)S(1)}, u32[]{:S(2)}, u32[]{:S(2)}) collective-permute-start(f32[32,16,1]{0,1,2:T(8,128)S(1)} %get-tuple-element.79), channel_id=1, source_target_pairs={{0,16},{16,32},{32,48},{1,17},{17,33},{33,49},{2,18},{18,34},{34,5... | collective-permute-start | bytes 6152 | tf_op jit(solution)/shard_map/ppermute | solution.py:14
  108.4 5.5 %collective-permute-start.5 = (f32[32,16,1]{0,1,2:T(8,128)S(1)}, f32[32,16,1]{0,1,2:T(8,128)S(1)}, u32[]{:S(2)}, u32[]{:S(2)}) collective-permute-start(f32[32,16,1]{0,1,2:T(8,128)S(1)} %get-tuple-element.80), channel_id=1, source_target_pairs={{16,0},{32,16},{48,32},{17,1},{33,17},{49,33},{18,2},{34,18},{50,3... | collective-permute-start | bytes 6152 | tf_op jit(solution)/shard_map/ppermute | solution.py:17
  114.2 12.3 %collective-permute-start.6 = (f32[32,1,130]{0,1,2:T(1,128)S(1)}, f32[32,1,130]{0,1,2:T(1,128)S(1)}, u32[]{:S(2)}, u32[]{:S(2)}) collective-permute-start(f32[32,1,130]{0,1,2:T(1,128)S(1)} %get-tuple-element.77), channel_id=1, source_target_pairs={{0,1},{1,2},{2,3},{3,4},{4,5},{5,6},{6,7},{7,8},{8,9},{9,10},{10,1... | collective-permute-start | bytes 49928 | tf_op jit(solution)/shard_map/ppermute | solution.py:14
  121.3 12.1 %collective-permute-start.7 = (f32[32,1,130]{0,1,2:T(1,128)S(1)}, f32[32,1,130]{0,1,2:T(1,128)S(1)}, u32[]{:S(2)}, u32[]{:S(2)}) collective-permute-start(f32[32,1,130]{0,1,2:T(1,128)S(1)} %get-tuple-element.78), channel_id=1, source_target_pairs={{1,0},{2,1},{3,2},{4,3},{5,4},{6,5},{7,6},{8,7},{9,8},{10,9},{11,1... | collective-permute-start | bytes 49928 | tf_op jit(solution)/shard_map/ppermute | solution.py:17
  134.4 12.7 %collective-permute-start.8 = (f32[4,2,128]{2,1,0:T(2,128)S(1)}, f32[4,2,128]{2,1,0:T(2,128)S(1)}, u32[]{:S(2)}, u32[]{:S(2)}) collective-permute-start(f32[4,2,128]{2,1,0:T(2,128)S(1)} %get-tuple-element.81), channel_id=1, source_target_pairs={{0,1},{1,2},{2,3},{3,4},{4,5},{5,6},{6,7},{7,8},{8,9},{9,10},{10,1... | collective-permute-start | bytes 12296 | tf_op jit(solution)/shard_map/ppermute | solution.py:14
  136.5 10.7 %collective-permute-start.9 = (f32[4,2,128]{2,1,0:T(2,128)S(1)}, f32[4,2,128]{2,1,0:T(2,128)S(1)}, u32[]{:S(2)}, u32[]{:S(2)}) collective-permute-start(f32[4,2,128]{2,1,0:T(2,128)S(1)} %get-tuple-element.82), channel_id=1, source_target_pairs={{1,0},{2,1},{3,2},{4,3},{5,4},{6,5},{7,6},{8,7},{9,8},{10,9},{11,1... | collective-permute-start | bytes 12296 | tf_op jit(solution)/shard_map/ppermute | solution.py:17
  147.5 3.8 %collective-permute-start.10 = (f32[4,2,2]{2,0,1:T(4,128)S(1)}, f32[4,2,2]{2,0,1:T(4,128)S(1)}, u32[]{:S(2)}, u32[]{:S(2)}) collective-permute-start(f32[4,2,2]{2,0,1:T(4,128)S(1)} %get-tuple-element.84), channel_id=1, source_target_pairs={{0,16},{16,32},{32,48},{1,17},{17,33},{33,49},{2,18},{18,34},{34,5... | collective-permute-start | bytes 200 | tf_op jit(solution)/shard_map/ppermute | solution.py:14
  149.9 5.5 %collective-permute-start.11 = (f32[4,2,2]{2,0,1:T(4,128)S(1)}, f32[4,2,2]{2,0,1:T(4,128)S(1)}, u32[]{:S(2)}, u32[]{:S(2)}) collective-permute-start(f32[4,2,2]{2,0,1:T(4,128)S(1)} %get-tuple-element.83), channel_id=1, source_target_pairs={{16,0},{32,16},{48,32},{17,1},{33,17},{49,33},{18,2},{34,18},{50,3... | collective-permute-start | bytes 200 | tf_op jit(solution)/shard_map/ppermute | solution.py:17
  155.9 4.2 %collective-permute-start.12 = (f32[2,16]{1,0:T(2,128)S(1)}, f32[2,16]{1,0:T(2,128)S(1)}, u32[]{:S(2)}, u32[]{:S(2)}) collective-permute-start(f32[2,16]{1,0:T(2,128)S(1)} %broadcast_multiply_fusion.1), channel_id=1, source_target_pairs={{448,0},{0,64},{64,128},{128,192},{192,256},{256,320},{320,384},{3... | collective-permute-start | bytes 392 | tf_op jit(solution)/shard_map/ppermute | solution.py:25
  156.0 4.2 %collective-permute-start.13 = (f32[2,16]{1,0:T(2,128)S(1)}, f32[2,16]{1,0:T(2,128)S(1)}, u32[]{:S(2)}, u32[]{:S(2)}) collective-permute-start(f32[2,16]{1,0:T(2,128)S(1)} %broadcast_multiply_fusion), channel_id=1, source_target_pairs={{64,0},{128,64},{192,128},{256,192},{320,256},{384,320},{448,384},... | collective-permute-start | bytes 392 | tf_op jit(solution)/shard_map/ppermute | solution.py:25
where the time goes:
time: 162 us; the launch traced here: 161 us
  starting transfers between devices  64.8 us (40%)
  other arithmetic  50.6 us (31%)
  waiting for transfers between devices  29.1 us (18%)
  local copies, waits for them, and re-layouts  12.6 us (8%)
  between operations  3.08 us (2%)
    ppermute x6, starting transfers between devices, with_halo(): lax.ppermute(lax.slice_in_dim(block, block.shape[dim] - width, None, axis...  40.9 us
    ppermute x6, waiting for transfers between devices, with_halo(): lax.ppermute(lax.slice_in_dim(block, 0, width, axis=dim), axis, backward)  24.9 us
    ppermute x6, starting transfers between devices, with_halo(): lax.ppermute(lax.slice_in_dim(block, 0, width, axis=dim), axis, backward)  20.9 us
    concatenate x5, other arithmetic, with_halo(): block = jnp.concatenate([low, block, high], axis=dim)  20.4 us
    div x2, other arithmetic, field_density(): (8.0 * (shifted(direction, 1) - shifted(direction, -1)) - (shifted(direct...  17.5 us
    convert_element_type x1, other arithmetic, shifted(): return lax.slice(padded, tuple(corner_at), limit_at).astype(jnp.float32)  6.22 us
    unnamed x19, local copies, waits for them, and re-layouts  6.01 us
    sub x1, other arithmetic, field_density(): return product_sum - centre[3] * div_adjoint - centre[7] * div_flow  5.9 us
  transfers between devices with their start and end apart: 14, of which 8 were waited for; matrix products, arithmetic and copies ran while one was open for 6% of the time, Pallas kernels for 0%

commit v1 on v0

--- a/solution.py
+++ b/solution.py
@@ -93,10 +93,14 @@
     rows_u = stacked.shape[3]
     columns_v = rows_v // RATIO + 4
     columns_u = rows_u // RATIO + 4
-    extended = with_halo(stacked, (("au", 3), ("vert", 2)), 2)
-    density = field_density(extended, 2, 0, layers_w, rows_v, rows_u)
-    widened = with_halo(density, (("au", 2), ("vert", 1)), 1)
-    smooth = blur(widened)
+    extended = with_halo(stacked, (("au", 3), ("vert", 2)), 3)
+    density = field_density(extended, 3, 1, layers_w, rows_v, rows_u)
+    inside_v = lax.axis_index("vert") * rows_v + jnp.arange(-1, rows_v + 1)
+    inside_u = lax.axis_index("au") * rows_u + jnp.arange(-1, rows_u + 1)
+    keep_v = (inside_v >= 0) & (inside_v < rows_v * lax.axis_size("vert"))
+    keep_u = (inside_u >= 0) & (inside_u < rows_u * lax.axis_size("au"))
+    keep = keep_v[:, None] & keep_u[None, :]
+    smooth = blur(jnp.where(keep[None], density, 0.0))
     mat_v = band_matrix(coef_v, columns_v, 2)
     mat_u = band_matrix(coef_u, columns_u, 2)
     mat_w = band_matrix(coef_w, layers_w // RATIO, 0)

time: 162 us -> 122 us (0.75)
  other arithmetic: 50.6 us -> 17.8 us
  starting transfers between devices: 64.8 us -> 35.3 us
  waiting for transfers between devices: 29.1 us -> 43.1 us
  local copies, waits for them, and re-layouts: 12.6 us -> 20.1 us
    ppermute x6 -> x4, starting transfers between devices: 40.9 us -> 21.8 us  [with_halo(): lax.ppermute(lax.slice_in_dim(block, block.shape[dim] - width, None, axis...]
    concatenate x5 -> x2, other arithmetic: 20.4 us -> 3.28 us  [with_halo(): block = jnp.concatenate([low, block, high], axis=dim)]
    ppermute x6 -> x4, starting transfers between devices: 20.9 us -> 10.6 us  [with_halo(): lax.ppermute(lax.slice_in_dim(block, 0, width, axis=dim), axis, backward)]
    ppermute x6 -> x4, waiting for transfers between devices: 2.97 us -> 12.1 us  [with_halo(): lax.ppermute(lax.slice_in_dim(block, block.shape[dim] - width, None, axis...]
    div x2 -> x1, other arithmetic: 17.5 us -> 11.5 us  [field_density(): (8.0 * (shifted(direction, 1) - shifted(direction, -1)) - (shifted(direct...]
    sub x1 -> x0, other arithmetic: 5.9 us -> none  [field_density(): return product_sum - centre[3] * div_adjoint - centre[7] * div_flow]
    convert_element_type x1, other arithmetic: 6.22 us -> 0.94 us  [shifted(): return lax.slice(padded, tuple(corner_at), limit_at).astype(jnp.float32)]
    concatenate x1, local copies, waits for them, and re-layouts: 0.6 us -> 5.68 us  [with_halo(): block = jnp.concatenate([low, block, high], axis=dim)]
  transfers between devices with their start and end apart: 14 -> 10, of which waited for: 8 -> 7; matrix products, arithmetic and copies ran while one was open for 6% -> 7% of each run, Pallas kernels for 0% -> 0%
where the time goes in v1:
time: 122 us; the launch traced here: 120 us
  waiting for transfers between devices  43.1 us (35%)
  starting transfers between devices  35.3 us (29%)
  local copies, waits for them, and re-layouts  20.1 us (16%)
  other arithmetic  17.8 us (15%)
  between operations  3 us (2%)
    ppermute x4, waiting for transfers between devices, with_halo(): lax.ppermute(lax.slice_in_dim(block, 0, width, axis=dim), axis, backward)  29.7 us
    ppermute x4, starting transfers between devices, with_halo(): lax.ppermute(lax.slice_in_dim(block, block.shape[dim] - width, None, axis...  21.8 us
    ppermute x4, waiting for transfers between devices, with_halo(): lax.ppermute(lax.slice_in_dim(block, block.shape[dim] - width, None, axis...  12.1 us
    div x1, other arithmetic, field_density(): (8.0 * (shifted(direction, 1) - shifted(direction, -1)) - (shifted(direct...  11.5 us
    ppermute x4, starting transfers between devices, with_halo(): lax.ppermute(lax.slice_in_dim(block, 0, width, axis=dim), axis, backward)  10.6 us
    unnamed x13, local copies, waits for them, and re-layouts  8.01 us
    concatenate x1, local copies, waits for them, and re-layouts, with_halo(): block = jnp.concatenate([low, block, high], axis=dim)  5.68 us
    concatenate x2, other arithmetic, with_halo(): block = jnp.concatenate([low, block, high], axis=dim)  3.28 us
  transfers between devices with their start and end apart: 10, of which 7 were waited for; matrix products, arithmetic and copies ran while one was open for 7% of the time, Pallas kernels for 0%

profile of v1, /device:TPU:6, one launch (start us, length us, event | category | flops | bytes accessed | tf_op | source)
XLA Modules:
  0.0 120.0 jit_solution(15591895408731146337)
XLA Ops:
  0.0 6.0 %copy.24 = bf16[1,8,32,16,128]{2,3,4,1,0:T(8,128)(2,1)} copy(bf16[1,8,32,16,128]{4,3,2,1,0:T(8,128)(2,1)} %param.18) | data formatting | bytes 2097152 | tf_op args[0]
  6.0 1.0 fusion.76
  6.9 3.8 %collective-permute-start = (bf16[8,32,16,3]{1,2,3,0:T(8,128)(2,1)S(1)}, bf16[8,32,16,3]{1,2,3,0:T(8,128)(2,1)S(1)}, u32[]{:S(2)}, u32[]{:S(2)}) collective-permute-start(bf16[8,32,16,3]{1,2,3,0:T(8,128)(2,1)S(1)} %get-tuple-element.73), channel_id=1, source_target_pairs={{0,16},{16,32},{32,48},{1,17},{17,33},{33,49},{2,18},{18,34},{34,5... | collective-permute-start | bytes 73736 | tf_op jit(solution)/shard_map/ppermute | solution.py:14
  10.8 1.3 %collective-permute-start.1 = (bf16[8,32,16,3]{1,2,3,0:T(8,128)(2,1)S(1)}, bf16[8,32,16,3]{1,2,3,0:T(8,128)(2,1)S(1)}, u32[]{:S(2)}, u32[]{:S(2)}) collective-permute-start(bf16[8,32,16,3]{1,2,3,0:T(8,128)(2,1)S(1)} %get-tuple-element.74), channel_id=1, source_target_pairs={{16,0},{32,16},{48,32},{17,1},{33,17},{49,33},{18,2},{34,18},{50,3... | collective-permute-start | bytes 73736 | tf_op jit(solution)/shard_map/ppermute | solution.py:17
  12.2 0.6 constant_dynamic-slice_fusion.1
  14.1 0.1 broadcast_and_fusion
  14.2 3.1 %collective-permute-done.1 = bf16[8,32,16,3]{1,2,3,0:T(8,128)(2,1)S(1)} collective-permute-done((bf16[8,32,16,3]{1,2,3,0:T(8,128)(2,1)S(1)}, bf16[8,32,16,3]{1,2,3,0:T(8,128)(2,1)S(1)}, u32[]{:S(2)}, u32[]{:S(2)}) %collective-permute-start.1) | collective-permute-done | bytes 24608 | tf_op jit(solution)/shard_map/ppermute | solution.py:17
  17.3 2.7 %pad_maximum_fusion = bf16[8,32,16,134]{1,2,3,0:T(8,128)(2,1)S(1)} fusion(bf16[8,32,16,3]{1,2,3,0:T(8,128)(2,1)S(1)} %collective-permute-done.1, bf16[8,32,16,128]{1,2,3,0:T(8,128)(2,1)} %bitcast.42, bf16[8,32,16,3]{1,2,3,0:T(8,128)(2,1)S(1)} %collective-permute-done), kind=kLoop, calls=%fused_computation.3 | loop fusion | flops 1097728 | bytes 2195456 | tf_op jit(solution)/shard_map/concatenate | solution.py:18
  20.0 2.0 %copy-done = bf16[8,32,16,134]{1,2,3,0:T(8,128)(2,1)} copy-done((bf16[8,32,16,134]{1,2,3,0:T(8,128)(2,1)}, bf16[8,32,16,134]{1,2,3,0:T(8,128)(2,1)S(1)}, u32[]{:S(2)}) %copy-start) | copy-done | bytes 1097752
  22.1 0.8 fusion.75
  22.9 0.7 copy.25
  23.6 9.1 %collective-permute-start.2 = (bf16[8,32,3,134]{3,1,2,0:T(8,128)(2,1)S(1)}, bf16[8,32,3,134]{3,1,2,0:T(8,128)(2,1)S(1)}, u32[]{:S(2)}, u32[]{:S(2)}) collective-permute-start(bf16[8,32,3,134]{3,1,2,0:T(8,128)(2,1)S(1)} %copy.25), channel_id=1, source_target_pairs={{0,1},{1,2},{2,3},{3,4},{4,5},{5,6},{6,7},{7,8},{8,9},{9,10},{10,1... | collective-permute-start | bytes 617480 | tf_op jit(solution)/shard_map/ppermute | solution.py:14
  32.7 1.4 %copy.26 = bf16[8,32,3,134]{3,1,2,0:T(8,128)(2,1)} copy(bf16[8,32,3,134]{1,2,3,0:T(4,128)(2,1)S(1)} %get-tuple-element.72) | data formatting | bytes 411648 | tf_op jit(solution)/shard_map/slice | solution.py:17
  34.1 4.9 %collective-permute-start.3 = (bf16[8,32,3,134]{3,1,2,0:T(8,128)(2,1)}, bf16[8,32,3,134]{3,1,2,0:T(8,128)(2,1)S(1)}, u32[]{:S(2)}, u32[]{:S(2)}) collective-permute-start(bf16[8,32,3,134]{3,1,2,0:T(8,128)(2,1)} %copy.26), channel_id=1, source_target_pairs={{1,0},{2,1},{3,2},{4,3},{5,4},{6,5},{7,6},{8,7},{9,8},{10,9},{11,1... | collective-permute-start | bytes 617480 | tf_op jit(solution)/shard_map/ppermute | solution.py:17
  39.1 5.7 %copy.27 = bf16[8,32,16,134]{3,1,2,0:T(8,128)(2,1)S(1)} copy(bf16[8,32,16,134]{1,2,3,0:T(8,128)(2,1)} %copy-done) | data formatting | bytes 2195456 | tf_op jit(solution)/shard_map/concatenate | solution.py:18
  44.8 12.0 %collective-permute-done.2 = bf16[8,32,3,134]{3,1,2,0:T(8,128)(2,1)S(1)} collective-permute-done((bf16[8,32,3,134]{3,1,2,0:T(8,128)(2,1)S(1)}, bf16[8,32,3,134]{3,1,2,0:T(8,128)(2,1)S(1)}, u32[]{:S(2)}, u32[]{:S(2)}) %collective-permute-start.2) | collective-permute-done | bytes 205856 | tf_op jit(solution)/shard_map/ppermute | solution.py:14
  56.8 18.4 %collective-permute-done.3 = bf16[8,32,3,134]{3,1,2,0:T(8,128)(2,1)S(1)} collective-permute-done((bf16[8,32,3,134]{3,1,2,0:T(8,128)(2,1)}, bf16[8,32,3,134]{3,1,2,0:T(8,128)(2,1)S(1)}, u32[]{:S(2)}, u32[]{:S(2)}) %collective-permute-start.3) | collective-permute-done | bytes 205856 | tf_op jit(solution)/shard_map/ppermute | solution.py:17
  75.2 0.5 pad_maximum_fusion.1
  75.8 0.9 slice_convert_fusion
  76.7 11.5 %subtract_multiply_fusion.2 = (f32[8,32,18,130]{3,1,2,0:T(8,128)S(1)}, f32[8,32,18,130]{3,1,2,0:T(8,128)S(1)}, f32[8,32,18,130]{3,1,2,0:T(8,128)S(1)}) fusion(bf16[8,32,22,134]{3,1,2,0:T(8,128)(2,1)S(1)} %pad_maximum_fusion.1, bf16[8,32,16,134]{3,1,2,0:T(8,128)(2,1)S(1)} %copy.27, bf16[8,32,3,134]{3,1,2,0:T(8,128)(2,1)S(1)} %collective-permute-done.2, ...), kind=kLoop, calls=%fused_computation.2 | loop fusion | flops 23362560 | bytes 22392832 | tf_op jit(solution)/shard_map/div | solution.py:45
  88.2 0.0 copy-start.1
  88.2 1.5 %fusion.7 = f32[32,18,130]{2,0,1:T(8,128)S(1)} fusion(f32[8,32,18,130]{3,1,2,0:T(8,128)S(1)} %slice_convert_fusion, f32[8,32,18,130]{3,1,2,0:T(8,128)S(1)} %get-tuple-element.76, f32[8,32,18,130]{3,1,2,0:T(8,128)S(1)} %get-tuple-element.94, f32[8,32,18,130]{3,1,2,0:T(8,128)S(1)} %get-tuple-element.75, pred[18,130]{1,0:T(8,128)(4,1)S(1)} %broadcast_and_fusion), kind=kLoop, calls=%fused_computation.27 | loop fusion | flops 1946880 | bytes 6292260 | tf_op jit(solution)/shard_map/jit(_where)/select_n | solution.py:103
  89.6 0.2 fusion.4
  89.8 0.1 fusion.17
  89.9 0.4 fusion.20
  90.3 0.1 convolution_bitcast_fusion
  90.5 7.5 %collective-permute-start.4 = (f32[4,2,128]{2,1,0:T(2,128)S(1)}, f32[4,2,128]{2,1,0:T(2,128)S(1)}, u32[]{:S(2)}, u32[]{:S(2)}) collective-permute-start(f32[4,2,128]{2,1,0:T(2,128)S(1)} %get-tuple-element.77), channel_id=1, source_target_pairs={{0,1},{1,2},{2,3},{3,4},{4,5},{5,6},{6,7},{7,8},{8,9},{9,10},{10,1... | collective-permute-start | bytes 12296 | tf_op jit(solution)/shard_map/ppermute | solution.py:14
  98.0 3.1 %collective-permute-start.5 = (f32[4,2,128]{2,1,0:T(2,128)S(1)}, f32[4,2,128]{2,1,0:T(2,128)S(1)}, u32[]{:S(2)}, u32[]{:S(2)}) collective-permute-start(f32[4,2,128]{2,1,0:T(2,128)S(1)} %get-tuple-element.78), channel_id=1, source_target_pairs={{1,0},{2,1},{3,2},{4,3},{5,4},{6,5},{7,6},{8,7},{9,8},{10,9},{11,1... | collective-permute-start | bytes 12296 | tf_op jit(solution)/shard_map/ppermute | solution.py:17
  101.2 0.7 fusion.79
  103.2 4.2 %collective-permute-done.5 = f32[4,2,128]{2,1,0:T(2,128)S(1)} collective-permute-done((f32[4,2,128]{2,1,0:T(2,128)S(1)}, f32[4,2,128]{2,1,0:T(2,128)S(1)}, u32[]{:S(2)}, u32[]{:S(2)}) %collective-permute-start.5) | collective-permute-done | bytes 4128 | tf_op jit(solution)/shard_map/ppermute | solution.py:17
  107.5 0.2 fusion.28
  107.6 0.1 fusion.78
  107.7 0.1 slice.391
  107.8 1.3 %collective-permute-start.6 = (f32[4,2,2]{2,0,1:T(4,128)S(1)}, f32[4,2,2]{2,0,1:T(4,128)S(1)}, u32[]{:S(2)}, u32[]{:S(2)}) collective-permute-start(f32[4,2,2]{2,0,1:T(4,128)S(1)} %get-tuple-element.80), channel_id=1, source_target_pairs={{0,16},{16,32},{32,48},{1,17},{17,33},{33,49},{2,18},{18,34},{34,5... | collective-permute-start | bytes 200 | tf_op jit(solution)/shard_map/ppermute | solution.py:14
  109.1 1.3 %collective-permute-start.7 = (f32[4,2,2]{2,0,1:T(4,128)S(1)}, f32[4,2,2]{2,0,1:T(4,128)S(1)}, u32[]{:S(2)}, u32[]{:S(2)}) collective-permute-start(f32[4,2,2]{2,0,1:T(4,128)S(1)} %get-tuple-element.79), channel_id=1, source_target_pairs={{16,0},{32,16},{48,32},{17,1},{33,17},{49,33},{18,2},{34,18},{50,3... | collective-permute-start | bytes 200 | tf_op jit(solution)/shard_map/ppermute | solution.py:17
  110.4 0.0 collective-permute-done.6
  110.4 0.1 slice_add_fusion.3
  110.5 0.1 scatter-add.6
  110.6 4.0 %collective-permute-done.7 = f32[4,2,2]{2,0,1:T(4,128)S(1)} collective-permute-done((f32[4,2,2]{2,0,1:T(4,128)S(1)}, f32[4,2,2]{2,0,1:T(4,128)S(1)}, u32[]{:S(2)}, u32[]{:S(2)}) %collective-permute-start.7) | collective-permute-done | bytes 96 | tf_op jit(solution)/shard_map/ppermute | solution.py:17
  114.6 0.1 slice_add_fusion.2
  114.6 0.3 scatter-add.9
  115.0 0.1 multiply_reduce_fusion.1
  115.1 0.0 collective-permute-start.8
  115.1 2.9 %collective-permute-start.9 = (f32[2,16]{1,0:T(2,128)S(1)}, f32[2,16]{1,0:T(2,128)S(1)}, u32[]{:S(2)}, u32[]{:S(2)}) collective-permute-start(f32[2,16]{1,0:T(2,128)S(1)} %broadcast_multiply_fusion), channel_id=1, source_target_pairs={{64,0},{128,64},{192,128},{256,192},{320,256},{384,320},{448,384},... | collective-permute-start | bytes 392 | tf_op jit(solution)/shard_map/ppermute | solution.py:25
  118.1 1.2 %collective-permute-done.8 = f32[2,16]{1,0:T(2,128)S(1)} collective-permute-done((f32[2,16]{1,0:T(2,128)S(1)}, f32[2,16]{1,0:T(2,128)S(1)}, u32[]{:S(2)}, u32[]{:S(2)}) %collective-permute-start.8) | collective-permute-done | bytes 160 | tf_op jit(solution)/shard_map/ppermute | solution.py:25
  119.3 0.1 collective-permute-done.9
  119.4 0.1 multiply_add_fusion
  119.4 0.6 copy.38
  (28 shorter events, 0.1 us)
Async XLA Ops:
  0.0 12.1 %copy-start.2 = (f32[3,32]{1,0:T(4,128)S(1)}, f32[3,32]{1,0:T(4,128)}, u32[]{:S(2)}) copy-start(f32[3,32]{1,0:T(4,128)} %param.21) | copy-start | bytes 1156
  0.0 12.2 %copy-start.3 = (f32[3,16]{1,0:T(4,128)S(1)}, f32[3,16]{1,0:T(4,128)}, u32[]{:S(2)}) copy-start(f32[3,16]{1,0:T(4,128)} %param.20) | copy-start | bytes 580
  0.0 12.2 %copy-start.5 = (s32[8,2]{0,1:T(2,128)S(1)}, s32[8,2]{0,1:T(2,128)}, u32[]{:S(2)}) copy-start(s32[8,2]{0,1:T(2,128)} %param.22) | copy-start | bytes 196
  6.9 7.2 %collective-permute-start = (bf16[8,32,16,3]{1,2,3,0:T(8,128)(2,1)S(1)}, bf16[8,32,16,3]{1,2,3,0:T(8,128)(2,1)S(1)}, u32[]{:S(2)}, u32[]{:S(2)}) collective-permute-start(bf16[8,32,16,3]{1,2,3,0:T(8,128)(2,1)S(1)} %get-tuple-element.73), channel_id=1, source_target_pairs={{0,16},{16,32},{32,48},{1,17},{17,33},{33,49},{2,18},{18,34},{34,5... | collective-permute-start | bytes 73736 | tf_op jit(solution)/shard_map/ppermute | solution.py:14
  10.8 6.5 %collective-permute-start.1 = (bf16[8,32,16,3]{1,2,3,0:T(8,128)(2,1)S(1)}, bf16[8,32,16,3]{1,2,3,0:T(8,128)(2,1)S(1)}, u32[]{:S(2)}, u32[]{:S(2)}) collective-permute-start(bf16[8,32,16,3]{1,2,3,0:T(8,128)(2,1)S(1)} %get-tuple-element.74), channel_id=1, source_target_pairs={{16,0},{32,16},{48,32},{17,1},{33,17},{49,33},{18,2},{34,18},{50,3... | collective-permute-start | bytes 73736 | tf_op jit(solution)/shard_map/ppermute | solution.py:17
  20.0 2.0 %copy-start = (bf16[8,32,16,134]{1,2,3,0:T(8,128)(2,1)}, bf16[8,32,16,134]{1,2,3,0:T(8,128)(2,1)S(1)}, u32[]{:S(2)}) copy-start(bf16[8,32,16,134]{1,2,3,0:T(8,128)(2,1)S(1)} %pad_maximum_fusion) | copy-start | bytes 3293188
  22.1 17.0 %copy-start.4 = (f32[3,128]{1,0:T(4,128)S(1)}, f32[3,128]{1,0:T(4,128)}, u32[]{:S(2)}) copy-start(f32[3,128]{1,0:T(4,128)} %param.19) | copy-start | bytes 4612
  23.6 33.2 %collective-permute-start.2 = (bf16[8,32,3,134]{3,1,2,0:T(8,128)(2,1)S(1)}, bf16[8,32,3,134]{3,1,2,0:T(8,128)(2,1)S(1)}, u32[]{:S(2)}, u32[]{:S(2)}) collective-permute-start(bf16[8,32,3,134]{3,1,2,0:T(8,128)(2,1)S(1)} %copy.25), channel_id=1, source_target_pairs={{0,1},{1,2},{2,3},{3,4},{4,5},{5,6},{6,7},{7,8},{8,9},{9,10},{10,1... | collective-permute-start | bytes 617480 | tf_op jit(solution)/shard_map/ppermute | solution.py:14
  34.1 41.1 %collective-permute-start.3 = (bf16[8,32,3,134]{3,1,2,0:T(8,128)(2,1)}, bf16[8,32,3,134]{3,1,2,0:T(8,128)(2,1)S(1)}, u32[]{:S(2)}, u32[]{:S(2)}) collective-permute-start(bf16[8,32,3,134]{3,1,2,0:T(8,128)(2,1)} %copy.26), channel_id=1, source_target_pairs={{1,0},{2,1},{3,2},{4,3},{5,4},{6,5},{7,6},{8,7},{9,8},{10,9},{11,1... | collective-permute-start | bytes 617480 | tf_op jit(solution)/shard_map/ppermute | solution.py:17
  88.2 13.0 %copy-start.1 = (s32[8]{0:T(128)S(1)}, s32[8]{0:T(128)}, u32[]{:S(2)}) copy-start(s32[8]{0:T(128)} %param.23) | copy-start | bytes 100
  90.5 12.7 %collective-permute-start.4 = (f32[4,2,128]{2,1,0:T(2,128)S(1)}, f32[4,2,128]{2,1,0:T(2,128)S(1)}, u32[]{:S(2)}, u32[]{:S(2)}) collective-permute-start(f32[4,2,128]{2,1,0:T(2,128)S(1)} %get-tuple-element.77), channel_id=1, source_target_pairs={{0,1},{1,2},{2,3},{3,4},{4,5},{5,6},{6,7},{7,8},{8,9},{9,10},{10,1... | collective-permute-start | bytes 12296 | tf_op jit(solution)/shard_map/ppermute | solution.py:14
  98.0 9.4 %collective-permute-start.5 = (f32[4,2,128]{2,1,0:T(2,128)S(1)}, f32[4,2,128]{2,1,0:T(2,128)S(1)}, u32[]{:S(2)}, u32[]{:S(2)}) collective-permute-start(f32[4,2,128]{2,1,0:T(2,128)S(1)} %get-tuple-element.78), channel_id=1, source_target_pairs={{1,0},{2,1},{3,2},{4,3},{5,4},{6,5},{7,6},{8,7},{9,8},{10,9},{11,1... | collective-permute-start | bytes 12296 | tf_op jit(solution)/shard_map/ppermute | solution.py:17
  107.8 2.6 %collective-permute-start.6 = (f32[4,2,2]{2,0,1:T(4,128)S(1)}, f32[4,2,2]{2,0,1:T(4,128)S(1)}, u32[]{:S(2)}, u32[]{:S(2)}) collective-permute-start(f32[4,2,2]{2,0,1:T(4,128)S(1)} %get-tuple-element.80), channel_id=1, source_target_pairs={{0,16},{16,32},{32,48},{1,17},{17,33},{33,49},{2,18},{18,34},{34,5... | collective-permute-start | bytes 200 | tf_op jit(solution)/shard_map/ppermute | solution.py:14
  109.1 5.5 %collective-permute-start.7 = (f32[4,2,2]{2,0,1:T(4,128)S(1)}, f32[4,2,2]{2,0,1:T(4,128)S(1)}, u32[]{:S(2)}, u32[]{:S(2)}) collective-permute-start(f32[4,2,2]{2,0,1:T(4,128)S(1)} %get-tuple-element.79), channel_id=1, source_target_pairs={{16,0},{32,16},{48,32},{17,1},{33,17},{49,33},{18,2},{34,18},{50,3... | collective-permute-start | bytes 200 | tf_op jit(solution)/shard_map/ppermute | solution.py:17
  115.1 4.2 %collective-permute-start.8 = (f32[2,16]{1,0:T(2,128)S(1)}, f32[2,16]{1,0:T(2,128)S(1)}, u32[]{:S(2)}, u32[]{:S(2)}) collective-permute-start(f32[2,16]{1,0:T(2,128)S(1)} %broadcast_multiply_fusion.1), channel_id=1, source_target_pairs={{448,0},{0,64},{64,128},{128,192},{192,256},{256,320},{320,384},{3... | collective-permute-start | bytes 392 | tf_op jit(solution)/shard_map/ppermute | solution.py:25
  115.1 4.2 %collective-permute-start.9 = (f32[2,16]{1,0:T(2,128)S(1)}, f32[2,16]{1,0:T(2,128)S(1)}, u32[]{:S(2)}, u32[]{:S(2)}) collective-permute-start(f32[2,16]{1,0:T(2,128)S(1)} %broadcast_multiply_fusion), channel_id=1, source_target_pairs={{64,0},{128,64},{192,128},{256,192},{320,256},{384,320},{448,384},... | collective-permute-start | bytes 392 | tf_op jit(solution)/shard_map/ppermute | solution.py:25

commit v2 on v0

--- a/solution.py
+++ b/solution.py
@@ -85,6 +85,37 @@
     return interior.at[:, :, -2:].add(widened[:, :, -2:])
 
 
+def neighbour_rows(block, axis, dim, width):
+    count = lax.axis_size(axis)
+    forward = [(i, i + 1) for i in range(count - 1)]
+    backward = [(target, source) for source, target in forward]
+    low = lax.ppermute(
+        lax.slice_in_dim(block, block.shape[dim] - width, None, axis=dim), axis, forward
+    )
+    high = lax.ppermute(lax.slice_in_dim(block, 0, width, axis=dim), axis, backward)
+    return low, high
+
+
+def slopes_along(low, core, high, dim):
+    joined = jnp.concatenate([low, core, high], axis=dim)
+    length = core.shape[dim]
+
+    def shifted(offset):
+        return lax.slice_in_dim(joined, 2 + offset, 2 + offset + length, axis=dim)
+
+    return (8.0 * (shifted(1) - shifted(-1)) - (shifted(2) - shifted(-2))) / 12.0
+
+
+def smoothed_band(coef_ext, columns, offset):
+    rows = coef_ext.shape[1] - 2
+    target = jnp.floor_divide(jnp.arange(-1, rows + 1), RATIO)[:, None] + offset
+    column = jnp.arange(columns)[None, :]
+    band = jnp.zeros((rows + 2, columns), jnp.float32)
+    for d in range(3):
+        band = band + jnp.where(column == target + (d - 1), coef_ext[d][:, None], 0.0)
+    return (band[:-2] + 4.0 * band[1:-1] + band[2:]) / 6.0
+
+
 def shards(fields, coef_u, coef_v, coef_w, orient, link):
     highest = lax.Precision.HIGHEST
     stacked = fields[0]
@@ -93,14 +124,34 @@
     rows_u = stacked.shape[3]
     columns_v = rows_v // RATIO + 4
     columns_u = rows_u // RATIO + 4
-    extended = with_halo(stacked, (("au", 3), ("vert", 2)), 2)
-    density = field_density(extended, 2, 0, layers_w, rows_v, rows_u)
-    widened = with_halo(density, (("au", 2), ("vert", 1)), 1)
-    smooth = blur(widened)
-    mat_v = band_matrix(coef_v, columns_v, 2)
-    mat_u = band_matrix(coef_u, columns_u, 2)
-    mat_w = band_matrix(coef_w, layers_w // RATIO, 0)
-    reduced = jnp.einsum("wvu,wa->avu", smooth, mat_w, precision=highest)
+    moving = jnp.concatenate([stacked[0:3], stacked[4:7]], axis=0)
+    low_u, high_u = neighbour_rows(moving, "au", 3, 2)
+    low_v, high_v = neighbour_rows(moving, "vert", 2, 2)
+    coef_low_u, coef_high_u = neighbour_rows(coef_u, "au", 1, 1)
+    coef_low_v, coef_high_v = neighbour_rows(coef_v, "vert", 1, 1)
+    values = stacked.astype(jnp.float32)
+    moving = moving.astype(jnp.float32)
+    zero_w = jnp.zeros_like(moving[:, :2])
+    slopes = (
+        slopes_along(zero_w, moving, zero_w, 1),
+        slopes_along(low_v.astype(jnp.float32), moving, high_v.astype(jnp.float32), 2),
+        slopes_along(low_u.astype(jnp.float32), moving, high_u.astype(jnp.float32), 3),
+    )
+    product_sum = jnp.zeros(values.shape[1:], jnp.float32)
+    div_flow = jnp.zeros(values.shape[1:], jnp.float32)
+    div_adjoint = jnp.zeros(values.shape[1:], jnp.float32)
+    for direction, slope in enumerate(slopes):
+        component = 2 - direction
+        for k in range(3):
+            product_sum = product_sum + slope[k] * slope[3 + k]
+        div_flow = div_flow + slope[component]
+        div_adjoint = div_adjoint + slope[3 + component]
+    density = product_sum - values[3] * div_adjoint - values[7] * div_flow
+    zero_coef = jnp.zeros_like(coef_w[:, :1])
+    mat_w = smoothed_band(jnp.concatenate([zero_coef, coef_w, zero_coef], axis=1), layers_w // RATIO, 0)
+    mat_v = smoothed_band(jnp.concatenate([coef_low_v, coef_v, coef_high_v], axis=1), columns_v, 2)
+    mat_u = smoothed_band(jnp.concatenate([coef_low_u, coef_u, coef_high_u], axis=1), columns_u, 2)
+    reduced = jnp.einsum("wvu,wa->avu", density, mat_w, precision=highest)
     reduced = fold_vert(jnp.einsum("avu,vb->abu", reduced, mat_v, precision=highest))
     reduced = fold_first(jnp.einsum("abu,uc->abc", reduced, mat_u, precision=highest))
     patch_index = lax.axis_index("patch")

time: 162 us -> 104 us (0.64)
  other arithmetic: 50.6 us -> 12.1 us
  starting transfers between devices: 64.8 us -> 55.7 us
  waiting for transfers between devices: 29.1 us -> 20.2 us
  local copies, waits for them, and re-layouts: 12.6 us -> 10.2 us
    ppermute x0 -> x8, starting transfers between devices: none -> 36.9 us  [the longest x4 21.5 us: neighbour_rows(): lax.ppermute(lax.slice_in_dim(block, 0, width, axis=dim), axis, backward)]
    ppermute x6 -> x2, starting transfers between devices: 40.9 us -> 9.86 us  [with_halo(): lax.ppermute(lax.slice_in_dim(block, block.shape[dim] - width, None, axis...]
    concatenate x5 -> x4, other arithmetic: 20.4 us -> 0.66 us  [the longest x2 0.51 us: shards(): moving = jnp.concatenate([stacked[0:3], stacked[4:7]], axis=0)]
    ppermute x6 -> x2, waiting for transfers between devices: 24.9 us -> 8.61 us  [with_halo(): lax.ppermute(lax.slice_in_dim(block, 0, width, axis=dim), axis, backward)]
    ppermute x6 -> x2, starting transfers between devices: 20.9 us -> 6 us  [with_halo(): lax.ppermute(lax.slice_in_dim(block, 0, width, axis=dim), axis, backward)]
    div x4 -> x1, other arithmetic: 17.7 us -> 6.01 us  [slopes_along(): (8.0 * (shifted(1) - shifted(-1)) - (shifted(2) - shifted(-2))) / 12.0]
    ppermute x0 -> x8, waiting for transfers between devices: none -> 10.3 us  [the longest x4 9.06 us: neighbour_rows(): lax.ppermute(lax.slice_in_dim(block, 0, width, axis=dim), axis, backward)]
    sub x1, other arithmetic: 5.9 us -> 1.37 us  [shards(): density = product_sum - values[3] * div_adjoint - values[7] * div_flow]
  transfers between devices with their start and end apart: 14 -> 14, of which waited for: 8 -> 7; matrix products, arithmetic and copies ran while one was open for 6% -> 11% of each run, Pallas kernels for 0% -> 0%
where the time goes in v2:
time: 104 us; the launch traced here: 102 us
  starting transfers between devices  55.7 us (54%)
  waiting for transfers between devices  20.2 us (19%)
  other arithmetic  12.1 us (12%)
  local copies, waits for them, and re-layouts  10.2 us (10%)
  between operations  2.92 us (3%)
    ppermute x4, starting transfers between devices, neighbour_rows(): lax.ppermute(lax.slice_in_dim(block, 0, width, axis=dim), axis, backward)  21.5 us
    ppermute x4, starting transfers between devices, neighbour_rows(): lax.ppermute(lax.slice_in_dim(block, block.shape[dim] - width, None, axis...  15.4 us
    ppermute x2, starting transfers between devices, with_halo(): lax.ppermute(lax.slice_in_dim(block, block.shape[dim] - width, None, axis...  9.86 us
    ppermute x4, waiting for transfers between devices, neighbour_rows(): lax.ppermute(lax.slice_in_dim(block, 0, width, axis=dim), axis, backward)  9.06 us
    ppermute x2, waiting for transfers between devices, with_halo(): lax.ppermute(lax.slice_in_dim(block, 0, width, axis=dim), axis, backward)  8.61 us
    div x1, other arithmetic, slopes_along(): (8.0 * (shifted(1) - shifted(-1)) - (shifted(2) - shifted(-2))) / 12.0  6.01 us
    ppermute x2, starting transfers between devices, with_halo(): lax.ppermute(lax.slice_in_dim(block, 0, width, axis=dim), axis, backward)  6 us
    ppermute x2, starting transfers between devices, from_behind(): return lax.ppermute(block, axis, route)  2.95 us
  transfers between devices with their start and end apart: 14, of which 7 were waited for; matrix products, arithmetic and copies ran while one was open for 11% of the time, Pallas kernels for 0%

profile of v2, /device:TPU:6, one launch (start us, length us, event | category | flops | bytes accessed | tf_op | source)
XLA Modules:
  0.0 101.9 jit_solution(5915845458119738658)
XLA Ops:
  0.0 1.2 %slice_bitcast_fusion = (bf16[3,32,16,128]{3,2,1,0:T(8,128)(2,1)S(1)}, bf16[3,32,16,128]{3,2,1,0:T(8,128)(2,1)S(1)}) fusion(bf16[1,8,32,16,128]{4,3,2,1,0:T(8,128)(2,1)} %param.18), kind=kLoop, calls=%fused_computation.48 | loop fusion | bytes 1572864 | tf_op jit(solution)/shard_map/slice | solution.py:127
  1.3 0.3 fusion.19
  1.6 0.8 copy.38
  2.3 1.3 %collective-permute-start.4 = (bf16[6,32,16,2]{1,2,3,0:T(8,128)(2,1)S(1)}, bf16[6,32,16,2]{1,2,3,0:T(8,128)(2,1)}, u32[]{:S(2)}, u32[]{:S(2)}) collective-permute-start(bf16[6,32,16,2]{1,2,3,0:T(8,128)(2,1)S(1)} %copy.38), channel_id=1, source_target_pairs={{16,0},{32,16},{48,32},{17,1},{33,17},{49,33},{18,2},{34,18},{50,3... | collective-permute-start | bytes 36872 | tf_op jit(solution)/shard_map/ppermute | solution.py:95
  3.6 1.4 %copy.39 = bf16[6,32,16,2]{1,2,3,0:T(8,128)(2,1)} copy(bf16[6,32,16,2]{3,2,1,0:T(8,128)(2,1)S(1)} %get-tuple-element.79) | data formatting | bytes 24576
  5.0 5.3 %collective-permute-start.5 = (bf16[6,32,16,2]{1,2,3,0:T(8,128)(2,1)}, bf16[6,32,16,2]{1,2,3,0:T(8,128)(2,1)}, u32[]{:S(2)}, u32[]{:S(2)}) collective-permute-start(bf16[6,32,16,2]{1,2,3,0:T(8,128)(2,1)} %copy.39), channel_id=1, source_target_pairs={{0,16},{16,32},{32,48},{1,17},{17,33},{33,49},{2,18},{18,34},{34,5... | collective-permute-start | bytes 36872 | tf_op jit(solution)/shard_map/ppermute | solution.py:92
  10.3 0.2 fusion.37
  10.5 13.0 %collective-permute-start.2 = (bf16[6,32,2,128]{3,2,1,0:T(2,128)(2,1)S(1)}, bf16[6,32,2,128]{3,2,1,0:T(2,128)(2,1)S(1)}, u32[]{:S(2)}, u32[]{:S(2)}) collective-permute-start(bf16[6,32,2,128]{3,2,1,0:T(2,128)(2,1)S(1)} %get-tuple-element.76), channel_id=1, source_target_pairs={{1,0},{2,1},{3,2},{4,3},{5,4},{6,5},{7,6},{8,7},{9,8},{10,9},{11,1... | collective-permute-start | bytes 294920 | tf_op jit(solution)/shard_map/ppermute | solution.py:95
  23.5 1.9 %collective-permute-start.3 = (bf16[6,32,2,128]{3,2,1,0:T(2,128)(2,1)S(1)}, bf16[6,32,2,128]{3,2,1,0:T(2,128)(2,1)S(1)}, u32[]{:S(2)}, u32[]{:S(2)}) collective-permute-start(bf16[6,32,2,128]{3,2,1,0:T(2,128)(2,1)S(1)} %get-tuple-element.77), channel_id=1, source_target_pairs={{0,1},{1,2},{2,3},{3,4},{4,5},{5,6},{6,7},{7,8},{8,9},{9,10},{10,1... | collective-permute-start | bytes 294920 | tf_op jit(solution)/shard_map/ppermute | solution.py:92
  25.5 5.2 %collective-permute-start = (f32[3,1]{1,0:T(4,128)S(1)}, f32[3,1]{1,0:T(4,128)S(1)}, u32[]{:S(2)}, u32[]{:S(2)}) collective-permute-start(f32[3,1]{1,0:T(4,128)S(1)} %get-tuple-element.90), channel_id=1, source_target_pairs={{0,1},{1,2},{2,3},{3,4},{4,5},{5,6},{6,7},{7,8},{8,9},{9,10},{10,1... | collective-permute-start | bytes 44 | tf_op jit(solution)/shard_map/ppermute | solution.py:92
  30.7 0.1 fusion.21
  30.9 1.6 %convert_element_type.50 = f32[1,8,32,16,128]{4,3,2,1,0:T(8,128)} convert(bf16[1,8,32,16,128]{4,3,2,1,0:T(8,128)(2,1)S(1)} %copy-done) | non-fusion elementwise | flops 524288 | bytes 3145728 | tf_op jit(solution)/shard_map/convert_element_type | solution.py:132
  32.5 0.6 broadcast_add_fusion
  33.1 0.6 broadcast_add_fusion.2
  33.7 0.1 pad_maximum_fusion.6
  33.8 0.6 constant_dynamic-slice_fusion.1
  35.7 0.7 fusion.81
  37.6 6.0 %collective-permute-start.1 = (f32[3,1]{1,0:T(4,128)S(1)}, f32[3,1]{1,0:T(4,128)S(1)}, u32[]{:S(2)}, u32[]{:S(2)}) collective-permute-start(f32[3,1]{1,0:T(4,128)S(1)} %get-tuple-element.91), channel_id=1, source_target_pairs={{1,0},{2,1},{3,2},{4,3},{5,4},{6,5},{7,6},{8,7},{9,8},{10,9},{11,1... | collective-permute-start | bytes 44 | tf_op jit(solution)/shard_map/ppermute | solution.py:95
  43.6 3.4 %collective-permute-done.1 = f32[3,1]{1,0:T(4,128)S(1)} collective-permute-done((f32[3,1]{1,0:T(4,128)S(1)}, f32[3,1]{1,0:T(4,128)S(1)}, u32[]{:S(2)}, u32[]{:S(2)}) %collective-permute-start.1) | collective-permute-done | bytes 44 | tf_op jit(solution)/shard_map/ppermute | solution.py:95
  47.0 3.0 %collective-permute-start.8 = (f32[3,1]{1,0:T(4,128)S(1)}, f32[3,1]{1,0:T(4,128)S(1)}, u32[]{:S(2)}, u32[]{:S(2)}) collective-permute-start(f32[3,1]{1,0:T(4,128)S(1)} %get-tuple-element.95), channel_id=1, source_target_pairs={{0,16},{16,32},{32,48},{1,17},{17,33},{33,49},{2,18},{18,34},{34,5... | collective-permute-start | bytes 44 | tf_op jit(solution)/shard_map/ppermute | solution.py:92
  50.0 0.1 pad_maximum_fusion.5
  50.1 1.2 %collective-permute-done.8 = f32[3,1]{1,0:T(4,128)S(1)} collective-permute-done((f32[3,1]{1,0:T(4,128)S(1)}, f32[3,1]{1,0:T(4,128)S(1)}, u32[]{:S(2)}, u32[]{:S(2)}) %collective-permute-start.8) | collective-permute-done | bytes 44 | tf_op jit(solution)/shard_map/ppermute | solution.py:92
  51.3 1.3 %collective-permute-start.9 = (f32[3,1]{1,0:T(4,128)S(1)}, f32[3,1]{1,0:T(4,128)S(1)}, u32[]{:S(2)}, u32[]{:S(2)}) collective-permute-start(f32[3,1]{1,0:T(4,128)S(1)} %get-tuple-element.96), channel_id=1, source_target_pairs={{16,0},{32,16},{48,32},{17,1},{33,17},{49,33},{18,2},{34,18},{50,3... | collective-permute-start | bytes 44 | tf_op jit(solution)/shard_map/ppermute | solution.py:95
  52.6 5.6 %collective-permute-done.9 = f32[3,1]{1,0:T(4,128)S(1)} collective-permute-done((f32[3,1]{1,0:T(4,128)S(1)}, f32[3,1]{1,0:T(4,128)S(1)}, u32[]{:S(2)}, u32[]{:S(2)}) %collective-permute-start.9) | collective-permute-done | bytes 44 | tf_op jit(solution)/shard_map/ppermute | solution.py:95
  58.3 0.7 pad_maximum_fusion.10
  58.9 1.5 %copy.31 = f32[6,32,16,2]{3,2,1,0:T(8,128)S(1)} copy(bf16[6,32,16,2]{1,2,3,0:T(8,128)(2,1)} %collective-permute-done.4) | data formatting | bytes 36864 | tf_op jit(solution)/shard_map/convert_element_type | solution.py:138
  60.5 2.6 %copy.33 = f32[6,32,16,2]{3,2,1,0:T(8,128)} copy(bf16[6,32,16,2]{1,2,3,0:T(8,128)(2,1)} %collective-permute-done.5) | data formatting | bytes 36864 | tf_op jit(solution)/shard_map/convert_element_type | solution.py:138
  63.3 6.0 %fusion.3 = (f32[6,32,16,128]{3,2,1,0:T(8,128)S(1)}, f32[6,32,16,128]{3,2,1,0:T(8,128)S(1)}, f32[6,32,16,128]{3,2,1,0:T(8,128)S(1)}) fusion(f32[6,32,16,128]{3,2,1,0:T(8,128)S(1)} %fusion.21, f32[6,32,16,2]{3,2,1,0:T(8,128)} %copy.33, f32[6,32,16,2]{3,2,1,0:T(8,128)S(1)} %copy.31, f32[6,32,2,128]{3,2,1,0:T(2,128)S(1)} %convert_element_type.47, ...), kind=kLoop, calls=%fused_computation.15 | loop fusion | flops 9043968 | bytes 6733824 | tf_op jit(solution)/shard_map/div | solution.py:106
  69.4 1.4 %fusion.23 = f32[32,16,128]{2,1,0:T(8,128)S(1)} fusion(f32[1,8,32,16,128]{4,3,2,1,0:T(8,128)} %convert_element_type.50, f32[6,32,16,128]{3,2,1,0:T(8,128)S(1)} %get-tuple-element.72, f32[6,32,16,128]{3,2,1,0:T(8,128)S(1)} %get-tuple-element.73, f32[6,32,16,128]{3,2,1,0:T(8,128)S(1)} %get-tuple-element.71), kind=kLoop, calls=%fused_computation.52 | loop fusion | flops 1638400 | bytes 5505024 | tf_op jit(solution)/shard_map/sub | solution.py:149
  70.7 0.3 fusion.35
  71.0 0.2 convolution_bitcast_fusion
  71.3 5.9 %collective-permute-start.6 = (f32[4,2,128]{2,1,0:T(2,128)S(1)}, f32[4,2,128]{2,1,0:T(2,128)S(1)}, u32[]{:S(2)}, u32[]{:S(2)}) collective-permute-start(f32[4,2,128]{2,1,0:T(2,128)S(1)} %get-tuple-element.80), channel_id=1, source_target_pairs={{0,1},{1,2},{2,3},{3,4},{4,5},{5,6},{6,7},{7,8},{8,9},{9,10},{10,1... | collective-permute-start | bytes 12296 | tf_op jit(solution)/shard_map/ppermute | solution.py:14
  77.2 4.7 %collective-permute-start.7 = (f32[4,2,128]{2,1,0:T(2,128)S(1)}, f32[4,2,128]{2,1,0:T(2,128)S(1)}, u32[]{:S(2)}, u32[]{:S(2)}) collective-permute-start(f32[4,2,128]{2,1,0:T(2,128)S(1)} %get-tuple-element.81), channel_id=1, source_target_pairs={{1,0},{2,1},{3,2},{4,3},{5,4},{6,5},{7,6},{8,7},{9,8},{10,9},{11,1... | collective-permute-start | bytes 12296 | tf_op jit(solution)/shard_map/ppermute | solution.py:17
  82.0 4.6 %collective-permute-done.7 = f32[4,2,128]{2,1,0:T(2,128)S(1)} collective-permute-done((f32[4,2,128]{2,1,0:T(2,128)S(1)}, f32[4,2,128]{2,1,0:T(2,128)S(1)}, u32[]{:S(2)}, u32[]{:S(2)}) %collective-permute-start.7) | collective-permute-done | bytes 4128 | tf_op jit(solution)/shard_map/ppermute | solution.py:17
  86.6 0.2 fusion.42
  86.9 0.1 fusion.78
  87.0 3.9 %collective-permute-start.10 = (f32[4,2,2]{2,0,1:T(4,128)S(1)}, f32[4,2,2]{2,0,1:T(4,128)S(1)}, u32[]{:S(2)}, u32[]{:S(2)}) collective-permute-start(f32[4,2,2]{2,0,1:T(4,128)S(1)} %get-tuple-element.86), channel_id=1, source_target_pairs={{0,16},{16,32},{32,48},{1,17},{17,33},{33,49},{2,18},{18,34},{34,5... | collective-permute-start | bytes 200 | tf_op jit(solution)/shard_map/ppermute | solution.py:14
  90.9 1.3 %collective-permute-start.11 = (f32[4,2,2]{2,0,1:T(4,128)S(1)}, f32[4,2,2]{2,0,1:T(4,128)S(1)}, u32[]{:S(2)}, u32[]{:S(2)}) collective-permute-start(f32[4,2,2]{2,0,1:T(4,128)S(1)} %get-tuple-element.85), channel_id=1, source_target_pairs={{16,0},{32,16},{48,32},{17,1},{33,17},{49,33},{18,2},{34,18},{50,3... | collective-permute-start | bytes 200 | tf_op jit(solution)/shard_map/ppermute | solution.py:17
  92.3 0.1 slice_add_fusion.2
  92.3 0.1 scatter-add.6
  92.4 4.0 %collective-permute-done.11 = f32[4,2,2]{2,0,1:T(4,128)S(1)} collective-permute-done((f32[4,2,2]{2,0,1:T(4,128)S(1)}, f32[4,2,2]{2,0,1:T(4,128)S(1)}, u32[]{:S(2)}, u32[]{:S(2)}) %collective-permute-start.11) | collective-permute-done | bytes 96 | tf_op jit(solution)/shard_map/ppermute | solution.py:17
  96.4 0.1 slice_add_fusion.1
  96.5 0.3 scatter-add.9
  96.9 0.1 multiply_reduce_fusion.1
  97.0 2.9 %collective-permute-start.13 = (f32[2,16]{1,0:T(2,128)S(1)}, f32[2,16]{1,0:T(2,128)S(1)}, u32[]{:S(2)}, u32[]{:S(2)}) collective-permute-start(f32[2,16]{1,0:T(2,128)S(1)} %broadcast_multiply_fusion), channel_id=1, source_target_pairs={{64,0},{128,64},{192,128},{256,192},{320,256},{384,320},{448,384},... | collective-permute-start | bytes 392 | tf_op jit(solution)/shard_map/ppermute | solution.py:25
  99.9 1.2 %collective-permute-done.12 = f32[2,16]{1,0:T(2,128)S(1)} collective-permute-done((f32[2,16]{1,0:T(2,128)S(1)}, f32[2,16]{1,0:T(2,128)S(1)}, u32[]{:S(2)}, u32[]{:S(2)}) %collective-permute-start.12) | collective-permute-done | bytes 160 | tf_op jit(solution)/shard_map/ppermute | solution.py:25
  101.2 0.1 multiply_add_fusion
  101.3 0.6 copy.47
  (53 shorter events, 0.6 us)
Async XLA Ops:
  1.6 23.9 %copy-start.1 = (f32[3,16]{1,0:T(4,128)S(1)}, f32[3,16]{1,0:T(4,128)}, u32[]{:S(2)}) copy-start(f32[3,16]{1,0:T(4,128)} %param.20) | copy-start | bytes 580
  2.3 56.6 %collective-permute-start.4 = (bf16[6,32,16,2]{1,2,3,0:T(8,128)(2,1)S(1)}, bf16[6,32,16,2]{1,2,3,0:T(8,128)(2,1)}, u32[]{:S(2)}, u32[]{:S(2)}) collective-permute-start(bf16[6,32,16,2]{1,2,3,0:T(8,128)(2,1)S(1)} %copy.38), channel_id=1, source_target_pairs={{16,0},{32,16},{48,32},{17,1},{33,17},{49,33},{18,2},{34,18},{50,3... | collective-permute-start | bytes 36872 | tf_op jit(solution)/shard_map/ppermute | solution.py:95
  5.0 25.8 %copy-start = (bf16[1,8,32,16,128]{4,3,2,1,0:T(8,128)(2,1)S(1)}, bf16[1,8,32,16,128]{4,3,2,1,0:T(8,128)(2,1)}, u32[]{:S(2)}) copy-start(bf16[1,8,32,16,128]{4,3,2,1,0:T(8,128)(2,1)} %param.18) | copy-start | bytes 3145732
  5.0 55.5 %collective-permute-start.5 = (bf16[6,32,16,2]{1,2,3,0:T(8,128)(2,1)}, bf16[6,32,16,2]{1,2,3,0:T(8,128)(2,1)}, u32[]{:S(2)}, u32[]{:S(2)}) collective-permute-start(bf16[6,32,16,2]{1,2,3,0:T(8,128)(2,1)} %copy.39), channel_id=1, source_target_pairs={{0,16},{16,32},{32,48},{1,17},{17,33},{33,49},{2,18},{18,34},{34,5... | collective-permute-start | bytes 36872 | tf_op jit(solution)/shard_map/ppermute | solution.py:92
  10.5 52.6 %collective-permute-start.2 = (bf16[6,32,2,128]{3,2,1,0:T(2,128)(2,1)S(1)}, bf16[6,32,2,128]{3,2,1,0:T(2,128)(2,1)S(1)}, u32[]{:S(2)}, u32[]{:S(2)}) collective-permute-start(bf16[6,32,2,128]{3,2,1,0:T(2,128)(2,1)S(1)} %get-tuple-element.76), channel_id=1, source_target_pairs={{1,0},{2,1},{3,2},{4,3},{5,4},{6,5},{7,6},{8,7},{9,8},{10,9},{11,1... | collective-permute-start | bytes 294920 | tf_op jit(solution)/shard_map/ppermute | solution.py:95
  23.5 39.7 %collective-permute-start.3 = (bf16[6,32,2,128]{3,2,1,0:T(2,128)(2,1)S(1)}, bf16[6,32,2,128]{3,2,1,0:T(2,128)(2,1)S(1)}, u32[]{:S(2)}, u32[]{:S(2)}) collective-permute-start(bf16[6,32,2,128]{3,2,1,0:T(2,128)(2,1)S(1)} %get-tuple-element.77), channel_id=1, source_target_pairs={{0,1},{1,2},{2,3},{3,4},{4,5},{5,6},{6,7},{7,8},{8,9},{9,10},{10,1... | collective-permute-start | bytes 294920 | tf_op jit(solution)/shard_map/ppermute | solution.py:92
  25.5 12.1 %collective-permute-start = (f32[3,1]{1,0:T(4,128)S(1)}, f32[3,1]{1,0:T(4,128)S(1)}, u32[]{:S(2)}, u32[]{:S(2)}) collective-permute-start(f32[3,1]{1,0:T(4,128)S(1)} %get-tuple-element.90), channel_id=1, source_target_pairs={{0,1},{1,2},{2,3},{3,4},{4,5},{5,6},{6,7},{7,8},{8,9},{9,10},{10,1... | collective-permute-start | bytes 44 | tf_op jit(solution)/shard_map/ppermute | solution.py:92
  30.8 2.9 %copy-start.8 = (f32[3,32]{1,0:T(4,128)S(1)}, f32[3,32]{1,0:T(4,128)}, u32[]{:S(2)}) copy-start(f32[3,32]{1,0:T(4,128)} %param.21) | copy-start | bytes 1156
  30.8 2.9 %copy-start.2 = (f32[3,128]{1,0:T(4,128)S(1)}, f32[3,128]{1,0:T(4,128)}, u32[]{:S(2)}) copy-start(f32[3,128]{1,0:T(4,128)} %param.19) | copy-start | bytes 4612
  30.8 3.0 %copy-start.11 = (s32[8,2]{0,1:T(2,128)S(1)}, s32[8,2]{0,1:T(2,128)}, u32[]{:S(2)}) copy-start(s32[8,2]{0,1:T(2,128)} %param.22) | copy-start | bytes 196
  30.9 4.8 %copy-start.9 = (s32[8]{0:T(128)S(1)}, s32[8]{0:T(128)}, u32[]{:S(2)}) copy-start(s32[8]{0:T(128)} %param.23) | copy-start | bytes 100
  37.6 9.4 %collective-permute-start.1 = (f32[3,1]{1,0:T(4,128)S(1)}, f32[3,1]{1,0:T(4,128)S(1)}, u32[]{:S(2)}, u32[]{:S(2)}) collective-permute-start(f32[3,1]{1,0:T(4,128)S(1)} %get-tuple-element.91), channel_id=1, source_target_pairs={{1,0},{2,1},{3,2},{4,3},{5,4},{6,5},{7,6},{8,7},{9,8},{10,9},{11,1... | collective-permute-start | bytes 44 | tf_op jit(solution)/shard_map/ppermute | solution.py:95
  47.0 4.3 %collective-permute-start.8 = (f32[3,1]{1,0:T(4,128)S(1)}, f32[3,1]{1,0:T(4,128)S(1)}, u32[]{:S(2)}, u32[]{:S(2)}) collective-permute-start(f32[3,1]{1,0:T(4,128)S(1)} %get-tuple-element.95), channel_id=1, source_target_pairs={{0,16},{16,32},{32,48},{1,17},{17,33},{33,49},{2,18},{18,34},{34,5... | collective-permute-start | bytes 44 | tf_op jit(solution)/shard_map/ppermute | solution.py:92
  51.3 6.9 %collective-permute-start.9 = (f32[3,1]{1,0:T(4,128)S(1)}, f32[3,1]{1,0:T(4,128)S(1)}, u32[]{:S(2)}, u32[]{:S(2)}) collective-permute-start(f32[3,1]{1,0:T(4,128)S(1)} %get-tuple-element.96), channel_id=1, source_target_pairs={{16,0},{32,16},{48,32},{17,1},{33,17},{49,33},{18,2},{34,18},{50,3... | collective-permute-start | bytes 44 | tf_op jit(solution)/shard_map/ppermute | solution.py:95
  69.3 12.6 %copy-start.3 = (f32[1,130]{1,0:T(1,128)S(1)}, f32[1,130]{1,0:T(1,128)}, u32[]{:S(2)}) copy-start(f32[1,130]{1,0:T(1,128)} %get-tuple-element.82) | copy-start | bytes 1564
  69.3 12.6 %copy-start.4 = (f32[1,130]{1,0:T(1,128)S(1)}, f32[1,130]{1,0:T(1,128)}, u32[]{:S(2)}) copy-start(f32[1,130]{1,0:T(1,128)} %get-tuple-element.83) | copy-start | bytes 1564
  69.3 12.6 %copy-start.5 = (f32[1,130]{1,0:T(1,128)S(1)}, f32[1,130]{1,0:T(1,128)}, u32[]{:S(2)}) copy-start(f32[1,130]{1,0:T(1,128)} %get-tuple-element.84) | copy-start | bytes 1564
  69.3 12.6 %copy-start.6 = (s32[130]{0:T(256)S(1)}, s32[130]{0:T(256)}, u32[]{:S(2)}) copy-start(s32[130]{0:T(256)} %get-tuple-element.105) | copy-start | bytes 1564
  69.3 12.6 %copy-start.7 = (s32[130]{0:T(256)S(1)}, s32[130]{0:T(256)}, u32[]{:S(2)}) copy-start(s32[130]{0:T(256)} %get-tuple-element.106) | copy-start | bytes 1564
  69.4 12.6 %copy-start.10 = (s32[130]{0:T(256)S(1)}, s32[130]{0:T(256)}, u32[]{:S(2)}) copy-start(s32[130]{0:T(256)} %broadcast_add_fusion.2) | copy-start | bytes 1564
  71.3 10.7 %collective-permute-start.6 = (f32[4,2,128]{2,1,0:T(2,128)S(1)}, f32[4,2,128]{2,1,0:T(2,128)S(1)}, u32[]{:S(2)}, u32[]{:S(2)}) collective-permute-start(f32[4,2,128]{2,1,0:T(2,128)S(1)} %get-tuple-element.80), channel_id=1, source_target_pairs={{0,1},{1,2},{2,3},{3,4},{4,5},{5,6},{6,7},{7,8},{8,9},{9,10},{10,1... | collective-permute-start | bytes 12296 | tf_op jit(solution)/shard_map/ppermute | solution.py:14
  77.2 9.4 %collective-permute-start.7 = (f32[4,2,128]{2,1,0:T(2,128)S(1)}, f32[4,2,128]{2,1,0:T(2,128)S(1)}, u32[]{:S(2)}, u32[]{:S(2)}) collective-permute-start(f32[4,2,128]{2,1,0:T(2,128)S(1)} %get-tuple-element.81), channel_id=1, source_target_pairs={{1,0},{2,1},{3,2},{4,3},{5,4},{6,5},{7,6},{8,7},{9,8},{10,9},{11,1... | collective-permute-start | bytes 12296 | tf_op jit(solution)/shard_map/ppermute | solution.py:17
  87.0 5.2 %collective-permute-start.10 = (f32[4,2,2]{2,0,1:T(4,128)S(1)}, f32[4,2,2]{2,0,1:T(4,128)S(1)}, u32[]{:S(2)}, u32[]{:S(2)}) collective-permute-start(f32[4,2,2]{2,0,1:T(4,128)S(1)} %get-tuple-element.86), channel_id=1, source_target_pairs={{0,16},{16,32},{32,48},{1,17},{17,33},{33,49},{2,18},{18,34},{34,5... | collective-permute-start | bytes 200 | tf_op jit(solution)/shard_map/ppermute | solution.py:14
  90.9 5.5 %collective-permute-start.11 = (f32[4,2,2]{2,0,1:T(4,128)S(1)}, f32[4,2,2]{2,0,1:T(4,128)S(1)}, u32[]{:S(2)}, u32[]{:S(2)}) collective-permute-start(f32[4,2,2]{2,0,1:T(4,128)S(1)} %get-tuple-element.85), channel_id=1, source_target_pairs={{16,0},{32,16},{48,32},{17,1},{33,17},{49,33},{18,2},{34,18},{50,3... | collective-permute-start | bytes 200 | tf_op jit(solution)/shard_map/ppermute | solution.py:17
  97.0 4.2 %collective-permute-start.12 = (f32[2,16]{1,0:T(2,128)S(1)}, f32[2,16]{1,0:T(2,128)S(1)}, u32[]{:S(2)}, u32[]{:S(2)}) collective-permute-start(f32[2,16]{1,0:T(2,128)S(1)} %broadcast_multiply_fusion.1), channel_id=1, source_target_pairs={{448,0},{0,64},{64,128},{128,192},{192,256},{256,320},{320,384},{3... | collective-permute-start | bytes 392 | tf_op jit(solution)/shard_map/ppermute | solution.py:25
  97.0 4.2 %collective-permute-start.13 = (f32[2,16]{1,0:T(2,128)S(1)}, f32[2,16]{1,0:T(2,128)S(1)}, u32[]{:S(2)}, u32[]{:S(2)}) collective-permute-start(f32[2,16]{1,0:T(2,128)S(1)} %broadcast_multiply_fusion), channel_id=1, source_target_pairs={{64,0},{128,64},{192,128},{256,192},{320,256},{384,320},{448,384},... | collective-permute-start | bytes 392 | tf_op jit(solution)/shard_map/ppermute | solution.py:25

commit v3 on v2

--- a/solution.py
+++ b/solution.py
@@ -85,15 +85,44 @@
     return interior.at[:, :, -2:].add(widened[:, :, -2:])
 
 
-def neighbour_rows(block, axis, dim, width):
+def split_exact(vector):
+    high = lax.reduce_precision(vector, exponent_bits=8, mantissa_bits=7)
+    rest = vector - high
+    middle = lax.reduce_precision(rest, exponent_bits=8, mantissa_bits=7)
+    low = rest - middle
+    return jnp.stack([high, middle, low]).astype(jnp.bfloat16).reshape(-1)
+
+
+def join_exact(parts):
+    high, middle, low = parts.astype(jnp.float32).reshape(3, -1)
+    return high + (middle + low)
+
+
+def with_rider(piece, vector):
+    parts = split_exact(vector)
+    carried = piece.shape[1]
+    assert parts.shape[0] <= carried
+    parts = jnp.pad(parts, (0, carried - parts.shape[0]))
+    shape = (1,) + piece.shape[1:]
+    slab = jnp.broadcast_to(parts.reshape((1, carried) + (1,) * (piece.ndim - 2)), shape)
+    return jnp.concatenate([piece, slab], axis=0)
+
+
+def neighbour_rows(block, coef, axis, dim, width):
     count = lax.axis_size(axis)
     forward = [(i, i + 1) for i in range(count - 1)]
     backward = [(target, source) for source, target in forward]
+    size = coef.shape[0] * 3
     low = lax.ppermute(
-        lax.slice_in_dim(block, block.shape[dim] - width, None, axis=dim), axis, forward
+        with_rider(lax.slice_in_dim(block, block.shape[dim] - width, None, axis=dim), coef[:, -1]),
+        axis,
+        forward,
     )
-    high = lax.ppermute(lax.slice_in_dim(block, 0, width, axis=dim), axis, backward)
-    return low, high
+    high = lax.ppermute(with_rider(lax.slice_in_dim(block, 0, width, axis=dim), coef[:, 0]), axis, backward)
+    rider_at = (-1, slice(0, size)) + (0,) * (block.ndim - 2)
+    coef_low = join_exact(low[rider_at])[:, None]
+    coef_high = join_exact(high[rider_at])[:, None]
+    return low[:-1], high[:-1], coef_low, coef_high
 
 
 def slopes_along(low, core, high, dim):
@@ -125,10 +154,8 @@
     columns_v = rows_v // RATIO + 4
     columns_u = rows_u // RATIO + 4
     moving = jnp.concatenate([stacked[0:3], stacked[4:7]], axis=0)
-    low_u, high_u = neighbour_rows(moving, "au", 3, 2)
-    low_v, high_v = neighbour_rows(moving, "vert", 2, 2)
-    coef_low_u, coef_high_u = neighbour_rows(coef_u, "au", 1, 1)
-    coef_low_v, coef_high_v = neighbour_rows(coef_v, "vert", 1, 1)
+    low_u, high_u, coef_low_u, coef_high_u = neighbour_rows(moving, coef_u, "au", 3, 2)
+    low_v, high_v, coef_low_v, coef_high_v = neighbour_rows(moving, coef_v, "vert", 2, 2)
     values = stacked.astype(jnp.float32)
     moving = moving.astype(jnp.float32)
     zero_w = jnp.zeros_like(moving[:, :2])

time: 104 us -> 84.4 us (0.81)
  starting transfers between devices: 55.7 us -> 36.1 us
  other arithmetic: 12.1 us -> 21.3 us
  waiting for transfers between devices: 20.2 us -> 12 us
    ppermute x8 -> x4, starting transfers between devices: 36.9 us -> 21.4 us  [the longest x2 14.3 us: neighbour_rows(): lax.ppermute(with_rider(lax.slice_in_dim(block, block.shape[dim] - width,...]
    ppermute x8 -> x4, waiting for transfers between devices: 10.3 us -> 0.01 us  [the longest x2 0.01 us: neighbour_rows(): lax.ppermute(with_rider(lax.slice_in_dim(block, block.shape[dim] - width,...]
    convert_element_type x0 -> x6, other arithmetic: none -> 4.36 us  [the longest x4 2.75 us: join_exact(): high, middle, low = parts.astype(jnp.float32).reshape(3, -1)]
    ppermute x2, waiting for transfers between devices: 1.3 us -> 3.87 us  [from_behind(): return lax.ppermute(block, axis, route)]
    ppermute x2, starting transfers between devices: 2.95 us -> 0.5 us  [from_behind(): return lax.ppermute(block, axis, route)]
    ppermute x2, starting transfers between devices: 9.86 us -> 7.52 us  [with_halo(): lax.ppermute(lax.slice_in_dim(block, block.shape[dim] - width, None, axis...]
    concatenate x0 -> x4, other arithmetic: none -> 2.25 us  [with_rider(): return jnp.concatenate([piece, slab], axis=0)]
    unnamed x26 -> x18, local copies, waits for them, and re-layouts: 2.19 us -> 0.05 us
  transfers between devices with their start and end apart: 14 -> 10, of which waited for: 7 -> 4; matrix products, arithmetic and copies ran while one was open for 11% -> 20% of each run, Pallas kernels for 0% -> 0%
where the time goes in v3:
time: 84.4 us; the launch traced here: 83 us
  starting transfers between devices  36.1 us (43%)
  other arithmetic  21.3 us (25%)
  waiting for transfers between devices  12 us (14%)
  local copies, waits for them, and re-layouts  9.82 us (12%)
  between operations  3.05 us (4%)
    ppermute x2, starting transfers between devices, neighbour_rows(): lax.ppermute(with_rider(lax.slice_in_dim(block, block.shape[dim] - width,...  14.3 us
    ppermute x2, waiting for transfers between devices, with_halo(): lax.ppermute(lax.slice_in_dim(block, 0, width, axis=dim), axis, backward)  8.07 us
    ppermute x2, starting transfers between devices, with_halo(): lax.ppermute(lax.slice_in_dim(block, block.shape[dim] - width, None, axis...  7.52 us
    ppermute x2, starting transfers between devices, neighbour_rows(): lax.ppermute(with_rider(lax.slice_in_dim(block, 0, width, axis=dim), coef...  7.09 us
    ppermute x2, starting transfers between devices, with_halo(): lax.ppermute(lax.slice_in_dim(block, 0, width, axis=dim), axis, backward)  6.75 us
    div x1, other arithmetic, slopes_along(): (8.0 * (shifted(1) - shifted(-1)) - (shifted(2) - shifted(-2))) / 12.0  6.06 us
    ppermute x2, waiting for transfers between devices, from_behind(): return lax.ppermute(block, axis, route)  3.87 us
    convert_element_type x4, other arithmetic, join_exact(): high, middle, low = parts.astype(jnp.float32).reshape(3, -1)  2.75 us
  transfers between devices with their start and end apart: 10, of which 4 were waited for; matrix products, arithmetic and copies ran while one was open for 20% of the time, Pallas kernels for 0%

profile of v3, /device:TPU:6, one launch (start us, length us, event | category | flops | bytes accessed | tf_op | source)
XLA Modules:
  0.0 83.0 jit_solution(11987893068058523063)
XLA Ops:
  0.0 1.0 %slice_reduce_fusion.2 = (f32[3]{0:T(128)S(1)}, f32[3]{0:T(128)S(1)}) fusion(f32[3,16]{1,0:T(4,128)} %param.20), kind=kLoop, calls=%fused_computation.140 | loop fusion | bytes 48 | tf_op jit(solution)/shard_map/slice | solution.py:121
  1.1 1.3 %slice_bitcast_fusion = (bf16[3,32,16,128]{3,2,1,0:T(8,128)(2,1)S(1)}, bf16[3,32,16,128]{3,2,1,0:T(8,128)(2,1)S(1)}) fusion(bf16[1,8,32,16,128]{4,3,2,1,0:T(8,128)(2,1)} %param.18), kind=kLoop, calls=%fused_computation.48 | loop fusion | bytes 1572864 | tf_op jit(solution)/shard_map/slice | solution.py:156
  2.4 0.2 fusion.38
  2.7 0.2 pad_maximum_fusion.5
  2.9 9.1 %collective-permute-start = (bf16[7,32,2,128]{3,2,1,0:T(2,128)(2,1)S(1)}, bf16[7,32,2,128]{3,2,1,0:T(2,128)(2,1)}, u32[]{:S(2)}, u32[]{:S(2)}) collective-permute-start(bf16[7,32,2,128]{3,2,1,0:T(2,128)(2,1)S(1)} %pad_maximum_fusion.5), channel_id=1, source_target_pairs={{0,1},{1,2},{2,3},{3,4},{4,5},{5,6},{6,7},{7,8},{8,9},{9,10},{10,1... | collective-permute-start | bytes 344072 | tf_op jit(solution)/shard_map/ppermute | solution.py:116
  12.2 0.8 pad_maximum_fusion.6
  13.0 5.8 %collective-permute-start.1 = (bf16[7,32,2,128]{3,2,1,0:T(2,128)(2,1)}, bf16[7,32,2,128]{3,2,1,0:T(2,128)(2,1)}, u32[]{:S(2)}, u32[]{:S(2)}) collective-permute-start(bf16[7,32,2,128]{3,2,1,0:T(2,128)(2,1)} %pad_maximum_fusion.6), channel_id=1, source_target_pairs={{1,0},{2,1},{3,2},{4,3},{5,4},{6,5},{7,6},{8,7},{9,8},{10,9},{11,1... | collective-permute-start | bytes 344072 | tf_op jit(solution)/shard_map/ppermute | solution.py:121
  18.8 0.3 fusion.20
  19.1 0.2 slice_reduce_fusion
  19.4 0.8 copy.68
  20.2 0.7 pad_maximum_fusion.7
  20.8 1.3 %collective-permute-start.2 = (bf16[7,32,16,2]{1,2,3,0:T(8,128)(2,1)}, bf16[7,32,16,2]{1,2,3,0:T(8,128)(2,1)}, u32[]{:S(2)}, u32[]{:S(2)}) collective-permute-start(bf16[7,32,16,2]{1,2,3,0:T(8,128)(2,1)} %pad_maximum_fusion.7), channel_id=1, source_target_pairs={{16,0},{32,16},{48,32},{17,1},{33,17},{49,33},{18,2},{34,18},{50,3... | collective-permute-start | bytes 43016 | tf_op jit(solution)/shard_map/ppermute | solution.py:121
  22.2 0.8 copy.70
  23.0 0.7 pad_maximum_fusion.8
  23.7 5.2 %collective-permute-start.3 = (bf16[7,32,16,2]{1,2,3,0:T(8,128)(2,1)}, bf16[7,32,16,2]{1,2,3,0:T(8,128)(2,1)}, u32[]{:S(2)}, u32[]{:S(2)}) collective-permute-start(bf16[7,32,16,2]{1,2,3,0:T(8,128)(2,1)} %pad_maximum_fusion.8), channel_id=1, source_target_pairs={{0,16},{16,32},{32,48},{1,17},{17,33},{33,49},{2,18},{18,34},{34,5... | collective-permute-start | bytes 43016 | tf_op jit(solution)/shard_map/ppermute | solution.py:116
  28.8 0.5 broadcast_add_fusion.5
  29.4 0.6 and_select_fusion.1
  30.1 0.7 constant_dynamic-slice_fusion.1
  32.2 0.7 select_add_fusion.2
  32.9 0.5 broadcast_add_fusion.7
  33.4 1.5 %convert_element_type.97 = f32[1,8,32,16,128]{4,3,2,1,0:T(8,128)} convert(bf16[1,8,32,16,128]{4,3,2,1,0:T(8,128)(2,1)S(1)} %copy-done) | non-fusion elementwise | flops 524288 | bytes 3145728 | tf_op jit(solution)/shard_map/convert_element_type | solution.py:159
  35.0 0.7 fusion.85
  37.0 0.7 slice_convert_fusion.6
  37.6 0.8 slice_convert_fusion.3
  38.5 0.7 slice_convert_fusion.7
  39.2 0.8 slice_convert_fusion.2
  40.3 0.8 copy.71
  41.0 1.8 %copy.69 = f32[6,32,16,2]{3,2,1,0:T(8,128)} copy(f32[6,32,16,2]{1,2,3,0:T(8,128)S(1)} %slice_convert_fusion.3) | data formatting | bytes 49152 | tf_op jit(solution)/shard_map/convert_element_type | solution.py:165
  42.9 0.7 slice_convert_fusion.5
  43.6 0.7 slice_convert_fusion.4
  44.4 1.0 %slice_convert_fusion = f32[6,32,2,128]{3,2,1,0:T(2,128)S(1)} fusion(bf16[7,32,2,128]{3,2,1,0:T(2,128)(2,1)} %collective-permute-done), kind=kLoop, calls=%fused_computation.77 | loop fusion | flops 49152 | bytes 294912 | tf_op jit(solution)/shard_map/convert_element_type | solution.py:164
  45.4 1.0 %slice_convert_fusion.1 = f32[6,32,2,128]{3,2,1,0:T(2,128)S(1)} fusion(bf16[7,32,2,128]{3,2,1,0:T(2,128)(2,1)} %collective-permute-done.1), kind=kLoop, calls=%fused_computation.78 | loop fusion | flops 49152 | bytes 294912 | tf_op jit(solution)/shard_map/convert_element_type | solution.py:164
  46.4 6.1 %fusion.3 = (f32[6,32,16,128]{3,2,1,0:T(8,128)S(1)}, f32[6,32,16,128]{3,2,1,0:T(8,128)S(1)}, f32[6,32,16,128]{3,2,1,0:T(8,128)S(1)}) fusion(f32[6,32,16,128]{3,2,1,0:T(8,128)S(1)} %fusion.21, f32[6,32,16,2]{3,2,1,0:T(8,128)S(1)} %copy.71, f32[6,32,16,2]{3,2,1,0:T(8,128)} %copy.69, f32[6,32,2,128]{3,2,1,0:T(2,128)S(1)} %slice_convert_fusion, ...), kind=kLoop, calls=%fused_computation.15 | loop fusion | flops 9043968 | bytes 6733824 | tf_op jit(solution)/shard_map/div | solution.py:135
  52.5 1.4 %fusion.23 = f32[32,16,128]{2,1,0:T(8,128)S(1)} fusion(f32[1,8,32,16,128]{4,3,2,1,0:T(8,128)} %convert_element_type.97, f32[6,32,16,128]{3,2,1,0:T(8,128)S(1)} %get-tuple-element.76, f32[6,32,16,128]{3,2,1,0:T(8,128)S(1)} %get-tuple-element.77, f32[6,32,16,128]{3,2,1,0:T(8,128)S(1)} %get-tuple-element.75), kind=kLoop, calls=%fused_computation.52 | loop fusion | flops 1638400 | bytes 5505024 | tf_op jit(solution)/shard_map/sub | solution.py:176
  53.9 0.3 fusion.35
  54.2 0.2 convolution_bitcast_fusion
  54.4 5.2 %collective-permute-start.4 = (f32[4,2,128]{2,1,0:T(2,128)S(1)}, f32[4,2,128]{2,1,0:T(2,128)S(1)}, u32[]{:S(2)}, u32[]{:S(2)}) collective-permute-start(f32[4,2,128]{2,1,0:T(2,128)S(1)} %get-tuple-element.84), channel_id=1, source_target_pairs={{0,1},{1,2},{2,3},{3,4},{4,5},{5,6},{6,7},{7,8},{8,9},{9,10},{10,1... | collective-permute-start | bytes 12296 | tf_op jit(solution)/shard_map/ppermute | solution.py:14
  59.6 5.5 %collective-permute-start.5 = (f32[4,2,128]{2,1,0:T(2,128)S(1)}, f32[4,2,128]{2,1,0:T(2,128)S(1)}, u32[]{:S(2)}, u32[]{:S(2)}) collective-permute-start(f32[4,2,128]{2,1,0:T(2,128)S(1)} %get-tuple-element.85), channel_id=1, source_target_pairs={{1,0},{2,1},{3,2},{4,3},{5,4},{6,5},{7,6},{8,7},{9,8},{10,9},{11,1... | collective-permute-start | bytes 12296 | tf_op jit(solution)/shard_map/ppermute | solution.py:17
  65.1 3.9 %collective-permute-done.5 = f32[4,2,128]{2,1,0:T(2,128)S(1)} collective-permute-done((f32[4,2,128]{2,1,0:T(2,128)S(1)}, f32[4,2,128]{2,1,0:T(2,128)S(1)}, u32[]{:S(2)}, u32[]{:S(2)}) %collective-permute-start.5) | collective-permute-done | bytes 4128 | tf_op jit(solution)/shard_map/ppermute | solution.py:17
  69.1 0.2 fusion.42
  69.4 2.3 %collective-permute-start.6 = (f32[4,2,2]{2,0,1:T(4,128)S(1)}, f32[4,2,2]{2,0,1:T(4,128)S(1)}, u32[]{:S(2)}, u32[]{:S(2)}) collective-permute-start(f32[4,2,2]{2,0,1:T(4,128)S(1)} %get-tuple-element.90), channel_id=1, source_target_pairs={{0,16},{16,32},{32,48},{1,17},{17,33},{33,49},{2,18},{18,34},{34,5... | collective-permute-start | bytes 200 | tf_op jit(solution)/shard_map/ppermute | solution.py:14
  71.8 1.3 %collective-permute-start.7 = (f32[4,2,2]{2,0,1:T(4,128)S(1)}, f32[4,2,2]{2,0,1:T(4,128)S(1)}, u32[]{:S(2)}, u32[]{:S(2)}) collective-permute-start(f32[4,2,2]{2,0,1:T(4,128)S(1)} %get-tuple-element.89), channel_id=1, source_target_pairs={{16,0},{32,16},{48,32},{17,1},{33,17},{49,33},{18,2},{34,18},{50,3... | collective-permute-start | bytes 200 | tf_op jit(solution)/shard_map/ppermute | solution.py:17
  73.3 4.2 %collective-permute-done.7 = f32[4,2,2]{2,0,1:T(4,128)S(1)} collective-permute-done((f32[4,2,2]{2,0,1:T(4,128)S(1)}, f32[4,2,2]{2,0,1:T(4,128)S(1)}, u32[]{:S(2)}, u32[]{:S(2)}) %collective-permute-start.7) | collective-permute-done | bytes 96 | tf_op jit(solution)/shard_map/ppermute | solution.py:17
  77.5 0.3 scatter-add.9
  78.0 0.5 collective-permute-start.8
  78.5 0.8 collective-permute-done.9
  79.3 3.1 %collective-permute-done.8 = f32[2,16]{1,0:T(2,128)S(1)} collective-permute-done((f32[2,16]{1,0:T(2,128)S(1)}, f32[2,16]{1,0:T(2,128)S(1)}, u32[]{:S(2)}, u32[]{:S(2)}) %collective-permute-start.8) | collective-permute-done | bytes 160 | tf_op jit(solution)/shard_map/ppermute | solution.py:25
  82.4 0.6 copy.89
  (73 shorter events, 2.1 us)
Async XLA Ops:
  2.6 16.5 %copy-start.1 = (f32[3,128]{1,0:T(4,128)S(1)}, f32[3,128]{1,0:T(4,128)}, u32[]{:S(2)}) copy-start(f32[3,128]{1,0:T(4,128)} %param.19) | copy-start | bytes 4612
  2.9 40.0 %collective-permute-start = (bf16[7,32,2,128]{3,2,1,0:T(2,128)(2,1)S(1)}, bf16[7,32,2,128]{3,2,1,0:T(2,128)(2,1)}, u32[]{:S(2)}, u32[]{:S(2)}) collective-permute-start(bf16[7,32,2,128]{3,2,1,0:T(2,128)(2,1)S(1)} %pad_maximum_fusion.5), channel_id=1, source_target_pairs={{0,1},{1,2},{2,3},{3,4},{4,5},{5,6},{6,7},{7,8},{8,9},{9,10},{10,1... | collective-permute-start | bytes 344072 | tf_op jit(solution)/shard_map/ppermute | solution.py:116
  13.0 30.6 %collective-permute-start.1 = (bf16[7,32,2,128]{3,2,1,0:T(2,128)(2,1)}, bf16[7,32,2,128]{3,2,1,0:T(2,128)(2,1)}, u32[]{:S(2)}, u32[]{:S(2)}) collective-permute-start(bf16[7,32,2,128]{3,2,1,0:T(2,128)(2,1)} %pad_maximum_fusion.6), channel_id=1, source_target_pairs={{1,0},{2,1},{3,2},{4,3},{5,4},{6,5},{7,6},{8,7},{9,8},{10,9},{11,1... | collective-permute-start | bytes 344072 | tf_op jit(solution)/shard_map/ppermute | solution.py:121
  20.8 16.1 %collective-permute-start.2 = (bf16[7,32,16,2]{1,2,3,0:T(8,128)(2,1)}, bf16[7,32,16,2]{1,2,3,0:T(8,128)(2,1)}, u32[]{:S(2)}, u32[]{:S(2)}) collective-permute-start(bf16[7,32,16,2]{1,2,3,0:T(8,128)(2,1)} %pad_maximum_fusion.7), channel_id=1, source_target_pairs={{16,0},{32,16},{48,32},{17,1},{33,17},{49,33},{18,2},{34,18},{50,3... | collective-permute-start | bytes 43016 | tf_op jit(solution)/shard_map/ppermute | solution.py:121
  22.2 7.9 %copy-start.5 = (s32[8,2]{0,1:T(2,128)S(1)}, s32[8,2]{0,1:T(2,128)}, u32[]{:S(2)}) copy-start(s32[8,2]{0,1:T(2,128)} %param.22) | copy-start | bytes 196
  22.2 9.9 %copy-start.3 = (f32[3,32]{1,0:T(4,128)S(1)}, f32[3,32]{1,0:T(4,128)}, u32[]{:S(2)}) copy-start(f32[3,32]{1,0:T(4,128)} %param.21) | copy-start | bytes 1156
  22.2 11.2 %copy-start = (bf16[1,8,32,16,128]{4,3,2,1,0:T(8,128)(2,1)S(1)}, bf16[1,8,32,16,128]{4,3,2,1,0:T(8,128)(2,1)}, u32[]{:S(2)}) copy-start(bf16[1,8,32,16,128]{4,3,2,1,0:T(8,128)(2,1)} %param.18) | copy-start | bytes 3145732
  23.7 14.9 %collective-permute-start.3 = (bf16[7,32,16,2]{1,2,3,0:T(8,128)(2,1)}, bf16[7,32,16,2]{1,2,3,0:T(8,128)(2,1)}, u32[]{:S(2)}, u32[]{:S(2)}) collective-permute-start(bf16[7,32,16,2]{1,2,3,0:T(8,128)(2,1)} %pad_maximum_fusion.8), channel_id=1, source_target_pairs={{0,16},{16,32},{32,48},{1,17},{17,33},{33,49},{2,18},{18,34},{34,5... | collective-permute-start | bytes 43016 | tf_op jit(solution)/shard_map/ppermute | solution.py:116
  33.4 1.5 %copy-start.4 = (s32[8]{0:T(128)S(1)}, s32[8]{0:T(128)}, u32[]{:S(2)}) copy-start(s32[8]{0:T(128)} %param.23) | copy-start | bytes 100
  40.3 4.1 %copy-start.2 = (f32[3,16]{1,0:T(4,128)S(1)}, f32[3,16]{1,0:T(4,128)}, u32[]{:S(2)}) copy-start(f32[3,16]{1,0:T(4,128)} %param.20) | copy-start | bytes 580
  52.4 1.7 %copy-start.6 = (s32[18]{0:T(128)S(1)}, s32[18]{0:T(128)}, u32[]{:S(2)}) copy-start(s32[18]{0:T(128)} %get-tuple-element.122) | copy-start | bytes 220
  52.4 1.7 %copy-start.7 = (s32[18]{0:T(128)S(1)}, s32[18]{0:T(128)}, u32[]{:S(2)}) copy-start(s32[18]{0:T(128)} %broadcast_add_fusion.7) | copy-start | bytes 220
  54.4 10.7 %collective-permute-start.4 = (f32[4,2,128]{2,1,0:T(2,128)S(1)}, f32[4,2,128]{2,1,0:T(2,128)S(1)}, u32[]{:S(2)}, u32[]{:S(2)}) collective-permute-start(f32[4,2,128]{2,1,0:T(2,128)S(1)} %get-tuple-element.84), channel_id=1, source_target_pairs={{0,1},{1,2},{2,3},{3,4},{4,5},{5,6},{6,7},{7,8},{8,9},{9,10},{10,1... | collective-permute-start | bytes 12296 | tf_op jit(solution)/shard_map/ppermute | solution.py:14
  59.6 9.4 %collective-permute-start.5 = (f32[4,2,128]{2,1,0:T(2,128)S(1)}, f32[4,2,128]{2,1,0:T(2,128)S(1)}, u32[]{:S(2)}, u32[]{:S(2)}) collective-permute-start(f32[4,2,128]{2,1,0:T(2,128)S(1)} %get-tuple-element.85), channel_id=1, source_target_pairs={{1,0},{2,1},{3,2},{4,3},{5,4},{6,5},{7,6},{8,7},{9,8},{10,9},{11,1... | collective-permute-start | bytes 12296 | tf_op jit(solution)/shard_map/ppermute | solution.py:17
  69.4 3.6 %collective-permute-start.6 = (f32[4,2,2]{2,0,1:T(4,128)S(1)}, f32[4,2,2]{2,0,1:T(4,128)S(1)}, u32[]{:S(2)}, u32[]{:S(2)}) collective-permute-start(f32[4,2,2]{2,0,1:T(4,128)S(1)} %get-tuple-element.90), channel_id=1, source_target_pairs={{0,16},{16,32},{32,48},{1,17},{17,33},{33,49},{2,18},{18,34},{34,5... | collective-permute-start | bytes 200 | tf_op jit(solution)/shard_map/ppermute | solution.py:14
  71.8 5.6 %collective-permute-start.7 = (f32[4,2,2]{2,0,1:T(4,128)S(1)}, f32[4,2,2]{2,0,1:T(4,128)S(1)}, u32[]{:S(2)}, u32[]{:S(2)}) collective-permute-start(f32[4,2,2]{2,0,1:T(4,128)S(1)} %get-tuple-element.89), channel_id=1, source_target_pairs={{16,0},{32,16},{48,32},{17,1},{33,17},{49,33},{18,2},{34,18},{50,3... | collective-permute-start | bytes 200 | tf_op jit(solution)/shard_map/ppermute | solution.py:17
  77.9 1.3 %collective-permute-start.9 = (f32[2,16]{1,0:T(2,128)S(1)}, f32[2,16]{1,0:T(2,128)S(1)}, u32[]{:S(2)}, u32[]{:S(2)}) collective-permute-start(f32[2,16]{1,0:T(2,128)S(1)} %broadcast_multiply_fusion), channel_id=1, source_target_pairs={{64,0},{128,64},{192,128},{256,192},{320,256},{384,320},{448,384},... | collective-permute-start | bytes 392 | tf_op jit(solution)/shard_map/ppermute | solution.py:25
  78.0 4.4 %collective-permute-start.8 = (f32[2,16]{1,0:T(2,128)S(1)}, f32[2,16]{1,0:T(2,128)S(1)}, u32[]{:S(2)}, u32[]{:S(2)}) collective-permute-start(f32[2,16]{1,0:T(2,128)S(1)} %broadcast_multiply_fusion.1), channel_id=1, source_target_pairs={{448,0},{0,64},{64,128},{128,192},{192,256},{256,320},{320,384},{3... | collective-permute-start | bytes 392 | tf_op jit(solution)/shard_map/ppermute | solution.py:25

commit v4 on v3

--- a/solution.py
+++ b/solution.py
@@ -71,18 +71,45 @@
     return result
 
 
-def fold_vert(partial_value):
-    widened = with_halo(partial_value, (("vert", 1),), 2)
-    interior = widened[:, 4:-4]
-    interior = interior.at[:, :2].add(widened[:, :2])
-    return interior.at[:, -2:].add(widened[:, -2:])
-
-
-def fold_first(partial_value):
-    widened = with_halo(partial_value, (("au", 2),), 2)
-    interior = widened[:, :, 4:-4]
-    interior = interior.at[:, :, :2].add(widened[:, :, :2])
-    return interior.at[:, :, -2:].add(widened[:, :, -2:])
+def fold_both(partial_value, spill):
+    count_u = lax.axis_size("au")
+    count_v = lax.axis_size("vert")
+    rows = partial_value.shape[1] - 2 * spill
+    cols = partial_value.shape[2] - 2 * spill
+    assert rows >= spill and cols >= spill
+
+    def send(piece, step_u, step_v):
+        route = []
+        for a in range(count_u):
+            for v in range(count_v):
+                if 0 <= a + step_u < count_u and 0 <= v + step_v < count_v:
+                    route.append((a * count_v + v, (a + step_u) * count_v + v + step_v))
+        return lax.ppermute(piece, ("au", "vert"), route)
+
+    inner_v = slice(spill, spill + rows)
+    inner_u = slice(spill, spill + cols)
+    low_v = slice(0, spill)
+    high_v = slice(spill + rows, None)
+    low_u = slice(0, spill)
+    high_u = slice(spill + cols, None)
+    design = partial_value[:, inner_v, inner_u]
+    from_v_low = send(partial_value[:, high_v, inner_u], 0, 1)
+    from_v_high = send(partial_value[:, low_v, inner_u], 0, -1)
+    from_u_low = send(partial_value[:, inner_v, high_u], 1, 0)
+    from_u_high = send(partial_value[:, inner_v, low_u], -1, 0)
+    from_corner_ll = send(partial_value[:, high_v, high_u], 1, 1)
+    from_corner_lh = send(partial_value[:, low_v, high_u], 1, -1)
+    from_corner_hl = send(partial_value[:, high_v, low_u], -1, 1)
+    from_corner_hh = send(partial_value[:, low_v, low_u], -1, -1)
+    design = design.at[:, :spill, :].add(from_v_low)
+    design = design.at[:, rows - spill:, :].add(from_v_high)
+    design = design.at[:, :, :spill].add(from_u_low)
+    design = design.at[:, :, cols - spill:].add(from_u_high)
+    design = design.at[:, :spill, :spill].add(from_corner_ll)
+    design = design.at[:, rows - spill:, :spill].add(from_corner_lh)
+    design = design.at[:, :spill, cols - spill:].add(from_corner_hl)
+    design = design.at[:, rows - spill:, cols - spill:].add(from_corner_hh)
+    return design
 
 
 def split_exact(vector):
@@ -179,8 +206,8 @@
     mat_v = smoothed_band(jnp.concatenate([coef_low_v, coef_v, coef_high_v], axis=1), columns_v, 2)
     mat_u = smoothed_band(jnp.concatenate([coef_low_u, coef_u, coef_high_u], axis=1), columns_u, 2)
     reduced = jnp.einsum("wvu,wa->avu", density, mat_w, precision=highest)
-    reduced = fold_vert(jnp.einsum("avu,vb->abu", reduced, mat_v, precision=highest))
-    reduced = fold_first(jnp.einsum("abu,uc->abc", reduced, mat_u, precision=highest))
+    reduced = jnp.einsum("avu,vb->abu", reduced, mat_v, precision=highest)
+    reduced = fold_both(jnp.einsum("abu,uc->abc", reduced, mat_u, precision=highest), 2)
     patch_index = lax.axis_index("patch")
     patches = lax.axis_size("patch")
     layers_d = reduced.shape[0]

time: 84.4 us -> 104 us (1.23)
  starting transfers between devices: 36.1 us -> 57.1 us
  waiting for transfers between devices: 12 us -> 9.39 us
  local copies, waits for them, and re-layouts: 9.82 us -> 11.2 us
    ppermute x4 -> x8, starting transfers between devices: 14.3 us -> 36.9 us  [send(): return lax.ppermute(piece, ('au', 'vert'), route)]
    ppermute x4 -> x8, waiting for transfers between devices: 8.08 us -> 5.51 us  [send(): return lax.ppermute(piece, ('au', 'vert'), route)]
    scatter-add x2 -> x6, local copies, waits for them, and re-layouts: 0.44 us -> 2.52 us  [the longest x1 0.69 us: fold_both(): design = design.at[:, rows - spill:, cols - spill:].add(from_corner_hh)]
    ppermute x2, starting transfers between devices: 14.3 us -> 12.6 us  [neighbour_rows(): lax.ppermute(with_rider(lax.slice_in_dim(block, block.shape[dim] - width,...]
  transfers between devices with their start and end apart: 10 -> 14, of which waited for: 4 -> 4; matrix products, arithmetic and copies ran while one was open for 20% -> 17% of each run, Pallas kernels for 0% -> 0%
where the time goes in v4:
time: 104 us; the launch traced here: 103 us
  starting transfers between devices  57.1 us (55%)
  other arithmetic  21.8 us (21%)
  local copies, waits for them, and re-layouts  11.2 us (11%)
  waiting for transfers between devices  9.39 us (9%)
  between operations  2.95 us (3%)
    ppermute x8, starting transfers between devices, send(): return lax.ppermute(piece, ('au', 'vert'), route)  36.9 us
    ppermute x2, starting transfers between devices, neighbour_rows(): lax.ppermute(with_rider(lax.slice_in_dim(block, block.shape[dim] - width,...  12.6 us
    ppermute x2, starting transfers between devices, neighbour_rows(): lax.ppermute(with_rider(lax.slice_in_dim(block, 0, width, axis=dim), coef...  7.09 us
    div x1, other arithmetic, slopes_along(): (8.0 * (shifted(1) - shifted(-1)) - (shifted(2) - shifted(-2))) / 12.0  6.04 us
    ppermute x8, waiting for transfers between devices, send(): return lax.ppermute(piece, ('au', 'vert'), route)  5.51 us
    ppermute x2, waiting for transfers between devices, from_behind(): return lax.ppermute(block, axis, route)  3.87 us
    convert_element_type x4, other arithmetic, join_exact(): high, middle, low = parts.astype(jnp.float32).reshape(3, -1)  2.74 us
    concatenate x4, other arithmetic, with_rider(): return jnp.concatenate([piece, slab], axis=0)  2.23 us
  transfers between devices with their start and end apart: 14, of which 4 were waited for; matrix products, arithmetic and copies ran while one was open for 17% of the time, Pallas kernels for 0%

profile of v4, /device:TPU:6, one launch (start us, length us, event | category | flops | bytes accessed | tf_op | source)
XLA Modules:
  0.0 103.3 jit_solution(6024541143356592498)
XLA Ops:
  0.0 1.0 slice_reduce_fusion.2
  1.1 1.3 %slice_bitcast_fusion = (bf16[3,32,16,128]{3,2,1,0:T(8,128)(2,1)S(1)}, bf16[3,32,16,128]{3,2,1,0:T(8,128)(2,1)S(1)}) fusion(bf16[1,8,32,16,128]{4,3,2,1,0:T(8,128)(2,1)} %param.26), kind=kLoop, calls=%fused_computation.48 | loop fusion | bytes 1572864 | tf_op jit(solution)/shard_map/slice | solution.py:183
  2.9 9.1 %collective-permute-start = (bf16[7,32,2,128]{3,2,1,0:T(2,128)(2,1)S(1)}, bf16[7,32,2,128]{3,2,1,0:T(2,128)(2,1)}, u32[]{:S(2)}, u32[]{:S(2)}) collective-permute-start(bf16[7,32,2,128]{3,2,1,0:T(2,128)(2,1)S(1)} %pad_maximum_fusion.5), channel_id=1, source_target_pairs={{0,1},{1,2},{2,3},{3,4},{4,5},{5,6},{6,7},{7,8},{8,9},{9,10},{10,1... | collective-permute-start | bytes 344072 | tf_op jit(solution)/shard_map/ppermute | solution.py:143
  12.2 0.8 pad_maximum_fusion.6
  13.0 5.8 %collective-permute-start.1 = (bf16[7,32,2,128]{3,2,1,0:T(2,128)(2,1)}, bf16[7,32,2,128]{3,2,1,0:T(2,128)(2,1)}, u32[]{:S(2)}, u32[]{:S(2)}) collective-permute-start(bf16[7,32,2,128]{3,2,1,0:T(2,128)(2,1)} %pad_maximum_fusion.6), channel_id=1, source_target_pairs={{1,0},{2,1},{3,2},{4,3},{5,4},{6,5},{7,6},{8,7},{9,8},{10,9},{11,1... | collective-permute-start | bytes 344072 | tf_op jit(solution)/shard_map/ppermute | solution.py:148
  19.4 0.8 copy.60
  20.2 0.6 pad_maximum_fusion.8
  20.8 3.5 %collective-permute-start.3 = (bf16[7,32,16,2]{1,2,3,0:T(8,128)(2,1)}, bf16[7,32,16,2]{1,2,3,0:T(8,128)(2,1)}, u32[]{:S(2)}, u32[]{:S(2)}) collective-permute-start(bf16[7,32,16,2]{1,2,3,0:T(8,128)(2,1)} %pad_maximum_fusion.8), channel_id=1, source_target_pairs={{0,16},{16,32},{32,48},{1,17},{17,33},{33,49},{2,18},{18,34},{34,5... | collective-permute-start | bytes 43016 | tf_op jit(solution)/shard_map/ppermute | solution.py:143
  24.5 0.8 copy.58
  25.3 0.6 pad_maximum_fusion.7
  25.9 1.3 %collective-permute-start.2 = (bf16[7,32,16,2]{1,2,3,0:T(8,128)(2,1)}, bf16[7,32,16,2]{1,2,3,0:T(8,128)(2,1)}, u32[]{:S(2)}, u32[]{:S(2)}) collective-permute-start(bf16[7,32,16,2]{1,2,3,0:T(8,128)(2,1)} %pad_maximum_fusion.7), channel_id=1, source_target_pairs={{16,0},{32,16},{48,32},{17,1},{33,17},{49,33},{18,2},{34,18},{50,3... | collective-permute-start | bytes 43016 | tf_op jit(solution)/shard_map/ppermute | solution.py:148
  27.3 0.5 broadcast_add_fusion.5
  27.8 0.5 and_select_fusion.1
  28.4 0.6 constant_dynamic-slice_fusion.1
  30.4 0.7 select_add_fusion.2
  31.1 0.5 broadcast_add_fusion.7
  31.6 1.5 %convert_element_type.97 = f32[1,8,32,16,128]{4,3,2,1,0:T(8,128)} convert(bf16[1,8,32,16,128]{4,3,2,1,0:T(8,128)(2,1)S(1)} %copy-done) | non-fusion elementwise | flops 524288 | bytes 3145728 | tf_op jit(solution)/shard_map/convert_element_type | solution.py:186
  33.1 0.6 fusion.86
  34.9 0.7 slice_convert_fusion.7
  35.8 0.7 slice_convert_fusion.6
  36.6 0.8 slice_convert_fusion.3
  37.5 0.8 copy.59
  38.2 0.8 slice_convert_fusion.2
  39.0 1.8 %copy.61 = f32[6,32,16,2]{3,2,1,0:T(8,128)} copy(f32[6,32,16,2]{1,2,3,0:T(8,128)S(1)} %slice_convert_fusion.2) | data formatting | bytes 49152 | tf_op jit(solution)/shard_map/convert_element_type | solution.py:192
  40.9 0.7 slice_convert_fusion.5
  41.6 0.7 slice_convert_fusion.4
  42.5 1.0 slice_convert_fusion
  43.4 1.0 slice_convert_fusion.1
  44.4 6.0 %fusion.3 = (f32[6,32,16,128]{3,2,1,0:T(8,128)S(1)}, f32[6,32,16,128]{3,2,1,0:T(8,128)S(1)}, f32[6,32,16,128]{3,2,1,0:T(8,128)S(1)}) fusion(f32[6,32,16,128]{3,2,1,0:T(8,128)S(1)} %fusion.21, f32[6,32,16,2]{3,2,1,0:T(8,128)} %copy.61, f32[6,32,16,2]{3,2,1,0:T(8,128)S(1)} %copy.59, f32[6,32,2,128]{3,2,1,0:T(2,128)S(1)} %slice_convert_fusion, ...), kind=kLoop, calls=%fused_computation.15 | loop fusion | flops 9043968 | bytes 6733824 | tf_op jit(solution)/shard_map/div | solution.py:162
  50.5 1.4 %fusion.23 = f32[32,16,128]{2,1,0:T(8,128)S(1)} fusion(f32[1,8,32,16,128]{4,3,2,1,0:T(8,128)} %convert_element_type.97, f32[6,32,16,128]{3,2,1,0:T(8,128)S(1)} %get-tuple-element.128, f32[6,32,16,128]{3,2,1,0:T(8,128)S(1)} %get-tuple-element.129, f32[6,32,16,128]{3,2,1,0:T(8,128)S(1)} %get-tuple-element.127), kind=kLoop, calls=%fused_computation.52 | loop fusion | flops 1638400 | bytes 5505024 | tf_op jit(solution)/shard_map/sub | solution.py:203
  51.8 0.3 fusion.35
  52.7 5.2 %collective-permute-start.4 = (f32[4,2,16]{2,1,0:T(2,128)S(1)}, f32[4,2,16]{2,1,0:T(2,128)S(1)}, u32[]{:S(2)}, u32[]{:S(2)}) collective-permute-start(f32[4,2,16]{2,1,0:T(2,128)S(1)} %get-tuple-element.142), channel_id=1, source_target_pairs={{0,1},{1,2},{2,3},{3,4},{4,5},{5,6},{6,7},{7,8},{8,9},{9,10},{10,1... | collective-permute-start | bytes 1544 | tf_op jit(solution)/shard_map/ppermute | solution.py:87
  57.9 5.5 %collective-permute-start.5 = (f32[4,2,16]{2,1,0:T(2,128)S(1)}, f32[4,2,16]{2,1,0:T(2,128)S(1)}, u32[]{:S(2)}, u32[]{:S(2)}) collective-permute-start(f32[4,2,16]{2,1,0:T(2,128)S(1)} %get-tuple-element.143), channel_id=1, source_target_pairs={{1,0},{2,1},{3,2},{4,3},{5,4},{6,5},{7,6},{8,7},{9,8},{10,9},{11,1... | collective-permute-start | bytes 1544 | tf_op jit(solution)/shard_map/ppermute | solution.py:87
  63.5 1.3 %collective-permute-start.10 = (f32[4,2,2]{2,1,0:T(2,128)S(1)}, f32[4,2,2]{2,1,0:T(2,128)S(1)}, u32[]{:S(2)}, u32[]{:S(2)}) collective-permute-start(f32[4,2,2]{2,1,0:T(2,128)S(1)} %get-tuple-element.136), channel_id=1, source_target_pairs={{16,1},{17,2},{18,3},{19,4},{20,5},{21,6},{22,7},{23,8},{24,9},{25... | collective-permute-start | bytes 200 | tf_op jit(solution)/shard_map/ppermute | solution.py:87
  64.8 1.3 %collective-permute-start.11 = (f32[4,2,2]{2,1,0:T(2,128)S(1)}, f32[4,2,2]{2,1,0:T(2,128)S(1)}, u32[]{:S(2)}, u32[]{:S(2)}) collective-permute-start(f32[4,2,2]{2,1,0:T(2,128)S(1)} %get-tuple-element.137), channel_id=1, source_target_pairs={{17,0},{18,1},{19,2},{20,3},{21,4},{22,5},{23,6},{24,7},{25,8},{26... | collective-permute-start | bytes 200 | tf_op jit(solution)/shard_map/ppermute | solution.py:87
  66.1 11.1 %collective-permute-start.9 = (f32[4,2,2]{2,1,0:T(2,128)S(1)}, f32[4,2,2]{2,1,0:T(2,128)S(1)}, u32[]{:S(2)}, u32[]{:S(2)}) collective-permute-start(f32[4,2,2]{2,1,0:T(2,128)S(1)} %get-tuple-element.138), channel_id=1, source_target_pairs={{1,16},{2,17},{3,18},{4,19},{5,20},{6,21},{7,22},{8,23},{9,24},{10... | collective-permute-start | bytes 200 | tf_op jit(solution)/shard_map/ppermute | solution.py:87
  77.2 7.0 %collective-permute-start.8 = (f32[4,2,2]{2,1,0:T(2,128)S(1)}, f32[4,2,2]{2,1,0:T(2,128)S(1)}, u32[]{:S(2)}, u32[]{:S(2)}) collective-permute-start(f32[4,2,2]{2,1,0:T(2,128)S(1)} %get-tuple-element.139), channel_id=1, source_target_pairs={{0,17},{1,18},{2,19},{3,20},{4,21},{5,22},{6,23},{7,24},{8,25},{9,... | collective-permute-start | bytes 200 | tf_op jit(solution)/shard_map/ppermute | solution.py:87
  84.2 4.3 %collective-permute-start.6 = (f32[4,2,2]{2,1,0:T(2,128)S(1)}, f32[4,2,2]{2,1,0:T(2,128)S(1)}, u32[]{:S(2)}, u32[]{:S(2)}) collective-permute-start(f32[4,2,2]{2,1,0:T(2,128)S(1)} %get-tuple-element.141), channel_id=1, source_target_pairs={{0,16},{1,17},{2,18},{3,19},{4,20},{5,21},{6,22},{7,23},{8,24},{9,... | collective-permute-start | bytes 200 | tf_op jit(solution)/shard_map/ppermute | solution.py:87
  88.5 1.2 %collective-permute-done.6 = f32[4,2,2]{2,1,0:T(2,128)S(1)} collective-permute-done((f32[4,2,2]{2,1,0:T(2,128)S(1)}, f32[4,2,2]{2,1,0:T(2,128)S(1)}, u32[]{:S(2)}, u32[]{:S(2)}) %collective-permute-start.6) | collective-permute-done | bytes 96 | tf_op jit(solution)/shard_map/ppermute | solution.py:87
  89.8 1.3 %collective-permute-start.7 = (f32[4,2,2]{2,1,0:T(2,128)S(1)}, f32[4,2,2]{2,1,0:T(2,128)S(1)}, u32[]{:S(2)}, u32[]{:S(2)}) collective-permute-start(f32[4,2,2]{2,1,0:T(2,128)S(1)} %get-tuple-element.140), channel_id=1, source_target_pairs={{16,0},{17,1},{18,2},{19,3},{20,4},{21,5},{22,6},{23,7},{24,8},{25... | collective-permute-start | bytes 200 | tf_op jit(solution)/shard_map/ppermute | solution.py:87
  91.3 4.3 %collective-permute-done.7 = f32[4,2,2]{2,1,0:T(2,128)S(1)} collective-permute-done((f32[4,2,2]{2,1,0:T(2,128)S(1)}, f32[4,2,2]{2,1,0:T(2,128)S(1)}, u32[]{:S(2)}, u32[]{:S(2)}) %collective-permute-start.7) | collective-permute-done | bytes 96 | tf_op jit(solution)/shard_map/ppermute | solution.py:87
  95.6 0.6 scatter-add.21
  96.8 0.7 scatter-add.26
  97.4 0.7 scatter-add.29
  98.2 0.5 collective-permute-start.12
  98.7 0.8 collective-permute-done.13
  99.5 3.1 %collective-permute-done.12 = f32[2,16]{1,0:T(2,128)S(1)} collective-permute-done((f32[2,16]{1,0:T(2,128)S(1)}, f32[2,16]{1,0:T(2,128)S(1)}, u32[]{:S(2)}, u32[]{:S(2)}) %collective-permute-start.12) | collective-permute-done | bytes 160 | tf_op jit(solution)/shard_map/ppermute | solution.py:25
  102.6 0.7 add_bitcast_fusion
  (85 shorter events, 3.8 us)
Async XLA Ops:
  2.6 16.5 %copy-start.1 = (f32[3,128]{1,0:T(4,128)S(1)}, f32[3,128]{1,0:T(4,128)}, u32[]{:S(2)}) copy-start(f32[3,128]{1,0:T(4,128)} %param.27) | copy-start | bytes 4612
  2.9 38.1 %collective-permute-start = (bf16[7,32,2,128]{3,2,1,0:T(2,128)(2,1)S(1)}, bf16[7,32,2,128]{3,2,1,0:T(2,128)(2,1)}, u32[]{:S(2)}, u32[]{:S(2)}) collective-permute-start(bf16[7,32,2,128]{3,2,1,0:T(2,128)(2,1)S(1)} %pad_maximum_fusion.5), channel_id=1, source_target_pairs={{0,1},{1,2},{2,3},{3,4},{4,5},{5,6},{6,7},{7,8},{8,9},{9,10},{10,1... | collective-permute-start | bytes 344072 | tf_op jit(solution)/shard_map/ppermute | solution.py:143
  13.0 28.7 %collective-permute-start.1 = (bf16[7,32,2,128]{3,2,1,0:T(2,128)(2,1)}, bf16[7,32,2,128]{3,2,1,0:T(2,128)(2,1)}, u32[]{:S(2)}, u32[]{:S(2)}) collective-permute-start(bf16[7,32,2,128]{3,2,1,0:T(2,128)(2,1)} %pad_maximum_fusion.6), channel_id=1, source_target_pairs={{1,0},{2,1},{3,2},{4,3},{5,4},{6,5},{7,6},{8,7},{9,8},{10,9},{11,1... | collective-permute-start | bytes 344072 | tf_op jit(solution)/shard_map/ppermute | solution.py:148
  20.8 14.1 %collective-permute-start.3 = (bf16[7,32,16,2]{1,2,3,0:T(8,128)(2,1)}, bf16[7,32,16,2]{1,2,3,0:T(8,128)(2,1)}, u32[]{:S(2)}, u32[]{:S(2)}) collective-permute-start(bf16[7,32,16,2]{1,2,3,0:T(8,128)(2,1)} %pad_maximum_fusion.8), channel_id=1, source_target_pairs={{0,16},{16,32},{32,48},{1,17},{17,33},{33,49},{2,18},{18,34},{34,5... | collective-permute-start | bytes 43016 | tf_op jit(solution)/shard_map/ppermute | solution.py:143
  24.5 4.0 %copy-start.5 = (s32[8,2]{0,1:T(2,128)S(1)}, s32[8,2]{0,1:T(2,128)}, u32[]{:S(2)}) copy-start(s32[8,2]{0,1:T(2,128)} %param.30) | copy-start | bytes 196
  24.5 5.8 %copy-start.3 = (f32[3,32]{1,0:T(4,128)S(1)}, f32[3,32]{1,0:T(4,128)}, u32[]{:S(2)}) copy-start(f32[3,32]{1,0:T(4,128)} %param.29) | copy-start | bytes 1156
  24.5 7.1 %copy-start = (bf16[1,8,32,16,128]{4,3,2,1,0:T(8,128)(2,1)S(1)}, bf16[1,8,32,16,128]{4,3,2,1,0:T(8,128)(2,1)}, u32[]{:S(2)}) copy-start(bf16[1,8,32,16,128]{4,3,2,1,0:T(8,128)(2,1)} %param.26) | copy-start | bytes 3145732
  25.9 9.9 %collective-permute-start.2 = (bf16[7,32,16,2]{1,2,3,0:T(8,128)(2,1)}, bf16[7,32,16,2]{1,2,3,0:T(8,128)(2,1)}, u32[]{:S(2)}, u32[]{:S(2)}) collective-permute-start(bf16[7,32,16,2]{1,2,3,0:T(8,128)(2,1)} %pad_maximum_fusion.7), channel_id=1, source_target_pairs={{16,0},{32,16},{48,32},{17,1},{33,17},{49,33},{18,2},{34,18},{50,3... | collective-permute-start | bytes 43016 | tf_op jit(solution)/shard_map/ppermute | solution.py:148
  31.6 1.5 %copy-start.4 = (s32[8]{0:T(128)S(1)}, s32[8]{0:T(128)}, u32[]{:S(2)}) copy-start(s32[8]{0:T(128)} %param.31) | copy-start | bytes 100
  37.5 4.9 %copy-start.2 = (f32[3,16]{1,0:T(4,128)S(1)}, f32[3,16]{1,0:T(4,128)}, u32[]{:S(2)}) copy-start(f32[3,16]{1,0:T(4,128)} %param.28) | copy-start | bytes 580
  50.4 1.7 %copy-start.6 = (s32[18]{0:T(128)S(1)}, s32[18]{0:T(128)}, u32[]{:S(2)}) copy-start(s32[18]{0:T(128)} %get-tuple-element.178) | copy-start | bytes 220
  50.4 1.7 %copy-start.7 = (s32[18]{0:T(128)S(1)}, s32[18]{0:T(128)}, u32[]{:S(2)}) copy-start(s32[18]{0:T(128)} %broadcast_add_fusion.7) | copy-start | bytes 220
  52.7 24.4 %collective-permute-start.4 = (f32[4,2,16]{2,1,0:T(2,128)S(1)}, f32[4,2,16]{2,1,0:T(2,128)S(1)}, u32[]{:S(2)}, u32[]{:S(2)}) collective-permute-start(f32[4,2,16]{2,1,0:T(2,128)S(1)} %get-tuple-element.142), channel_id=1, source_target_pairs={{0,1},{1,2},{2,3},{3,4},{4,5},{5,6},{6,7},{7,8},{8,9},{9,10},{10,1... | collective-permute-start | bytes 1544 | tf_op jit(solution)/shard_map/ppermute | solution.py:87
  57.9 26.3 %collective-permute-start.5 = (f32[4,2,16]{2,1,0:T(2,128)S(1)}, f32[4,2,16]{2,1,0:T(2,128)S(1)}, u32[]{:S(2)}, u32[]{:S(2)}) collective-permute-start(f32[4,2,16]{2,1,0:T(2,128)S(1)} %get-tuple-element.143), channel_id=1, source_target_pairs={{1,0},{2,1},{3,2},{4,3},{5,4},{6,5},{7,6},{8,7},{9,8},{10,9},{11,1... | collective-permute-start | bytes 1544 | tf_op jit(solution)/shard_map/ppermute | solution.py:87
  63.5 33.2 %collective-permute-start.10 = (f32[4,2,2]{2,1,0:T(2,128)S(1)}, f32[4,2,2]{2,1,0:T(2,128)S(1)}, u32[]{:S(2)}, u32[]{:S(2)}) collective-permute-start(f32[4,2,2]{2,1,0:T(2,128)S(1)} %get-tuple-element.136), channel_id=1, source_target_pairs={{16,1},{17,2},{18,3},{19,4},{20,5},{21,6},{22,7},{23,8},{24,9},{25... | collective-permute-start | bytes 200 | tf_op jit(solution)/shard_map/ppermute | solution.py:87
  64.8 31.9 %collective-permute-start.11 = (f32[4,2,2]{2,1,0:T(2,128)S(1)}, f32[4,2,2]{2,1,0:T(2,128)S(1)}, u32[]{:S(2)}, u32[]{:S(2)}) collective-permute-start(f32[4,2,2]{2,1,0:T(2,128)S(1)} %get-tuple-element.137), channel_id=1, source_target_pairs={{17,0},{18,1},{19,2},{20,3},{21,4},{22,5},{23,6},{24,7},{25,8},{26... | collective-permute-start | bytes 200 | tf_op jit(solution)/shard_map/ppermute | solution.py:87
  66.1 30.2 %collective-permute-start.9 = (f32[4,2,2]{2,1,0:T(2,128)S(1)}, f32[4,2,2]{2,1,0:T(2,128)S(1)}, u32[]{:S(2)}, u32[]{:S(2)}) collective-permute-start(f32[4,2,2]{2,1,0:T(2,128)S(1)} %get-tuple-element.138), channel_id=1, source_target_pairs={{1,16},{2,17},{3,18},{4,19},{5,20},{6,21},{7,22},{8,23},{9,24},{10... | collective-permute-start | bytes 200 | tf_op jit(solution)/shard_map/ppermute | solution.py:87
  77.2 19.1 %collective-permute-start.8 = (f32[4,2,2]{2,1,0:T(2,128)S(1)}, f32[4,2,2]{2,1,0:T(2,128)S(1)}, u32[]{:S(2)}, u32[]{:S(2)}) collective-permute-start(f32[4,2,2]{2,1,0:T(2,128)S(1)} %get-tuple-element.139), channel_id=1, source_target_pairs={{0,17},{1,18},{2,19},{3,20},{4,21},{5,22},{6,23},{7,24},{8,25},{9,... | collective-permute-start | bytes 200 | tf_op jit(solution)/shard_map/ppermute | solution.py:87
  84.2 5.6 %collective-permute-start.6 = (f32[4,2,2]{2,1,0:T(2,128)S(1)}, f32[4,2,2]{2,1,0:T(2,128)S(1)}, u32[]{:S(2)}, u32[]{:S(2)}) collective-permute-start(f32[4,2,2]{2,1,0:T(2,128)S(1)} %get-tuple-element.141), channel_id=1, source_target_pairs={{0,16},{1,17},{2,18},{3,19},{4,20},{5,21},{6,22},{7,23},{8,24},{9,... | collective-permute-start | bytes 200 | tf_op jit(solution)/shard_map/ppermute | solution.py:87
  89.8 5.8 %collective-permute-start.7 = (f32[4,2,2]{2,1,0:T(2,128)S(1)}, f32[4,2,2]{2,1,0:T(2,128)S(1)}, u32[]{:S(2)}, u32[]{:S(2)}) collective-permute-start(f32[4,2,2]{2,1,0:T(2,128)S(1)} %get-tuple-element.140), channel_id=1, source_target_pairs={{16,0},{17,1},{18,2},{19,3},{20,4},{21,5},{22,6},{23,7},{24,8},{25... | collective-permute-start | bytes 200 | tf_op jit(solution)/shard_map/ppermute | solution.py:87
  98.2 1.3 %collective-permute-start.13 = (f32[2,16]{1,0:T(2,128)S(1)}, f32[2,16]{1,0:T(2,128)S(1)}, u32[]{:S(2)}, u32[]{:S(2)}) collective-permute-start(f32[2,16]{1,0:T(2,128)S(1)} %broadcast_multiply_fusion), channel_id=1, source_target_pairs={{64,0},{128,64},{192,128},{256,192},{320,256},{384,320},{448,384},... | collective-permute-start | bytes 392 | tf_op jit(solution)/shard_map/ppermute | solution.py:25
  98.2 4.4 %collective-permute-start.12 = (f32[2,16]{1,0:T(2,128)S(1)}, f32[2,16]{1,0:T(2,128)S(1)}, u32[]{:S(2)}, u32[]{:S(2)}) collective-permute-start(f32[2,16]{1,0:T(2,128)S(1)} %broadcast_multiply_fusion.1), channel_id=1, source_target_pairs={{448,0},{0,64},{64,128},{128,192},{192,256},{256,320},{320,384},{3... | collective-permute-start | bytes 392 | tf_op jit(solution)/shard_map/ppermute | solution.py:25

commit v5 on v3

--- a/solution.py
+++ b/solution.py
@@ -98,13 +98,20 @@
     return high + (middle + low)
 
 
+def rider_dim(piece):
+    return piece.ndim - 1 if piece.shape[-1] >= 9 else piece.ndim - 2
+
+
 def with_rider(piece, vector):
     parts = split_exact(vector)
-    carried = piece.shape[1]
+    dim = rider_dim(piece)
+    carried = piece.shape[dim]
     assert parts.shape[0] <= carried
     parts = jnp.pad(parts, (0, carried - parts.shape[0]))
     shape = (1,) + piece.shape[1:]
-    slab = jnp.broadcast_to(parts.reshape((1, carried) + (1,) * (piece.ndim - 2)), shape)
+    layout = [1] * piece.ndim
+    layout[dim] = carried
+    slab = jnp.broadcast_to(parts.reshape(layout), shape)
     return jnp.concatenate([piece, slab], axis=0)
 
 
@@ -119,7 +126,9 @@
         forward,
     )
     high = lax.ppermute(with_rider(lax.slice_in_dim(block, 0, width, axis=dim), coef[:, 0]), axis, backward)
-    rider_at = (-1, slice(0, size)) + (0,) * (block.ndim - 2)
+    rider_at = [-1] + [0] * (block.ndim - 1)
+    rider_at[rider_dim(low)] = slice(0, size)
+    rider_at = tuple(rider_at)
     coef_low = join_exact(low[rider_at])[:, None]
     coef_high = join_exact(high[rider_at])[:, None]
     return low[:-1], high[:-1], coef_low, coef_high
@@ -130,7 +139,7 @@
     length = core.shape[dim]
 
     def shifted(offset):
-        return lax.slice_in_dim(joined, 2 + offset, 2 + offset + length, axis=dim)
+        return lax.slice_in_dim(joined, 2 + offset, 2 + offset + length, axis=dim).astype(jnp.float32)
 
     return (8.0 * (shifted(1) - shifted(-1)) - (shifted(2) - shifted(-2))) / 12.0
 
@@ -157,12 +166,11 @@
     low_u, high_u, coef_low_u, coef_high_u = neighbour_rows(moving, coef_u, "au", 3, 2)
     low_v, high_v, coef_low_v, coef_high_v = neighbour_rows(moving, coef_v, "vert", 2, 2)
     values = stacked.astype(jnp.float32)
-    moving = moving.astype(jnp.float32)
     zero_w = jnp.zeros_like(moving[:, :2])
     slopes = (
         slopes_along(zero_w, moving, zero_w, 1),
-        slopes_along(low_v.astype(jnp.float32), moving, high_v.astype(jnp.float32), 2),
-        slopes_along(low_u.astype(jnp.float32), moving, high_u.astype(jnp.float32), 3),
+        slopes_along(low_v, moving, high_v, 2),
+        slopes_along(low_u, moving, high_u, 3),
     )
     product_sum = jnp.zeros(values.shape[1:], jnp.float32)
     div_flow = jnp.zeros(values.shape[1:], jnp.float32)

time: 84.4 us -> 88 us (1.043)
  local copies, waits for them, and re-layouts: 9.82 us -> 13.7 us
    slice x0 -> x6, local copies, waits for them, and re-layouts: none -> 5.92 us  [neighbour_rows(): return (low[:-1], high[:-1], coef_low, coef_high)]
    convert_element_type x5 -> x0, other arithmetic: 3.64 us -> none  [the longest x1 0.96 us: shards(): low_v.astype(jnp.float32)]
    concatenate x0 -> x2, other arithmetic: none -> 3 us  [slopes_along(): joined = jnp.concatenate([low, core, high], axis=dim)]
    convert_element_type x2 -> x0, local copies, waits for them, and re-layouts: 2.54 us -> none  [the longest x1 1.79 us: shards(): high_u.astype(jnp.float32)]
    concatenate x2 -> x3, other arithmetic: 0.51 us -> 1.47 us  [shards(): moving = jnp.concatenate([stacked[0:3], stacked[4:7]], axis=0)]
    div x1 -> x3, other arithmetic: 6.06 us -> 5.46 us  [slopes_along(): (8.0 * (shifted(1) - shifted(-1)) - (shifted(2) - shifted(-2))) / 12.0]
  transfers between devices with their start and end apart: 10 -> 10, of which waited for: 4 -> 4; matrix products, arithmetic and copies ran while one was open for 20% -> 28% of each run, Pallas kernels for 0% -> 0%
where the time goes in v5:
time: 88 us; the launch traced here: 86.4 us
  starting transfers between devices  36.1 us (41%)
  other arithmetic  21 us (24%)
  local copies, waits for them, and re-layouts  13.7 us (16%)
  waiting for transfers between devices  12 us (14%)
  between operations  2.99 us (3%)
    ppermute x2, starting transfers between devices, neighbour_rows(): lax.ppermute(with_rider(lax.slice_in_dim(block, block.shape[dim] - width,...  14.3 us
    ppermute x2, waiting for transfers between devices, with_halo(): lax.ppermute(lax.slice_in_dim(block, 0, width, axis=dim), axis, backward)  8.06 us
    ppermute x2, starting transfers between devices, with_halo(): lax.ppermute(lax.slice_in_dim(block, block.shape[dim] - width, None, axis...  7.53 us
    ppermute x2, starting transfers between devices, neighbour_rows(): lax.ppermute(with_rider(lax.slice_in_dim(block, 0, width, axis=dim), coef...  7.09 us
    ppermute x2, starting transfers between devices, with_halo(): lax.ppermute(lax.slice_in_dim(block, 0, width, axis=dim), axis, backward)  6.75 us
    slice x6, local copies, waits for them, and re-layouts, neighbour_rows(): return (low[:-1], high[:-1], coef_low, coef_high)  5.92 us
    div x3, other arithmetic, slopes_along(): (8.0 * (shifted(1) - shifted(-1)) - (shifted(2) - shifted(-2))) / 12.0  5.46 us
    ppermute x2, waiting for transfers between devices, from_behind(): return lax.ppermute(block, axis, route)  3.87 us
  transfers between devices with their start and end apart: 10, of which 4 were waited for; matrix products, arithmetic and copies ran while one was open for 28% of the time, Pallas kernels for 0%

profile of v5, /device:TPU:6, one launch (start us, length us, event | category | flops | bytes accessed | tf_op | source)
XLA Modules:
  0.0 86.4 jit_solution(10480811744229466527)
XLA Ops:
  0.0 1.0 %slice_reduce_fusion.2 = (f32[3]{0:T(128)S(1)}, f32[3]{0:T(128)S(1)}) fusion(f32[3,16]{1,0:T(4,128)} %param.20), kind=kLoop, calls=%fused_computation.111 | loop fusion | bytes 48 | tf_op jit(solution)/shard_map/slice | solution.py:128
  1.1 1.3 %slice_bitcast_fusion = (bf16[3,32,16,128]{3,2,1,0:T(8,128)(2,1)S(1)}, bf16[3,32,16,128]{3,2,1,0:T(8,128)(2,1)S(1)}) fusion(bf16[1,8,32,16,128]{4,3,2,1,0:T(8,128)(2,1)} %param.18), kind=kLoop, calls=%fused_computation.19 | loop fusion | bytes 1572864 | tf_op jit(solution)/shard_map/slice | solution.py:165
  2.8 9.1 %collective-permute-start = (bf16[7,32,2,128]{3,2,1,0:T(2,128)(2,1)S(1)}, bf16[7,32,2,128]{3,2,1,0:T(2,128)(2,1)}, u32[]{:S(2)}, u32[]{:S(2)}) collective-permute-start(bf16[7,32,2,128]{3,2,1,0:T(2,128)(2,1)S(1)} %pad_maximum_fusion.3), channel_id=1, source_target_pairs={{0,1},{1,2},{2,3},{3,4},{4,5},{5,6},{6,7},{7,8},{8,9},{9,10},{10,1... | collective-permute-start | bytes 344072 | tf_op jit(solution)/shard_map/ppermute | solution.py:123
  12.0 0.8 pad_maximum_fusion.4
  12.8 5.8 %collective-permute-start.1 = (bf16[7,32,2,128]{3,2,1,0:T(2,128)(2,1)}, bf16[7,32,2,128]{3,2,1,0:T(2,128)(2,1)}, u32[]{:S(2)}, u32[]{:S(2)}) collective-permute-start(bf16[7,32,2,128]{3,2,1,0:T(2,128)(2,1)} %pad_maximum_fusion.4), channel_id=1, source_target_pairs={{1,0},{2,1},{3,2},{4,3},{5,4},{6,5},{7,6},{8,7},{9,8},{10,9},{11,1... | collective-permute-start | bytes 344072 | tf_op jit(solution)/shard_map/ppermute | solution.py:128
  19.2 0.8 copy.79
  20.1 0.6 pad_maximum_fusion.5
  20.7 1.3 %collective-permute-start.2 = (bf16[7,32,16,2]{1,2,3,0:T(8,128)(2,1)}, bf16[7,32,16,2]{1,2,3,0:T(8,128)(2,1)}, u32[]{:S(2)}, u32[]{:S(2)}) collective-permute-start(bf16[7,32,16,2]{1,2,3,0:T(8,128)(2,1)} %pad_maximum_fusion.5), channel_id=1, source_target_pairs={{16,0},{32,16},{48,32},{17,1},{33,17},{49,33},{18,2},{34,18},{50,3... | collective-permute-start | bytes 43016 | tf_op jit(solution)/shard_map/ppermute | solution.py:128
  22.1 0.8 copy.81
  23.0 0.6 pad_maximum_fusion.6
  23.6 5.2 %collective-permute-start.3 = (bf16[7,32,16,2]{1,2,3,0:T(8,128)(2,1)}, bf16[7,32,16,2]{1,2,3,0:T(8,128)(2,1)}, u32[]{:S(2)}, u32[]{:S(2)}) collective-permute-start(bf16[7,32,16,2]{1,2,3,0:T(8,128)(2,1)} %pad_maximum_fusion.6), channel_id=1, source_target_pairs={{0,16},{16,32},{32,48},{1,17},{17,33},{33,49},{2,18},{18,34},{34,5... | collective-permute-start | bytes 43016 | tf_op jit(solution)/shard_map/ppermute | solution.py:123
  28.8 0.6 broadcast_add_fusion.5
  29.4 0.6 and_select_fusion.1
  30.0 1.0 %pad_maximum_fusion.1 = bf16[6,32,16,128]{3,2,1,0:T(8,128)(2,1)} fusion(bf16[3,32,16,128]{3,2,1,0:T(8,128)(2,1)S(1)} %get-tuple-element.75, bf16[3,32,16,128]{3,2,1,0:T(8,128)(2,1)S(1)} %get-tuple-element.76), kind=kLoop, calls=%fused_computation.9 | loop fusion | flops 393216 | bytes 1572864 | tf_op jit(solution)/shard_map/concatenate | solution.py:165
  30.9 0.6 constant_dynamic-slice_fusion.1
  32.9 2.6 %subtract_multiply_fusion.2 = f32[6,32,16,128]{3,2,1,0:T(8,128)S(1)} fusion(bf16[6,32,16,128]{3,2,1,0:T(8,128)(2,1)} %pad_maximum_fusion.1), kind=kLoop, calls=%fused_computation.4 | loop fusion | flops 3538944 | bytes 2359296 | tf_op jit(solution)/shard_map/div | solution.py:144
  35.5 0.7 select_add_fusion.2
  36.1 0.5 broadcast_add_fusion.7
  36.7 1.5 %convert_element_type.126 = f32[1,8,32,16,128]{4,3,2,1,0:T(8,128)} convert(bf16[1,8,32,16,128]{4,3,2,1,0:T(8,128)(2,1)S(1)} %copy-done.1) | non-fusion elementwise | flops 524288 | bytes 3145728 | tf_op jit(solution)/shard_map/convert_element_type | solution.py:168
  38.2 0.7 fusion.67
  40.2 0.7 slice_convert_fusion
  40.9 0.8 slice.467
  41.7 0.8 copy.82
  42.5 0.8 slice.463
  43.3 1.6 %copy.80 = bf16[6,32,16,2]{3,2,1,0:T(8,128)(2,1)} copy(bf16[6,32,16,2]{1,2,3,0:T(8,128)(2,1)S(1)} %slice.463) | data formatting | bytes 24576 | tf_op jit(solution)/shard_map/slice | solution.py:134
  44.9 2.1 %pad_maximum_fusion = (bf16[6,32,16,130]{3,2,1,0:T(8,128)(2,1)S(1)}, bf16[6,32,16,130]{3,2,1,0:T(8,128)(2,1)S(1)}) fusion(bf16[6,32,16,2]{3,2,1,0:T(8,128)(2,1)} %copy.80, bf16[3,32,16,128]{3,2,1,0:T(8,128)(2,1)S(1)} %get-tuple-element.75, bf16[3,32,16,128]{3,2,1,0:T(8,128)(2,1)S(1)} %get-tuple-element.76, bf16[6,32,16,2]{3,2,1,0:T(8,128)(2,1)S(1)} %copy.82), kind=kLoop, calls=%fused_computation | loop fusion | flops 4792320 | bytes 2408448 | tf_op jit(solution)/shard_map/concatenate | solution.py:138
  47.0 2.1 %subtract_multiply_fusion = f32[6,32,16,128]{3,2,1,0:T(8,128)} fusion(bf16[6,32,16,130]{3,2,1,0:T(8,128)(2,1)S(1)} %get-tuple-element.82, bf16[6,32,16,130]{3,2,1,0:T(8,128)(2,1)S(1)} %get-tuple-element.81), kind=kLoop, calls=%fused_computation.2 | loop fusion | flops 3538944 | bytes 4718592 | tf_op jit(solution)/shard_map/div | solution.py:144
  49.1 0.7 slice_convert_fusion.1
  49.9 0.6 slice_convert_fusion.3
  50.7 0.7 slice_convert_fusion.2
  51.6 1.0 %slice.451 = bf16[6,32,2,128]{3,2,1,0:T(2,128)(2,1)S(1)} slice(bf16[7,32,2,128]{3,2,1,0:T(2,128)(2,1)} %collective-permute-done), slice={[0:6], [0:32], [0:2], [0:128]} | slice | bytes 196608 | tf_op jit(solution)/shard_map/slice | solution.py:134
  52.6 1.0 %slice.449 = bf16[6,32,2,128]{3,2,1,0:T(2,128)(2,1)S(1)} slice(bf16[7,32,2,128]{3,2,1,0:T(2,128)(2,1)} %collective-permute-done.1), slice={[0:6], [0:32], [0:2], [0:128]} | slice | bytes 196608 | tf_op jit(solution)/shard_map/slice | solution.py:134
  53.5 0.9 %pad_maximum_fusion.2 = (bf16[6,32,18,128]{3,2,1,0:T(8,128)(2,1)S(1)}, bf16[6,32,18,128]{3,2,1,0:T(8,128)(2,1)S(1)}) fusion(bf16[6,32,2,128]{3,2,1,0:T(2,128)(2,1)S(1)} %slice.449, bf16[3,32,16,128]{3,2,1,0:T(8,128)(2,1)S(1)} %get-tuple-element.75, bf16[3,32,16,128]{3,2,1,0:T(8,128)(2,1)S(1)} %get-tuple-element.76, bf16[6,32,2,128]{3,2,1,0:T(2,128)(2,1)S(1)} %slice.451), kind=kLoop, calls=%fused_computation.14 | loop fusion | flops 5308416 | bytes 2752512 | tf_op jit(solution)/shard_map/concatenate | solution.py:138
  54.5 0.8 subtract_multiply_fusion.1
  55.3 0.6 copy-done
  55.9 1.4 %fusion.3 = f32[32,16,128]{2,1,0:T(8,128)S(1)} fusion(f32[1,8,32,16,128]{4,3,2,1,0:T(8,128)} %convert_element_type.126, f32[6,32,16,128]{3,2,1,0:T(8,128)S(1)} %copy-done, f32[6,32,16,128]{3,2,1,0:T(8,128)S(1)} %subtract_multiply_fusion.1, f32[6,32,16,128]{3,2,1,0:T(8,128)S(1)} %subtract_multiply_fusion.2), kind=kLoop, calls=%fused_computation.23 | loop fusion | flops 1638400 | bytes 5505024 | tf_op jit(solution)/shard_map/sub | solution.py:184
  57.3 0.3 fusion.15
  57.9 5.2 %collective-permute-start.4 = (f32[4,2,128]{2,1,0:T(2,128)S(1)}, f32[4,2,128]{2,1,0:T(2,128)S(1)}, u32[]{:S(2)}, u32[]{:S(2)}) collective-permute-start(f32[4,2,128]{2,1,0:T(2,128)S(1)} %get-tuple-element.85), channel_id=1, source_target_pairs={{0,1},{1,2},{2,3},{3,4},{4,5},{5,6},{6,7},{7,8},{8,9},{9,10},{10,1... | collective-permute-start | bytes 12296 | tf_op jit(solution)/shard_map/ppermute | solution.py:14
  63.1 5.5 %collective-permute-start.5 = (f32[4,2,128]{2,1,0:T(2,128)S(1)}, f32[4,2,128]{2,1,0:T(2,128)S(1)}, u32[]{:S(2)}, u32[]{:S(2)}) collective-permute-start(f32[4,2,128]{2,1,0:T(2,128)S(1)} %get-tuple-element.86), channel_id=1, source_target_pairs={{1,0},{2,1},{3,2},{4,3},{5,4},{6,5},{7,6},{8,7},{9,8},{10,9},{11,1... | collective-permute-start | bytes 12296 | tf_op jit(solution)/shard_map/ppermute | solution.py:17
  68.6 3.9 %collective-permute-done.5 = f32[4,2,128]{2,1,0:T(2,128)S(1)} collective-permute-done((f32[4,2,128]{2,1,0:T(2,128)S(1)}, f32[4,2,128]{2,1,0:T(2,128)S(1)}, u32[]{:S(2)}, u32[]{:S(2)}) %collective-permute-start.5) | collective-permute-done | bytes 4128 | tf_op jit(solution)/shard_map/ppermute | solution.py:17
  72.9 2.3 %collective-permute-start.6 = (f32[4,2,2]{2,0,1:T(4,128)S(1)}, f32[4,2,2]{2,0,1:T(4,128)S(1)}, u32[]{:S(2)}, u32[]{:S(2)}) collective-permute-start(f32[4,2,2]{2,0,1:T(4,128)S(1)} %get-tuple-element.91), channel_id=1, source_target_pairs={{0,16},{16,32},{32,48},{1,17},{17,33},{33,49},{2,18},{18,34},{34,5... | collective-permute-start | bytes 200 | tf_op jit(solution)/shard_map/ppermute | solution.py:14
  75.2 1.3 %collective-permute-start.7 = (f32[4,2,2]{2,0,1:T(4,128)S(1)}, f32[4,2,2]{2,0,1:T(4,128)S(1)}, u32[]{:S(2)}, u32[]{:S(2)}) collective-permute-start(f32[4,2,2]{2,0,1:T(4,128)S(1)} %get-tuple-element.90), channel_id=1, source_target_pairs={{16,0},{32,16},{48,32},{17,1},{33,17},{49,33},{18,2},{34,18},{50,3... | collective-permute-start | bytes 200 | tf_op jit(solution)/shard_map/ppermute | solution.py:17
  76.7 4.2 %collective-permute-done.7 = f32[4,2,2]{2,0,1:T(4,128)S(1)} collective-permute-done((f32[4,2,2]{2,0,1:T(4,128)S(1)}, f32[4,2,2]{2,0,1:T(4,128)S(1)}, u32[]{:S(2)}, u32[]{:S(2)}) %collective-permute-start.7) | collective-permute-done | bytes 96 | tf_op jit(solution)/shard_map/ppermute | solution.py:17
  80.9 0.3 scatter-add.9
  81.4 0.5 collective-permute-start.8
  81.9 0.8 collective-permute-done.9
  82.7 3.1 %collective-permute-done.8 = f32[2,16]{1,0:T(2,128)S(1)} collective-permute-done((f32[2,16]{1,0:T(2,128)S(1)}, f32[2,16]{1,0:T(2,128)S(1)}, u32[]{:S(2)}, u32[]{:S(2)}) %collective-permute-start.8) | collective-permute-done | bytes 160 | tf_op jit(solution)/shard_map/ppermute | solution.py:25
  85.8 0.6 copy.96
  (79 shorter events, 3.2 us)
Async XLA Ops:
  2.6 16.3 %copy-start.2 = (f32[3,128]{1,0:T(4,128)S(1)}, f32[3,128]{1,0:T(4,128)}, u32[]{:S(2)}) copy-start(f32[3,128]{1,0:T(4,128)} %param.19) | copy-start | bytes 4612
  2.8 47.1 %collective-permute-start = (bf16[7,32,2,128]{3,2,1,0:T(2,128)(2,1)S(1)}, bf16[7,32,2,128]{3,2,1,0:T(2,128)(2,1)}, u32[]{:S(2)}, u32[]{:S(2)}) collective-permute-start(bf16[7,32,2,128]{3,2,1,0:T(2,128)(2,1)S(1)} %pad_maximum_fusion.3), channel_id=1, source_target_pairs={{0,1},{1,2},{2,3},{3,4},{4,5},{5,6},{6,7},{7,8},{8,9},{9,10},{10,1... | collective-permute-start | bytes 344072 | tf_op jit(solution)/shard_map/ppermute | solution.py:123
  12.8 37.9 %collective-permute-start.1 = (bf16[7,32,2,128]{3,2,1,0:T(2,128)(2,1)}, bf16[7,32,2,128]{3,2,1,0:T(2,128)(2,1)}, u32[]{:S(2)}, u32[]{:S(2)}) collective-permute-start(bf16[7,32,2,128]{3,2,1,0:T(2,128)(2,1)} %pad_maximum_fusion.4), channel_id=1, source_target_pairs={{1,0},{2,1},{3,2},{4,3},{5,4},{6,5},{7,6},{8,7},{9,8},{10,9},{11,1... | collective-permute-start | bytes 344072 | tf_op jit(solution)/shard_map/ppermute | solution.py:128
  19.2 11.7 %copy-start.6 = (s32[8,2]{0,1:T(2,128)S(1)}, s32[8,2]{0,1:T(2,128)}, u32[]{:S(2)}) copy-start(s32[8,2]{0,1:T(2,128)} %param.22) | copy-start | bytes 196
  19.2 13.6 %copy-start.4 = (f32[3,32]{1,0:T(4,128)S(1)}, f32[3,32]{1,0:T(4,128)}, u32[]{:S(2)}) copy-start(f32[3,32]{1,0:T(4,128)} %param.21) | copy-start | bytes 1156
  20.7 19.5 %collective-permute-start.2 = (bf16[7,32,16,2]{1,2,3,0:T(8,128)(2,1)}, bf16[7,32,16,2]{1,2,3,0:T(8,128)(2,1)}, u32[]{:S(2)}, u32[]{:S(2)}) collective-permute-start(bf16[7,32,16,2]{1,2,3,0:T(8,128)(2,1)} %pad_maximum_fusion.5), channel_id=1, source_target_pairs={{16,0},{32,16},{48,32},{17,1},{33,17},{49,33},{18,2},{34,18},{50,3... | collective-permute-start | bytes 43016 | tf_op jit(solution)/shard_map/ppermute | solution.py:128
  23.6 17.3 %collective-permute-start.3 = (bf16[7,32,16,2]{1,2,3,0:T(8,128)(2,1)}, bf16[7,32,16,2]{1,2,3,0:T(8,128)(2,1)}, u32[]{:S(2)}, u32[]{:S(2)}) collective-permute-start(bf16[7,32,16,2]{1,2,3,0:T(8,128)(2,1)} %pad_maximum_fusion.6), channel_id=1, source_target_pairs={{0,16},{16,32},{32,48},{1,17},{17,33},{33,49},{2,18},{18,34},{34,5... | collective-permute-start | bytes 43016 | tf_op jit(solution)/shard_map/ppermute | solution.py:123
  30.9 5.7 %copy-start.1 = (bf16[1,8,32,16,128]{4,3,2,1,0:T(8,128)(2,1)S(1)}, bf16[1,8,32,16,128]{4,3,2,1,0:T(8,128)(2,1)}, u32[]{:S(2)}) copy-start(bf16[1,8,32,16,128]{4,3,2,1,0:T(8,128)(2,1)} %param.18) | copy-start | bytes 3145732
  36.7 1.5 %copy-start.5 = (s32[8]{0:T(128)S(1)}, s32[8]{0:T(128)}, u32[]{:S(2)}) copy-start(s32[8]{0:T(128)} %param.23) | copy-start | bytes 100
  47.0 4.5 %copy-start.3 = (f32[3,16]{1,0:T(4,128)S(1)}, f32[3,16]{1,0:T(4,128)}, u32[]{:S(2)}) copy-start(f32[3,16]{1,0:T(4,128)} %param.20) | copy-start | bytes 580
  54.5 1.4 %copy-start = (f32[6,32,16,128]{3,2,1,0:T(8,128)S(1)}, f32[6,32,16,128]{3,2,1,0:T(8,128)}, u32[]{:S(2)}) copy-start(f32[6,32,16,128]{3,2,1,0:T(8,128)} %subtract_multiply_fusion) | copy-start | bytes 4718596
  55.9 1.7 %copy-start.7 = (s32[18]{0:T(128)S(1)}, s32[18]{0:T(128)}, u32[]{:S(2)}) copy-start(s32[18]{0:T(128)} %get-tuple-element.122) | copy-start | bytes 220
  55.9 1.8 %copy-start.8 = (s32[18]{0:T(128)S(1)}, s32[18]{0:T(128)}, u32[]{:S(2)}) copy-start(s32[18]{0:T(128)} %get-tuple-element.123) | copy-start | bytes 220
  55.9 1.8 %copy-start.9 = (s32[18]{0:T(128)S(1)}, s32[18]{0:T(128)}, u32[]{:S(2)}) copy-start(s32[18]{0:T(128)} %broadcast_add_fusion.7) | copy-start | bytes 220
  57.9 10.7 %collective-permute-start.4 = (f32[4,2,128]{2,1,0:T(2,128)S(1)}, f32[4,2,128]{2,1,0:T(2,128)S(1)}, u32[]{:S(2)}, u32[]{:S(2)}) collective-permute-start(f32[4,2,128]{2,1,0:T(2,128)S(1)} %get-tuple-element.85), channel_id=1, source_target_pairs={{0,1},{1,2},{2,3},{3,4},{4,5},{5,6},{6,7},{7,8},{8,9},{9,10},{10,1... | collective-permute-start | bytes 12296 | tf_op jit(solution)/shard_map/ppermute | solution.py:14
  63.1 9.4 %collective-permute-start.5 = (f32[4,2,128]{2,1,0:T(2,128)S(1)}, f32[4,2,128]{2,1,0:T(2,128)S(1)}, u32[]{:S(2)}, u32[]{:S(2)}) collective-permute-start(f32[4,2,128]{2,1,0:T(2,128)S(1)} %get-tuple-element.86), channel_id=1, source_target_pairs={{1,0},{2,1},{3,2},{4,3},{5,4},{6,5},{7,6},{8,7},{9,8},{10,9},{11,1... | collective-permute-start | bytes 12296 | tf_op jit(solution)/shard_map/ppermute | solution.py:17
  72.9 3.6 %collective-permute-start.6 = (f32[4,2,2]{2,0,1:T(4,128)S(1)}, f32[4,2,2]{2,0,1:T(4,128)S(1)}, u32[]{:S(2)}, u32[]{:S(2)}) collective-permute-start(f32[4,2,2]{2,0,1:T(4,128)S(1)} %get-tuple-element.91), channel_id=1, source_target_pairs={{0,16},{16,32},{32,48},{1,17},{17,33},{33,49},{2,18},{18,34},{34,5... | collective-permute-start | bytes 200 | tf_op jit(solution)/shard_map/ppermute | solution.py:14
  75.2 5.6 %collective-permute-start.7 = (f32[4,2,2]{2,0,1:T(4,128)S(1)}, f32[4,2,2]{2,0,1:T(4,128)S(1)}, u32[]{:S(2)}, u32[]{:S(2)}) collective-permute-start(f32[4,2,2]{2,0,1:T(4,128)S(1)} %get-tuple-element.90), channel_id=1, source_target_pairs={{16,0},{32,16},{48,32},{17,1},{33,17},{49,33},{18,2},{34,18},{50,3... | collective-permute-start | bytes 200 | tf_op jit(solution)/shard_map/ppermute | solution.py:17
  81.4 1.3 %collective-permute-start.9 = (f32[2,16]{1,0:T(2,128)S(1)}, f32[2,16]{1,0:T(2,128)S(1)}, u32[]{:S(2)}, u32[]{:S(2)}) collective-permute-start(f32[2,16]{1,0:T(2,128)S(1)} %broadcast_multiply_fusion), channel_id=1, source_target_pairs={{64,0},{128,64},{192,128},{256,192},{320,256},{384,320},{448,384},... | collective-permute-start | bytes 392 | tf_op jit(solution)/shard_map/ppermute | solution.py:25
  81.4 4.4 %collective-permute-start.8 = (f32[2,16]{1,0:T(2,128)S(1)}, f32[2,16]{1,0:T(2,128)S(1)}, u32[]{:S(2)}, u32[]{:S(2)}) collective-permute-start(f32[2,16]{1,0:T(2,128)S(1)} %broadcast_multiply_fusion.1), channel_id=1, source_target_pairs={{448,0},{0,64},{64,128},{128,192},{192,256},{256,320},{320,384},{3... | collective-permute-start | bytes 392 | tf_op jit(solution)/shard_map/ppermute | solution.py:25

commit v6 on v3

--- a/solution.py
+++ b/solution.py
@@ -1,3 +1,4 @@
+import numpy as np
 import jax
 import jax.numpy as jnp
 from jax import lax
@@ -90,43 +91,50 @@
     rest = vector - high
     middle = lax.reduce_precision(rest, exponent_bits=8, mantissa_bits=7)
     low = rest - middle
-    return jnp.stack([high, middle, low]).astype(jnp.bfloat16).reshape(-1)
+    return jnp.stack([high, middle, low]).astype(jnp.bfloat16)
 
 
 def join_exact(parts):
-    high, middle, low = parts.astype(jnp.float32).reshape(3, -1)
-    return high + (middle + low)
+    parts = parts.astype(jnp.float32)
+    return parts[0] + (parts[1] + parts[2])
+
+
+def spread_dim(piece):
+    return piece.ndim - 1 if piece.shape[-1] >= 3 else piece.ndim - 2
 
 
 def with_rider(piece, vector):
     parts = split_exact(vector)
-    carried = piece.shape[1]
-    assert parts.shape[0] <= carried
-    parts = jnp.pad(parts, (0, carried - parts.shape[0]))
     shape = (1,) + piece.shape[1:]
-    slab = jnp.broadcast_to(parts.reshape((1, carried) + (1,) * (piece.ndim - 2)), shape)
+    spread = spread_dim(piece)
+    assert shape[1] >= parts.shape[0] and shape[spread] >= parts.shape[1]
+    grid = jnp.pad(parts, ((0, shape[1] - parts.shape[0]), (0, shape[spread] - parts.shape[1])))
+    layout = [1] * piece.ndim
+    layout[1] = shape[1]
+    layout[spread] = shape[spread]
+    slab = jnp.broadcast_to(grid.reshape(layout), shape)
     return jnp.concatenate([piece, slab], axis=0)
 
 
-def neighbour_rows(block, coef, axis, dim, width):
+def neighbour_rows(stacked, coef, axis, dim, width):
     count = lax.axis_size(axis)
     forward = [(i, i + 1) for i in range(count - 1)]
     backward = [(target, source) for source, target in forward]
-    size = coef.shape[0] * 3
+    length = stacked.shape[dim]
     low = lax.ppermute(
-        with_rider(lax.slice_in_dim(block, block.shape[dim] - width, None, axis=dim), coef[:, -1]),
-        axis,
-        forward,
-    )
-    high = lax.ppermute(with_rider(lax.slice_in_dim(block, 0, width, axis=dim), coef[:, 0]), axis, backward)
-    rider_at = (-1, slice(0, size)) + (0,) * (block.ndim - 2)
+        with_rider(lax.slice_in_dim(stacked, length - width, None, axis=dim), coef[:, -1]), axis, forward
+    )
+    high = lax.ppermute(with_rider(lax.slice_in_dim(stacked, 0, width, axis=dim), coef[:, 0]), axis, backward)
+    rider_at = [-1, slice(0, 3)] + [0] * (stacked.ndim - 2)
+    rider_at[spread_dim(low)] = slice(0, coef.shape[0])
+    rider_at = tuple(rider_at)
     coef_low = join_exact(low[rider_at])[:, None]
     coef_high = join_exact(high[rider_at])[:, None]
     return low[:-1], high[:-1], coef_low, coef_high
 
 
 def slopes_along(low, core, high, dim):
-    joined = jnp.concatenate([low, core, high], axis=dim)
+    joined = jnp.concatenate([low.astype(jnp.float32), core, high.astype(jnp.float32)], axis=dim)
     length = core.shape[dim]
 
     def shifted(offset):
@@ -137,8 +145,8 @@
 
 def smoothed_band(coef_ext, columns, offset):
     rows = coef_ext.shape[1] - 2
-    target = jnp.floor_divide(jnp.arange(-1, rows + 1), RATIO)[:, None] + offset
-    column = jnp.arange(columns)[None, :]
+    target = np.floor_divide(np.arange(-1, rows + 1), RATIO)[:, None] + offset
+    column = np.arange(columns)[None, :]
     band = jnp.zeros((rows + 2, columns), jnp.float32)
     for d in range(3):
         band = band + jnp.where(column == target + (d - 1), coef_ext[d][:, None], 0.0)
@@ -156,24 +164,27 @@
     moving = jnp.concatenate([stacked[0:3], stacked[4:7]], axis=0)
     low_u, high_u, coef_low_u, coef_high_u = neighbour_rows(moving, coef_u, "au", 3, 2)
     low_v, high_v, coef_low_v, coef_high_v = neighbour_rows(moving, coef_v, "vert", 2, 2)
-    values = stacked.astype(jnp.float32)
     moving = moving.astype(jnp.float32)
     zero_w = jnp.zeros_like(moving[:, :2])
     slopes = (
         slopes_along(zero_w, moving, zero_w, 1),
-        slopes_along(low_v.astype(jnp.float32), moving, high_v.astype(jnp.float32), 2),
-        slopes_along(low_u.astype(jnp.float32), moving, high_u.astype(jnp.float32), 3),
-    )
-    product_sum = jnp.zeros(values.shape[1:], jnp.float32)
-    div_flow = jnp.zeros(values.shape[1:], jnp.float32)
-    div_adjoint = jnp.zeros(values.shape[1:], jnp.float32)
+        slopes_along(low_v, moving, high_v, 2),
+        slopes_along(low_u, moving, high_u, 3),
+    )
+    product_sum = jnp.zeros(moving.shape[1:], jnp.float32)
+    div_flow = jnp.zeros(moving.shape[1:], jnp.float32)
+    div_adjoint = jnp.zeros(moving.shape[1:], jnp.float32)
     for direction, slope in enumerate(slopes):
         component = 2 - direction
         for k in range(3):
             product_sum = product_sum + slope[k] * slope[3 + k]
         div_flow = div_flow + slope[component]
         div_adjoint = div_adjoint + slope[3 + component]
-    density = product_sum - values[3] * div_adjoint - values[7] * div_flow
+    density = (
+        product_sum
+        - stacked[3].astype(jnp.float32) * div_adjoint
+        - stacked[7].astype(jnp.float32) * div_flow
+    )
     zero_coef = jnp.zeros_like(coef_w[:, :1])
     mat_w = smoothed_band(jnp.concatenate([zero_coef, coef_w, zero_coef], axis=1), layers_w // RATIO, 0)
     mat_v = smoothed_band(jnp.concatenate([coef_low_v, coef_v, coef_high_v], axis=1), columns_v, 2)

time: 84.4 us -> 75.2 us (0.89)
  other arithmetic: 21.3 us -> 13.1 us
    convert_element_type x9 -> x8, other arithmetic: 7.81 us -> 3.29 us  [the longest x4 1.35 us: join_exact(): parts = parts.astype(jnp.float32)]
    concatenate x4, other arithmetic: 2.25 us -> 1 us  [with_rider(): return jnp.concatenate([piece, slab], axis=0)]
    add x9 -> x4, other arithmetic: 1.23 us -> 0.16 us  [join_exact(): return parts[0] + (parts[1] + parts[2])]
    convert_element_type x6 -> x2, local copies, waits for them, and re-layouts: 2.88 us -> 2.57 us  [the longest x1 1.82 us: slopes_along(): high.astype(jnp.float32)]
  transfers between devices with their start and end apart: 10 -> 10, of which waited for: 4 -> 4; matrix products, arithmetic and copies ran while one was open for 20% -> 11% of each run, Pallas kernels for 0% -> 0%
where the time goes in v6:
time: 75.2 us; the launch traced here: 74.4 us
  starting transfers between devices  36.1 us (48%)
  other arithmetic  13.1 us (17%)
  waiting for transfers between devices  11.8 us (16%)
  local copies, waits for them, and re-layouts  9.56 us (13%)
  between operations  3.1 us (4%)
    ppermute x2, starting transfers between devices, neighbour_rows(): lax.ppermute(with_rider(lax.slice_in_dim(stacked, length - width, None, a...  13.6 us
    ppermute x2, starting transfers between devices, with_halo(): lax.ppermute(lax.slice_in_dim(block, block.shape[dim] - width, None, axis...  8.12 us
    ppermute x2, waiting for transfers between devices, with_halo(): lax.ppermute(lax.slice_in_dim(block, 0, width, axis=dim), axis, backward)  7.89 us
    ppermute x2, starting transfers between devices, neighbour_rows(): lax.ppermute(with_rider(lax.slice_in_dim(stacked, 0, width, axis=dim), co...  7.1 us
    ppermute x2, starting transfers between devices, with_halo(): lax.ppermute(lax.slice_in_dim(block, 0, width, axis=dim), axis, backward)  6.75 us
    div x1, other arithmetic, slopes_along(): (8.0 * (shifted(1) - shifted(-1)) - (shifted(2) - shifted(-2))) / 12.0  6.02 us
    ppermute x2, waiting for transfers between devices, from_behind(): return lax.ppermute(block, axis, route)  3.87 us
    convert_element_type x1, local copies, waits for them, and re-layouts, slopes_along(): high.astype(jnp.float32)  1.82 us
  transfers between devices with their start and end apart: 10, of which 4 were waited for; matrix products, arithmetic and copies ran while one was open for 11% of the time, Pallas kernels for 0%

profile of v6, /device:TPU:6, one launch (start us, length us, event | category | flops | bytes accessed | tf_op | source)
XLA Modules:
  0.0 74.4 jit_solution(12130766945615126353)
XLA Ops:
  0.0 1.0 %slice_reduce_fusion.2 = (f32[3]{0:T(128)S(1)}, f32[3]{0:T(128)S(1)}) fusion(f32[3,16]{1,0:T(4,128)} %param.29), kind=kLoop, calls=%fused_computation.146 | loop fusion | bytes 48 | tf_op jit(solution)/shard_map/slice | solution.py:127
  1.0 1.3 %slice_bitcast_fusion = (bf16[3,32,16,128]{3,2,1,0:T(8,128)(2,1)S(1)}, bf16[3,32,16,128]{3,2,1,0:T(8,128)(2,1)S(1)}) fusion(bf16[1,8,32,16,128]{4,3,2,1,0:T(8,128)(2,1)} %param.27), kind=kLoop, calls=%fused_computation.48 | loop fusion | bytes 1572864 | tf_op jit(solution)/shard_map/slice | solution.py:164
  2.2 0.2 fusion.36
  2.5 0.2 pad_maximum_fusion.5
  2.7 9.1 %collective-permute-start = (bf16[7,32,2,128]{3,2,1,0:T(2,128)(2,1)S(1)}, bf16[7,32,2,128]{3,2,1,0:T(2,128)(2,1)}, u32[]{:S(2)}, u32[]{:S(2)}) collective-permute-start(bf16[7,32,2,128]{3,2,1,0:T(2,128)(2,1)S(1)} %pad_maximum_fusion.5), channel_id=1, source_target_pairs={{0,1},{1,2},{2,3},{3,4},{4,5},{5,6},{6,7},{7,8},{8,9},{9,10},{10,1... | collective-permute-start | bytes 344072 | tf_op jit(solution)/shard_map/ppermute | solution.py:124
  11.8 0.8 %pad_maximum_fusion.6 = bf16[7,32,2,128]{3,2,1,0:T(2,128)(2,1)} fusion(bf16[1,32,2,128]{3,2,1,0:T(2,128)(2,1)S(1)} %broadcast_in_dim.123, bf16[6,32,2,128]{3,2,1,0:T(2,128)(2,1)S(1)} %get-tuple-element.80), kind=kLoop, calls=%fused_computation.72 | loop fusion | flops 57344 | bytes 229376 | tf_op jit(solution)/shard_map/concatenate | solution.py:116
  12.6 5.8 %collective-permute-start.1 = (bf16[7,32,2,128]{3,2,1,0:T(2,128)(2,1)}, bf16[7,32,2,128]{3,2,1,0:T(2,128)(2,1)}, u32[]{:S(2)}, u32[]{:S(2)}) collective-permute-start(bf16[7,32,2,128]{3,2,1,0:T(2,128)(2,1)} %pad_maximum_fusion.6), channel_id=1, source_target_pairs={{1,0},{2,1},{3,2},{4,3},{5,4},{6,5},{7,6},{8,7},{9,8},{10,9},{11,1... | collective-permute-start | bytes 344072 | tf_op jit(solution)/shard_map/ppermute | solution.py:127
  18.5 0.3 fusion.20
  18.8 0.2 slice_reduce_fusion
  19.0 0.1 copy.114
  19.1 0.8 %copy.103 = bf16[6,32,16,2]{1,2,3,0:T(8,128)(2,1)S(1)} copy(bf16[6,32,16,2]{3,2,1,0:T(8,128)(2,1)S(1)} %get-tuple-element.83) | data formatting | bytes 24576 | tf_op jit(solution)/shard_map/slice | solution.py:127
  19.9 1.3 %collective-permute-start.2 = (bf16[7,32,16,2]{1,2,3,0:T(8,128)(2,1)S(1)}, bf16[7,32,16,2]{1,2,3,0:T(8,128)(2,1)S(1)}, u32[]{:S(2)}, u32[]{:S(2)}) collective-permute-start(bf16[7,32,16,2]{1,2,3,0:T(8,128)(2,1)S(1)} %pad_maximum_fusion.7), channel_id=1, source_target_pairs={{16,0},{32,16},{48,32},{17,1},{33,17},{49,33},{18,2},{34,18},{50,3... | collective-permute-start | bytes 43016 | tf_op jit(solution)/shard_map/ppermute | solution.py:127
  21.2 0.1 copy.115
  21.4 0.8 %copy.106 = bf16[6,32,16,2]{1,2,3,0:T(8,128)(2,1)S(1)} copy(bf16[6,32,16,2]{3,2,1,0:T(8,128)(2,1)S(1)} %get-tuple-element.82) | data formatting | bytes 24576 | tf_op jit(solution)/shard_map/slice | solution.py:125
  22.2 4.5 %collective-permute-start.3 = (bf16[7,32,16,2]{1,2,3,0:T(8,128)(2,1)S(1)}, bf16[7,32,16,2]{1,2,3,0:T(8,128)(2,1)S(1)}, u32[]{:S(2)}, u32[]{:S(2)}) collective-permute-start(bf16[7,32,16,2]{1,2,3,0:T(8,128)(2,1)S(1)} %pad_maximum_fusion.8), channel_id=1, source_target_pairs={{0,16},{16,32},{32,48},{1,17},{17,33},{33,49},{2,18},{18,34},{34,5... | collective-permute-start | bytes 43016 | tf_op jit(solution)/shard_map/ppermute | solution.py:124
  26.7 0.1 fusion.21
  26.9 0.7 constant_dynamic-slice_fusion
  28.8 0.1 pad_maximum_fusion.10
  29.0 0.7 fusion.102
  31.1 0.8 %copy.107 = f32[6,32,16,2]{3,2,1,0:T(8,128)S(1)} copy(f32[6,32,16,2]{1,2,3,0:T(8,128)S(1)} %slice_convert_fusion.2) | data formatting | bytes 49152 | tf_op jit(solution)/shard_map/convert_element_type | solution.py:137
  31.9 1.8 %copy.104 = f32[6,32,16,2]{3,2,1,0:T(8,128)} copy(f32[6,32,16,2]{1,2,3,0:T(8,128)S(1)} %slice_convert_fusion.3) | data formatting | bytes 49152 | tf_op jit(solution)/shard_map/convert_element_type | solution.py:137
  33.7 0.1 pad_maximum_fusion.14
  33.8 0.7 slice_convert_fusion.5
  34.5 0.1 copy.100
  34.6 0.7 slice_convert_fusion.4
  35.2 0.1 copy.101
  35.3 0.1 pad_maximum_fusion.9
  35.4 1.0 %slice_convert_fusion = f32[6,32,2,128]{3,2,1,0:T(2,128)S(1)} fusion(bf16[7,32,2,128]{3,2,1,0:T(2,128)(2,1)} %collective-permute-done), kind=kLoop, calls=%fused_computation.75 | loop fusion | flops 49152 | bytes 294912 | tf_op jit(solution)/shard_map/convert_element_type | solution.py:137
  36.4 1.0 %slice_convert_fusion.1 = f32[6,32,2,128]{3,2,1,0:T(2,128)S(1)} fusion(bf16[7,32,2,128]{3,2,1,0:T(2,128)(2,1)} %collective-permute-done.1), kind=kLoop, calls=%fused_computation.76 | loop fusion | flops 49152 | bytes 294912 | tf_op jit(solution)/shard_map/convert_element_type | solution.py:137
  37.4 6.0 %fusion.3 = (f32[6,32,16,128]{3,2,1,0:T(8,128)S(1)}, f32[6,32,16,128]{3,2,1,0:T(8,128)S(1)}, f32[6,32,16,128]{3,2,1,0:T(8,128)S(1)}) fusion(f32[6,32,16,128]{3,2,1,0:T(8,128)S(1)} %fusion.21, f32[6,32,16,2]{3,2,1,0:T(8,128)S(1)} %copy.107, f32[6,32,16,2]{3,2,1,0:T(8,128)} %copy.104, f32[6,32,2,128]{3,2,1,0:T(2,128)S(1)} %slice_convert_fusion, ...), kind=kLoop, calls=%fused_computation.15 | loop fusion | flops 9043968 | bytes 6733824 | tf_op jit(solution)/shard_map/div | solution.py:143
  43.5 1.3 %fusion.25 = f32[32,16,128]{2,1,0:T(8,128)S(1)} fusion(f32[6,32,16,128]{3,2,1,0:T(8,128)S(1)} %get-tuple-element.76, f32[6,32,16,128]{3,2,1,0:T(8,128)S(1)} %get-tuple-element.77, f32[6,32,16,128]{3,2,1,0:T(8,128)S(1)} %get-tuple-element.75, bf16[1,8,32,16,128]{4,3,2,1,0:T(8,128)(2,1)} %param.27), kind=kLoop, calls=%fused_computation.54 | loop fusion | flops 1769472 | bytes 5242880 | tf_op jit(solution)/shard_map/sub | solution.py:184
  44.8 0.3 fusion.33
  45.1 0.2 convolution_bitcast_fusion
  45.4 5.2 %collective-permute-start.4 = (f32[4,2,128]{2,1,0:T(2,128)S(1)}, f32[4,2,128]{2,1,0:T(2,128)S(1)}, u32[]{:S(2)}, u32[]{:S(2)}) collective-permute-start(f32[4,2,128]{2,1,0:T(2,128)S(1)} %get-tuple-element.84), channel_id=1, source_target_pairs={{0,1},{1,2},{2,3},{3,4},{4,5},{5,6},{6,7},{7,8},{8,9},{9,10},{10,1... | collective-permute-start | bytes 12296 | tf_op jit(solution)/shard_map/ppermute | solution.py:15
  50.6 5.5 %collective-permute-start.5 = (f32[4,2,128]{2,1,0:T(2,128)S(1)}, f32[4,2,128]{2,1,0:T(2,128)S(1)}, u32[]{:S(2)}, u32[]{:S(2)}) collective-permute-start(f32[4,2,128]{2,1,0:T(2,128)S(1)} %get-tuple-element.85), channel_id=1, source_target_pairs={{1,0},{2,1},{3,2},{4,3},{5,4},{6,5},{7,6},{8,7},{9,8},{10,9},{11,1... | collective-permute-start | bytes 12296 | tf_op jit(solution)/shard_map/ppermute | solution.py:18
  56.1 3.9 %collective-permute-done.5 = f32[4,2,128]{2,1,0:T(2,128)S(1)} collective-permute-done((f32[4,2,128]{2,1,0:T(2,128)S(1)}, f32[4,2,128]{2,1,0:T(2,128)S(1)}, u32[]{:S(2)}, u32[]{:S(2)}) %collective-permute-start.5) | collective-permute-done | bytes 4128 | tf_op jit(solution)/shard_map/ppermute | solution.py:18
  60.0 0.2 fusion.47
  60.2 0.1 slice.527
  60.4 2.9 %collective-permute-start.6 = (f32[4,2,2]{2,0,1:T(4,128)S(1)}, f32[4,2,2]{2,0,1:T(4,128)S(1)}, u32[]{:S(2)}, u32[]{:S(2)}) collective-permute-start(f32[4,2,2]{2,0,1:T(4,128)S(1)} %get-tuple-element.90), channel_id=1, source_target_pairs={{0,16},{16,32},{32,48},{1,17},{17,33},{33,49},{2,18},{18,34},{34,5... | collective-permute-start | bytes 200 | tf_op jit(solution)/shard_map/ppermute | solution.py:15
  63.3 1.3 %collective-permute-start.7 = (f32[4,2,2]{2,0,1:T(4,128)S(1)}, f32[4,2,2]{2,0,1:T(4,128)S(1)}, u32[]{:S(2)}, u32[]{:S(2)}) collective-permute-start(f32[4,2,2]{2,0,1:T(4,128)S(1)} %get-tuple-element.89), channel_id=1, source_target_pairs={{16,0},{32,16},{48,32},{17,1},{33,17},{49,33},{18,2},{34,18},{50,3... | collective-permute-start | bytes 200 | tf_op jit(solution)/shard_map/ppermute | solution.py:18
  64.7 0.1 scatter-add.6
  64.8 4.0 %collective-permute-done.7 = f32[4,2,2]{2,0,1:T(4,128)S(1)} collective-permute-done((f32[4,2,2]{2,0,1:T(4,128)S(1)}, f32[4,2,2]{2,0,1:T(4,128)S(1)}, u32[]{:S(2)}, u32[]{:S(2)}) %collective-permute-start.7) | collective-permute-done | bytes 96 | tf_op jit(solution)/shard_map/ppermute | solution.py:18
  68.9 0.3 scatter-add.9
  69.2 0.1 multiply_reduce_fusion.1
  69.4 0.5 collective-permute-start.8
  69.8 0.8 %collective-permute-done.9 = f32[2,16]{1,0:T(2,128)S(1)} collective-permute-done((f32[2,16]{1,0:T(2,128)S(1)}, f32[2,16]{1,0:T(2,128)S(1)}, u32[]{:S(2)}, u32[]{:S(2)}) %collective-permute-start.9) | collective-permute-done | bytes 160 | tf_op jit(solution)/shard_map/ppermute | solution.py:26
  70.6 3.1 %collective-permute-done.8 = f32[2,16]{1,0:T(2,128)S(1)} collective-permute-done((f32[2,16]{1,0:T(2,128)S(1)}, f32[2,16]{1,0:T(2,128)S(1)}, u32[]{:S(2)}, u32[]{:S(2)}) %collective-permute-start.8) | collective-permute-done | bytes 160 | tf_op jit(solution)/shard_map/ppermute | solution.py:26
  73.8 0.6 copy.123
  (72 shorter events, 0.9 us)
Async XLA Ops:
  2.5 16.3 %copy-start = (f32[3,128]{1,0:T(4,128)S(1)}, f32[3,128]{1,0:T(4,128)}, u32[]{:S(2)}) copy-start(f32[3,128]{1,0:T(4,128)} %param.28) | copy-start | bytes 4612
  2.7 31.1 %collective-permute-start = (bf16[7,32,2,128]{3,2,1,0:T(2,128)(2,1)S(1)}, bf16[7,32,2,128]{3,2,1,0:T(2,128)(2,1)}, u32[]{:S(2)}, u32[]{:S(2)}) collective-permute-start(bf16[7,32,2,128]{3,2,1,0:T(2,128)(2,1)S(1)} %pad_maximum_fusion.5), channel_id=1, source_target_pairs={{0,1},{1,2},{2,3},{3,4},{4,5},{5,6},{6,7},{7,8},{8,9},{9,10},{10,1... | collective-permute-start | bytes 344072 | tf_op jit(solution)/shard_map/ppermute | solution.py:124
  12.6 21.9 %collective-permute-start.1 = (bf16[7,32,2,128]{3,2,1,0:T(2,128)(2,1)}, bf16[7,32,2,128]{3,2,1,0:T(2,128)(2,1)}, u32[]{:S(2)}, u32[]{:S(2)}) collective-permute-start(bf16[7,32,2,128]{3,2,1,0:T(2,128)(2,1)} %pad_maximum_fusion.6), channel_id=1, source_target_pairs={{1,0},{2,1},{3,2},{4,3},{5,4},{6,5},{7,6},{8,7},{9,8},{10,9},{11,1... | collective-permute-start | bytes 344072 | tf_op jit(solution)/shard_map/ppermute | solution.py:127
  19.9 11.0 %collective-permute-start.2 = (bf16[7,32,16,2]{1,2,3,0:T(8,128)(2,1)S(1)}, bf16[7,32,16,2]{1,2,3,0:T(8,128)(2,1)S(1)}, u32[]{:S(2)}, u32[]{:S(2)}) collective-permute-start(bf16[7,32,16,2]{1,2,3,0:T(8,128)(2,1)S(1)} %pad_maximum_fusion.7), channel_id=1, source_target_pairs={{16,0},{32,16},{48,32},{17,1},{33,17},{49,33},{18,2},{34,18},{50,3... | collective-permute-start | bytes 43016 | tf_op jit(solution)/shard_map/ppermute | solution.py:127
  21.3 5.5 %copy-start.10 = (s32[8,2]{0,1:T(2,128)S(1)}, s32[8,2]{0,1:T(2,128)}, u32[]{:S(2)}) copy-start(s32[8,2]{0,1:T(2,128)} %param.31) | copy-start | bytes 196
  21.3 7.5 %copy-start.5 = (f32[3,32]{1,0:T(4,128)S(1)}, f32[3,32]{1,0:T(4,128)}, u32[]{:S(2)}) copy-start(f32[3,32]{1,0:T(4,128)} %param.30) | copy-start | bytes 1156
  21.3 7.6 %copy-start.11 = (pred[34,4]{0,1:T(4,128)(4,1)S(1)}, pred[34,4]{0,1:T(4,128)(4,1)}, u32[]{:S(2)}) copy-start(pred[34,4]{0,1:T(4,128)(4,1)} %constant.198.clone) | copy-start | bytes 412
  21.3 7.6 %copy-start.12 = (pred[34,4]{0,1:T(4,128)(4,1)S(1)}, pred[34,4]{0,1:T(4,128)(4,1)}, u32[]{:S(2)}) copy-start(pred[34,4]{0,1:T(4,128)(4,1)} %constant.197.clone) | copy-start | bytes 412
  21.4 7.6 %copy-start.13 = (pred[34,4]{0,1:T(4,128)(4,1)S(1)}, pred[34,4]{0,1:T(4,128)(4,1)}, u32[]{:S(2)}) copy-start(pred[34,4]{0,1:T(4,128)(4,1)} %constant.196.clone) | copy-start | bytes 412
  21.4 7.6 %copy-start.6 = (s32[8]{0:T(128)S(1)}, s32[8]{0:T(128)}, u32[]{:S(2)}) copy-start(s32[8]{0:T(128)} %param.32) | copy-start | bytes 100
  22.2 8.9 %collective-permute-start.3 = (bf16[7,32,16,2]{1,2,3,0:T(8,128)(2,1)S(1)}, bf16[7,32,16,2]{1,2,3,0:T(8,128)(2,1)S(1)}, u32[]{:S(2)}, u32[]{:S(2)}) collective-permute-start(bf16[7,32,16,2]{1,2,3,0:T(8,128)(2,1)S(1)} %pad_maximum_fusion.8), channel_id=1, source_target_pairs={{0,16},{16,32},{32,48},{1,17},{17,33},{33,49},{2,18},{18,34},{34,5... | collective-permute-start | bytes 43016 | tf_op jit(solution)/shard_map/ppermute | solution.py:124
  31.1 4.2 %copy-start.1 = (f32[3,16]{1,0:T(4,128)S(1)}, f32[3,16]{1,0:T(4,128)}, u32[]{:S(2)}) copy-start(f32[3,16]{1,0:T(4,128)} %param.29) | copy-start | bytes 580
  43.4 1.7 %copy-start.7 = (pred[18,6]{0,1:T(8,128)(4,1)S(1)}, pred[18,6]{0,1:T(8,128)(4,1)}, u32[]{:S(2)}) copy-start(pred[18,6]{0,1:T(8,128)(4,1)} %constant.201.clone) | copy-start | bytes 328
  43.4 1.7 %copy-start.8 = (pred[18,6]{0,1:T(8,128)(4,1)S(1)}, pred[18,6]{0,1:T(8,128)(4,1)}, u32[]{:S(2)}) copy-start(pred[18,6]{0,1:T(8,128)(4,1)} %constant.200.clone) | copy-start | bytes 328
  43.4 1.7 %copy-start.9 = (pred[18,6]{0,1:T(8,128)(4,1)S(1)}, pred[18,6]{0,1:T(8,128)(4,1)}, u32[]{:S(2)}) copy-start(pred[18,6]{0,1:T(8,128)(4,1)} %constant.199.clone) | copy-start | bytes 328
  43.4 12.6 %copy-start.2 = (pred[130,20]{0,1:T(8,128)(4,1)S(1)}, pred[130,20]{0,1:T(8,128)(4,1)}, u32[]{:S(2)}) copy-start(pred[130,20]{0,1:T(8,128)(4,1)} %constant.204.clone) | copy-start | bytes 7804
  43.4 12.6 %copy-start.3 = (pred[130,20]{0,1:T(8,128)(4,1)S(1)}, pred[130,20]{0,1:T(8,128)(4,1)}, u32[]{:S(2)}) copy-start(pred[130,20]{0,1:T(8,128)(4,1)} %constant.203.clone) | copy-start | bytes 7804
  43.4 12.6 %copy-start.4 = (pred[130,20]{0,1:T(8,128)(4,1)S(1)}, pred[130,20]{0,1:T(8,128)(4,1)}, u32[]{:S(2)}) copy-start(pred[130,20]{0,1:T(8,128)(4,1)} %constant.202.clone) | copy-start | bytes 7804
  45.4 10.7 %collective-permute-start.4 = (f32[4,2,128]{2,1,0:T(2,128)S(1)}, f32[4,2,128]{2,1,0:T(2,128)S(1)}, u32[]{:S(2)}, u32[]{:S(2)}) collective-permute-start(f32[4,2,128]{2,1,0:T(2,128)S(1)} %get-tuple-element.84), channel_id=1, source_target_pairs={{0,1},{1,2},{2,3},{3,4},{4,5},{5,6},{6,7},{7,8},{8,9},{9,10},{10,1... | collective-permute-start | bytes 12296 | tf_op jit(solution)/shard_map/ppermute | solution.py:15
  50.6 9.4 %collective-permute-start.5 = (f32[4,2,128]{2,1,0:T(2,128)S(1)}, f32[4,2,128]{2,1,0:T(2,128)S(1)}, u32[]{:S(2)}, u32[]{:S(2)}) collective-permute-start(f32[4,2,128]{2,1,0:T(2,128)S(1)} %get-tuple-element.85), channel_id=1, source_target_pairs={{1,0},{2,1},{3,2},{4,3},{5,4},{6,5},{7,6},{8,7},{9,8},{10,9},{11,1... | collective-permute-start | bytes 12296 | tf_op jit(solution)/shard_map/ppermute | solution.py:18
  60.4 4.2 %collective-permute-start.6 = (f32[4,2,2]{2,0,1:T(4,128)S(1)}, f32[4,2,2]{2,0,1:T(4,128)S(1)}, u32[]{:S(2)}, u32[]{:S(2)}) collective-permute-start(f32[4,2,2]{2,0,1:T(4,128)S(1)} %get-tuple-element.90), channel_id=1, source_target_pairs={{0,16},{16,32},{32,48},{1,17},{17,33},{33,49},{2,18},{18,34},{34,5... | collective-permute-start | bytes 200 | tf_op jit(solution)/shard_map/ppermute | solution.py:15
  63.3 5.5 %collective-permute-start.7 = (f32[4,2,2]{2,0,1:T(4,128)S(1)}, f32[4,2,2]{2,0,1:T(4,128)S(1)}, u32[]{:S(2)}, u32[]{:S(2)}) collective-permute-start(f32[4,2,2]{2,0,1:T(4,128)S(1)} %get-tuple-element.89), channel_id=1, source_target_pairs={{16,0},{32,16},{48,32},{17,1},{33,17},{49,33},{18,2},{34,18},{50,3... | collective-permute-start | bytes 200 | tf_op jit(solution)/shard_map/ppermute | solution.py:18
  69.3 1.3 %collective-permute-start.9 = (f32[2,16]{1,0:T(2,128)S(1)}, f32[2,16]{1,0:T(2,128)S(1)}, u32[]{:S(2)}, u32[]{:S(2)}) collective-permute-start(f32[2,16]{1,0:T(2,128)S(1)} %broadcast_multiply_fusion), channel_id=1, source_target_pairs={{64,0},{128,64},{192,128},{256,192},{320,256},{384,320},{448,384},... | collective-permute-start | bytes 392 | tf_op jit(solution)/shard_map/ppermute | solution.py:26
  69.4 4.4 %collective-permute-start.8 = (f32[2,16]{1,0:T(2,128)S(1)}, f32[2,16]{1,0:T(2,128)S(1)}, u32[]{:S(2)}, u32[]{:S(2)}) collective-permute-start(f32[2,16]{1,0:T(2,128)S(1)} %broadcast_multiply_fusion.1), channel_id=1, source_target_pairs={{448,0},{0,64},{64,128},{128,192},{192,256},{256,320},{320,384},{3... | collective-permute-start | bytes 392 | tf_op jit(solution)/shard_map/ppermute | solution.py:26

commit v7 on v6

--- a/solution.py
+++ b/solution.py
@@ -195,15 +195,19 @@
     patch_index = lax.axis_index("patch")
     patches = lax.axis_size("patch")
     layers_d = reduced.shape[0]
-    out_index = jnp.where(orient[patch_index, 0] == 1, 0, layers_d - 1).astype(jnp.int32)
-    in_index = jnp.where(orient[patch_index, 1] == 1, layers_d - 1, 0).astype(jnp.int32)
-    layer_ids = jnp.arange(layers_d)
-    out_mask = (layer_ids == out_index).astype(jnp.float32)[:, None, None]
-    in_mask = (layer_ids == in_index).astype(jnp.float32)[:, None, None]
+    ids = jnp.arange(patches)
+    here = ids == patch_index
+    before = ids == (patch_index + patches - 1) % patches
+    orient_here = jnp.sum(jnp.where(here[:, None], orient, 0), axis=0, keepdims=True)
+    out_index = jnp.where(orient_here[:, 0:1] == 1, 0, layers_d - 1)
+    in_index = jnp.where(orient_here[:, 1:2] == 1, layers_d - 1, 0)
+    layer_ids = jnp.arange(layers_d)[:, None]
+    out_mask = (layer_ids == out_index).astype(jnp.float32)[:, :, None]
+    in_mask = (layer_ids == in_index).astype(jnp.float32)[:, :, None]
     out_face = jnp.sum(out_mask * reduced, axis=0)
     in_face = jnp.sum(in_mask * reduced, axis=0)
-    gate_here = link[patch_index].astype(jnp.float32)
-    gate_before = link[(patch_index + patches - 1) % patches].astype(jnp.float32)
+    gate_here = jnp.sum(jnp.where(here, link, 0), keepdims=True).astype(jnp.float32)[:, None]
+    gate_before = jnp.sum(jnp.where(before, link, 0), keepdims=True).astype(jnp.float32)[:, None]
     from_before = from_behind(out_face * gate_here, "patch", 1)
     from_after = from_behind(in_face * gate_before, "patch", -1)
     design = reduced + in_mask * from_before[None] + out_mask * from_after[None]

time: 75.2 us -> 75.3 us (level)
  other arithmetic: 13.1 us -> 13.9 us
    dynamic_slice x2 -> x0, local copies, waits for them, and re-layouts: 1.31 us -> none  [the longest x1 0.66 us: shards(): gate_here = link[patch_index].astype(jnp.float32)]
    reduce_sum x0 -> x2, other arithmetic: none -> 0.81 us  [the longest x1 0.69 us: shards(): jnp.sum(jnp.where(here, link, 0), keepdims=True).astype(jnp.float32)]
where the time goes in v7:
time: 75.3 us; the launch traced here: 74.5 us
  starting transfers between devices  36.1 us (48%)
  other arithmetic  13.9 us (18%)
  waiting for transfers between devices  11.8 us (16%)
  local copies, waits for them, and re-layouts  8.85 us (12%)
  between operations  3.06 us (4%)
    ppermute x2, starting transfers between devices, neighbour_rows(): lax.ppermute(with_rider(lax.slice_in_dim(stacked, length - width, None, a...  13.6 us
    ppermute x2, starting transfers between devices, with_halo(): lax.ppermute(lax.slice_in_dim(block, block.shape[dim] - width, None, axis...  8.12 us
    ppermute x2, waiting for transfers between devices, with_halo(): lax.ppermute(lax.slice_in_dim(block, 0, width, axis=dim), axis, backward)  7.89 us
    ppermute x2, starting transfers between devices, neighbour_rows(): lax.ppermute(with_rider(lax.slice_in_dim(stacked, 0, width, axis=dim), co...  7.1 us
    ppermute x2, starting transfers between devices, with_halo(): lax.ppermute(lax.slice_in_dim(block, 0, width, axis=dim), axis, backward)  6.75 us
    div x1, other arithmetic, slopes_along(): (8.0 * (shifted(1) - shifted(-1)) - (shifted(2) - shifted(-2))) / 12.0  6.07 us
    ppermute x2, waiting for transfers between devices, from_behind(): return lax.ppermute(block, axis, route)  3.87 us
    convert_element_type x1, local copies, waits for them, and re-layouts, slopes_along(): high.astype(jnp.float32)  1.82 us
  transfers between devices with their start and end apart: 10, of which 4 were waited for; matrix products, arithmetic and copies ran while one was open for 11% of the time, Pallas kernels for 0%

profile of v7, /device:TPU:6, one launch (start us, length us, event | category | flops | bytes accessed | tf_op | source)
XLA Modules:
  0.0 74.5 jit_solution(17604675480362475491)
XLA Ops:
  0.0 1.0 %slice_reduce_fusion.2 = (f32[3]{0:T(128)S(1)}, f32[3]{0:T(128)S(1)}) fusion(f32[3,16]{1,0:T(4,128)} %param.29), kind=kLoop, calls=%fused_computation.146 | loop fusion | bytes 48 | tf_op jit(solution)/shard_map/slice | solution.py:127
  1.0 1.3 %slice_bitcast_fusion = (bf16[3,32,16,128]{3,2,1,0:T(8,128)(2,1)S(1)}, bf16[3,32,16,128]{3,2,1,0:T(8,128)(2,1)S(1)}) fusion(bf16[1,8,32,16,128]{4,3,2,1,0:T(8,128)(2,1)} %param.27), kind=kLoop, calls=%fused_computation.48 | loop fusion | bytes 1572864 | tf_op jit(solution)/shard_map/slice | solution.py:164
  2.2 0.2 fusion.36
  2.5 0.2 pad_maximum_fusion.5
  2.7 9.1 %collective-permute-start = (bf16[7,32,2,128]{3,2,1,0:T(2,128)(2,1)S(1)}, bf16[7,32,2,128]{3,2,1,0:T(2,128)(2,1)}, u32[]{:S(2)}, u32[]{:S(2)}) collective-permute-start(bf16[7,32,2,128]{3,2,1,0:T(2,128)(2,1)S(1)} %pad_maximum_fusion.5), channel_id=1, source_target_pairs={{0,1},{1,2},{2,3},{3,4},{4,5},{5,6},{6,7},{7,8},{8,9},{9,10},{10,1... | collective-permute-start | bytes 344072 | tf_op jit(solution)/shard_map/ppermute | solution.py:124
  11.8 0.8 %pad_maximum_fusion.6 = bf16[7,32,2,128]{3,2,1,0:T(2,128)(2,1)} fusion(bf16[1,32,2,128]{3,2,1,0:T(2,128)(2,1)S(1)} %broadcast_in_dim.155, bf16[6,32,2,128]{3,2,1,0:T(2,128)(2,1)S(1)} %get-tuple-element.82), kind=kLoop, calls=%fused_computation.72 | loop fusion | flops 57344 | bytes 229376 | tf_op jit(solution)/shard_map/concatenate | solution.py:116
  12.6 5.8 %collective-permute-start.1 = (bf16[7,32,2,128]{3,2,1,0:T(2,128)(2,1)}, bf16[7,32,2,128]{3,2,1,0:T(2,128)(2,1)}, u32[]{:S(2)}, u32[]{:S(2)}) collective-permute-start(bf16[7,32,2,128]{3,2,1,0:T(2,128)(2,1)} %pad_maximum_fusion.6), channel_id=1, source_target_pairs={{1,0},{2,1},{3,2},{4,3},{5,4},{6,5},{7,6},{8,7},{9,8},{10,9},{11,1... | collective-permute-start | bytes 344072 | tf_op jit(solution)/shard_map/ppermute | solution.py:127
  18.5 0.3 fusion.20
  18.8 0.2 slice_reduce_fusion
  19.0 0.1 copy.114
  19.1 0.8 %copy.103 = bf16[6,32,16,2]{1,2,3,0:T(8,128)(2,1)S(1)} copy(bf16[6,32,16,2]{3,2,1,0:T(8,128)(2,1)S(1)} %get-tuple-element.85) | data formatting | bytes 24576 | tf_op jit(solution)/shard_map/slice | solution.py:127
  19.9 1.3 %collective-permute-start.2 = (bf16[7,32,16,2]{1,2,3,0:T(8,128)(2,1)S(1)}, bf16[7,32,16,2]{1,2,3,0:T(8,128)(2,1)S(1)}, u32[]{:S(2)}, u32[]{:S(2)}) collective-permute-start(bf16[7,32,16,2]{1,2,3,0:T(8,128)(2,1)S(1)} %pad_maximum_fusion.7), channel_id=1, source_target_pairs={{16,0},{32,16},{48,32},{17,1},{33,17},{49,33},{18,2},{34,18},{50,3... | collective-permute-start | bytes 43016 | tf_op jit(solution)/shard_map/ppermute | solution.py:127
  21.2 0.1 copy.115
  21.4 0.8 %copy.106 = bf16[6,32,16,2]{1,2,3,0:T(8,128)(2,1)S(1)} copy(bf16[6,32,16,2]{3,2,1,0:T(8,128)(2,1)S(1)} %get-tuple-element.84) | data formatting | bytes 24576 | tf_op jit(solution)/shard_map/slice | solution.py:125
  22.2 4.5 %collective-permute-start.3 = (bf16[7,32,16,2]{1,2,3,0:T(8,128)(2,1)S(1)}, bf16[7,32,16,2]{1,2,3,0:T(8,128)(2,1)S(1)}, u32[]{:S(2)}, u32[]{:S(2)}) collective-permute-start(bf16[7,32,16,2]{1,2,3,0:T(8,128)(2,1)S(1)} %pad_maximum_fusion.8), channel_id=1, source_target_pairs={{0,16},{16,32},{32,48},{1,17},{17,33},{33,49},{2,18},{18,34},{34,5... | collective-permute-start | bytes 43016 | tf_op jit(solution)/shard_map/ppermute | solution.py:124
  26.7 0.1 fusion.21
  26.9 0.1 select_reduce_fusion
  27.0 0.6 fusion.103
  28.9 0.1 pad_maximum_fusion.10
  29.0 0.7 select_reduce_fusion.1
  31.2 0.8 %copy.107 = f32[6,32,16,2]{3,2,1,0:T(8,128)S(1)} copy(f32[6,32,16,2]{1,2,3,0:T(8,128)S(1)} %slice_convert_fusion.2) | data formatting | bytes 49152 | tf_op jit(solution)/shard_map/convert_element_type | solution.py:137
  31.9 1.8 %copy.104 = f32[6,32,16,2]{3,2,1,0:T(8,128)} copy(f32[6,32,16,2]{1,2,3,0:T(8,128)S(1)} %slice_convert_fusion.3) | data formatting | bytes 49152 | tf_op jit(solution)/shard_map/convert_element_type | solution.py:137
  33.8 0.1 pad_maximum_fusion.14
  33.8 0.7 slice_convert_fusion.5
  34.5 0.1 copy.100
  34.6 0.7 slice_convert_fusion.4
  35.3 0.1 copy.101
  35.5 1.0 %slice_convert_fusion = f32[6,32,2,128]{3,2,1,0:T(2,128)S(1)} fusion(bf16[7,32,2,128]{3,2,1,0:T(2,128)(2,1)} %collective-permute-done), kind=kLoop, calls=%fused_computation.75 | loop fusion | flops 49152 | bytes 294912 | tf_op jit(solution)/shard_map/convert_element_type | solution.py:137
  36.4 1.0 %slice_convert_fusion.1 = f32[6,32,2,128]{3,2,1,0:T(2,128)S(1)} fusion(bf16[7,32,2,128]{3,2,1,0:T(2,128)(2,1)} %collective-permute-done.1), kind=kLoop, calls=%fused_computation.76 | loop fusion | flops 49152 | bytes 294912 | tf_op jit(solution)/shard_map/convert_element_type | solution.py:137
  37.4 6.1 %fusion.3 = (f32[6,32,16,128]{3,2,1,0:T(8,128)S(1)}, f32[6,32,16,128]{3,2,1,0:T(8,128)S(1)}, f32[6,32,16,128]{3,2,1,0:T(8,128)S(1)}) fusion(f32[6,32,16,128]{3,2,1,0:T(8,128)S(1)} %fusion.21, f32[6,32,16,2]{3,2,1,0:T(8,128)S(1)} %copy.107, f32[6,32,16,2]{3,2,1,0:T(8,128)} %copy.104, f32[6,32,2,128]{3,2,1,0:T(2,128)S(1)} %slice_convert_fusion, ...), kind=kLoop, calls=%fused_computation.15 | loop fusion | flops 9043968 | bytes 6733824 | tf_op jit(solution)/shard_map/div | solution.py:143
  43.6 1.3 %fusion.25 = f32[32,16,128]{2,1,0:T(8,128)S(1)} fusion(f32[6,32,16,128]{3,2,1,0:T(8,128)S(1)} %get-tuple-element.78, f32[6,32,16,128]{3,2,1,0:T(8,128)S(1)} %get-tuple-element.79, f32[6,32,16,128]{3,2,1,0:T(8,128)S(1)} %get-tuple-element.77, bf16[1,8,32,16,128]{4,3,2,1,0:T(8,128)(2,1)} %param.27), kind=kLoop, calls=%fused_computation.54 | loop fusion | flops 1769472 | bytes 5242880 | tf_op jit(solution)/shard_map/sub | solution.py:184
  44.9 0.3 fusion.33
  45.3 0.2 convolution_bitcast_fusion
  45.5 5.2 %collective-permute-start.4 = (f32[4,2,128]{2,1,0:T(2,128)S(1)}, f32[4,2,128]{2,1,0:T(2,128)S(1)}, u32[]{:S(2)}, u32[]{:S(2)}) collective-permute-start(f32[4,2,128]{2,1,0:T(2,128)S(1)} %get-tuple-element.86), channel_id=1, source_target_pairs={{0,1},{1,2},{2,3},{3,4},{4,5},{5,6},{6,7},{7,8},{8,9},{9,10},{10,1... | collective-permute-start | bytes 12296 | tf_op jit(solution)/shard_map/ppermute | solution.py:15
  50.7 5.5 %collective-permute-start.5 = (f32[4,2,128]{2,1,0:T(2,128)S(1)}, f32[4,2,128]{2,1,0:T(2,128)S(1)}, u32[]{:S(2)}, u32[]{:S(2)}) collective-permute-start(f32[4,2,128]{2,1,0:T(2,128)S(1)} %get-tuple-element.87), channel_id=1, source_target_pairs={{1,0},{2,1},{3,2},{4,3},{5,4},{6,5},{7,6},{8,7},{9,8},{10,9},{11,1... | collective-permute-start | bytes 12296 | tf_op jit(solution)/shard_map/ppermute | solution.py:18
  56.2 3.9 %collective-permute-done.5 = f32[4,2,128]{2,1,0:T(2,128)S(1)} collective-permute-done((f32[4,2,128]{2,1,0:T(2,128)S(1)}, f32[4,2,128]{2,1,0:T(2,128)S(1)}, u32[]{:S(2)}, u32[]{:S(2)}) %collective-permute-start.5) | collective-permute-done | bytes 4128 | tf_op jit(solution)/shard_map/ppermute | solution.py:18
  60.1 0.2 fusion.47
  60.3 0.1 slice.535
  60.5 2.9 %collective-permute-start.6 = (f32[4,2,2]{2,0,1:T(4,128)S(1)}, f32[4,2,2]{2,0,1:T(4,128)S(1)}, u32[]{:S(2)}, u32[]{:S(2)}) collective-permute-start(f32[4,2,2]{2,0,1:T(4,128)S(1)} %get-tuple-element.92), channel_id=1, source_target_pairs={{0,16},{16,32},{32,48},{1,17},{17,33},{33,49},{2,18},{18,34},{34,5... | collective-permute-start | bytes 200 | tf_op jit(solution)/shard_map/ppermute | solution.py:15
  63.4 1.3 %collective-permute-start.7 = (f32[4,2,2]{2,0,1:T(4,128)S(1)}, f32[4,2,2]{2,0,1:T(4,128)S(1)}, u32[]{:S(2)}, u32[]{:S(2)}) collective-permute-start(f32[4,2,2]{2,0,1:T(4,128)S(1)} %get-tuple-element.91), channel_id=1, source_target_pairs={{16,0},{32,16},{48,32},{17,1},{33,17},{49,33},{18,2},{34,18},{50,3... | collective-permute-start | bytes 200 | tf_op jit(solution)/shard_map/ppermute | solution.py:18
  64.8 0.1 scatter-add.6
  64.9 4.0 %collective-permute-done.7 = f32[4,2,2]{2,0,1:T(4,128)S(1)} collective-permute-done((f32[4,2,2]{2,0,1:T(4,128)S(1)}, f32[4,2,2]{2,0,1:T(4,128)S(1)}, u32[]{:S(2)}, u32[]{:S(2)}) %collective-permute-start.7) | collective-permute-done | bytes 96 | tf_op jit(solution)/shard_map/ppermute | solution.py:18
  69.0 0.3 scatter-add.9
  69.3 0.1 multiply_reduce_fusion.1
  69.5 0.5 collective-permute-start.8
  70.0 0.8 %collective-permute-done.9 = f32[2,16]{1,0:T(2,128)S(1)} collective-permute-done((f32[2,16]{1,0:T(2,128)S(1)}, f32[2,16]{1,0:T(2,128)S(1)}, u32[]{:S(2)}, u32[]{:S(2)}) %collective-permute-start.9) | collective-permute-done | bytes 160 | tf_op jit(solution)/shard_map/ppermute | solution.py:26
  70.7 3.1 %collective-permute-done.8 = f32[2,16]{1,0:T(2,128)S(1)} collective-permute-done((f32[2,16]{1,0:T(2,128)S(1)}, f32[2,16]{1,0:T(2,128)S(1)}, u32[]{:S(2)}, u32[]{:S(2)}) %collective-permute-start.8) | collective-permute-done | bytes 160 | tf_op jit(solution)/shard_map/ppermute | solution.py:26
  73.9 0.6 copy.123
  (74 shorter events, 0.9 us)
Async XLA Ops:
  2.5 16.3 %copy-start = (f32[3,128]{1,0:T(4,128)S(1)}, f32[3,128]{1,0:T(4,128)}, u32[]{:S(2)}) copy-start(f32[3,128]{1,0:T(4,128)} %param.28) | copy-start | bytes 4612
  2.7 31.1 %collective-permute-start = (bf16[7,32,2,128]{3,2,1,0:T(2,128)(2,1)S(1)}, bf16[7,32,2,128]{3,2,1,0:T(2,128)(2,1)}, u32[]{:S(2)}, u32[]{:S(2)}) collective-permute-start(bf16[7,32,2,128]{3,2,1,0:T(2,128)(2,1)S(1)} %pad_maximum_fusion.5), channel_id=1, source_target_pairs={{0,1},{1,2},{2,3},{3,4},{4,5},{5,6},{6,7},{7,8},{8,9},{9,10},{10,1... | collective-permute-start | bytes 344072 | tf_op jit(solution)/shard_map/ppermute | solution.py:124
  12.6 22.0 %collective-permute-start.1 = (bf16[7,32,2,128]{3,2,1,0:T(2,128)(2,1)}, bf16[7,32,2,128]{3,2,1,0:T(2,128)(2,1)}, u32[]{:S(2)}, u32[]{:S(2)}) collective-permute-start(bf16[7,32,2,128]{3,2,1,0:T(2,128)(2,1)} %pad_maximum_fusion.6), channel_id=1, source_target_pairs={{1,0},{2,1},{3,2},{4,3},{5,4},{6,5},{7,6},{8,7},{9,8},{10,9},{11,1... | collective-permute-start | bytes 344072 | tf_op jit(solution)/shard_map/ppermute | solution.py:127
  19.9 11.1 %collective-permute-start.2 = (bf16[7,32,16,2]{1,2,3,0:T(8,128)(2,1)S(1)}, bf16[7,32,16,2]{1,2,3,0:T(8,128)(2,1)S(1)}, u32[]{:S(2)}, u32[]{:S(2)}) collective-permute-start(bf16[7,32,16,2]{1,2,3,0:T(8,128)(2,1)S(1)} %pad_maximum_fusion.7), channel_id=1, source_target_pairs={{16,0},{32,16},{48,32},{17,1},{33,17},{49,33},{18,2},{34,18},{50,3... | collective-permute-start | bytes 43016 | tf_op jit(solution)/shard_map/ppermute | solution.py:127
  21.3 5.6 %copy-start.9 = (s32[8,2]{0,1:T(2,128)S(1)}, s32[8,2]{0,1:T(2,128)}, u32[]{:S(2)}) copy-start(s32[8,2]{0,1:T(2,128)} %param.31) | copy-start | bytes 196
  21.3 7.6 %copy-start.5 = (f32[3,32]{1,0:T(4,128)S(1)}, f32[3,32]{1,0:T(4,128)}, u32[]{:S(2)}) copy-start(f32[3,32]{1,0:T(4,128)} %param.30) | copy-start | bytes 1156
  21.3 7.6 %copy-start.10 = (s32[8]{0:T(128)S(1)}, s32[8]{0:T(128)}, u32[]{:S(2)}) copy-start(s32[8]{0:T(128)} %param.32) | copy-start | bytes 100
  21.3 8.3 %copy-start.11 = (pred[34,4]{0,1:T(4,128)(4,1)S(1)}, pred[34,4]{0,1:T(4,128)(4,1)}, u32[]{:S(2)}) copy-start(pred[34,4]{0,1:T(4,128)(4,1)} %constant.194.clone) | copy-start | bytes 412
  21.4 8.3 %copy-start.12 = (pred[34,4]{0,1:T(4,128)(4,1)S(1)}, pred[34,4]{0,1:T(4,128)(4,1)}, u32[]{:S(2)}) copy-start(pred[34,4]{0,1:T(4,128)(4,1)} %constant.193.clone) | copy-start | bytes 412
  21.4 8.3 %copy-start.13 = (pred[34,4]{0,1:T(4,128)(4,1)S(1)}, pred[34,4]{0,1:T(4,128)(4,1)}, u32[]{:S(2)}) copy-start(pred[34,4]{0,1:T(4,128)(4,1)} %constant.192.clone) | copy-start | bytes 412
  22.2 8.9 %collective-permute-start.3 = (bf16[7,32,16,2]{1,2,3,0:T(8,128)(2,1)S(1)}, bf16[7,32,16,2]{1,2,3,0:T(8,128)(2,1)S(1)}, u32[]{:S(2)}, u32[]{:S(2)}) collective-permute-start(bf16[7,32,16,2]{1,2,3,0:T(8,128)(2,1)S(1)} %pad_maximum_fusion.8), channel_id=1, source_target_pairs={{0,16},{16,32},{32,48},{1,17},{17,33},{33,49},{2,18},{18,34},{34,5... | collective-permute-start | bytes 43016 | tf_op jit(solution)/shard_map/ppermute | solution.py:124
  31.2 4.2 %copy-start.1 = (f32[3,16]{1,0:T(4,128)S(1)}, f32[3,16]{1,0:T(4,128)}, u32[]{:S(2)}) copy-start(f32[3,16]{1,0:T(4,128)} %param.29) | copy-start | bytes 580
  43.5 1.7 %copy-start.6 = (pred[18,6]{0,1:T(8,128)(4,1)S(1)}, pred[18,6]{0,1:T(8,128)(4,1)}, u32[]{:S(2)}) copy-start(pred[18,6]{0,1:T(8,128)(4,1)} %constant.197.clone) | copy-start | bytes 328
  43.5 1.7 %copy-start.7 = (pred[18,6]{0,1:T(8,128)(4,1)S(1)}, pred[18,6]{0,1:T(8,128)(4,1)}, u32[]{:S(2)}) copy-start(pred[18,6]{0,1:T(8,128)(4,1)} %constant.196.clone) | copy-start | bytes 328
  43.5 1.7 %copy-start.8 = (pred[18,6]{0,1:T(8,128)(4,1)S(1)}, pred[18,6]{0,1:T(8,128)(4,1)}, u32[]{:S(2)}) copy-start(pred[18,6]{0,1:T(8,128)(4,1)} %constant.195.clone) | copy-start | bytes 328
  43.5 12.6 %copy-start.2 = (pred[130,20]{0,1:T(8,128)(4,1)S(1)}, pred[130,20]{0,1:T(8,128)(4,1)}, u32[]{:S(2)}) copy-start(pred[130,20]{0,1:T(8,128)(4,1)} %constant.200.clone) | copy-start | bytes 7804
  43.5 12.6 %copy-start.3 = (pred[130,20]{0,1:T(8,128)(4,1)S(1)}, pred[130,20]{0,1:T(8,128)(4,1)}, u32[]{:S(2)}) copy-start(pred[130,20]{0,1:T(8,128)(4,1)} %constant.199.clone) | copy-start | bytes 7804
  43.6 12.6 %copy-start.4 = (pred[130,20]{0,1:T(8,128)(4,1)S(1)}, pred[130,20]{0,1:T(8,128)(4,1)}, u32[]{:S(2)}) copy-start(pred[130,20]{0,1:T(8,128)(4,1)} %constant.198.clone) | copy-start | bytes 7804
  45.5 10.7 %collective-permute-start.4 = (f32[4,2,128]{2,1,0:T(2,128)S(1)}, f32[4,2,128]{2,1,0:T(2,128)S(1)}, u32[]{:S(2)}, u32[]{:S(2)}) collective-permute-start(f32[4,2,128]{2,1,0:T(2,128)S(1)} %get-tuple-element.86), channel_id=1, source_target_pairs={{0,1},{1,2},{2,3},{3,4},{4,5},{5,6},{6,7},{7,8},{8,9},{9,10},{10,1... | collective-permute-start | bytes 12296 | tf_op jit(solution)/shard_map/ppermute | solution.py:15
  50.7 9.4 %collective-permute-start.5 = (f32[4,2,128]{2,1,0:T(2,128)S(1)}, f32[4,2,128]{2,1,0:T(2,128)S(1)}, u32[]{:S(2)}, u32[]{:S(2)}) collective-permute-start(f32[4,2,128]{2,1,0:T(2,128)S(1)} %get-tuple-element.87), channel_id=1, source_target_pairs={{1,0},{2,1},{3,2},{4,3},{5,4},{6,5},{7,6},{8,7},{9,8},{10,9},{11,1... | collective-permute-start | bytes 12296 | tf_op jit(solution)/shard_map/ppermute | solution.py:18
  60.5 4.2 %collective-permute-start.6 = (f32[4,2,2]{2,0,1:T(4,128)S(1)}, f32[4,2,2]{2,0,1:T(4,128)S(1)}, u32[]{:S(2)}, u32[]{:S(2)}) collective-permute-start(f32[4,2,2]{2,0,1:T(4,128)S(1)} %get-tuple-element.92), channel_id=1, source_target_pairs={{0,16},{16,32},{32,48},{1,17},{17,33},{33,49},{2,18},{18,34},{34,5... | collective-permute-start | bytes 200 | tf_op jit(solution)/shard_map/ppermute | solution.py:15
  63.4 5.5 %collective-permute-start.7 = (f32[4,2,2]{2,0,1:T(4,128)S(1)}, f32[4,2,2]{2,0,1:T(4,128)S(1)}, u32[]{:S(2)}, u32[]{:S(2)}) collective-permute-start(f32[4,2,2]{2,0,1:T(4,128)S(1)} %get-tuple-element.91), channel_id=1, source_target_pairs={{16,0},{32,16},{48,32},{17,1},{33,17},{49,33},{18,2},{34,18},{50,3... | collective-permute-start | bytes 200 | tf_op jit(solution)/shard_map/ppermute | solution.py:18
  69.4 1.3 %collective-permute-start.9 = (f32[2,16]{1,0:T(2,128)S(1)}, f32[2,16]{1,0:T(2,128)S(1)}, u32[]{:S(2)}, u32[]{:S(2)}) collective-permute-start(f32[2,16]{1,0:T(2,128)S(1)} %broadcast_multiply_fusion), channel_id=1, source_target_pairs={{64,0},{128,64},{192,128},{256,192},{320,256},{384,320},{448,384},... | collective-permute-start | bytes 392 | tf_op jit(solution)/shard_map/ppermute | solution.py:26
  69.5 4.4 %collective-permute-start.8 = (f32[2,16]{1,0:T(2,128)S(1)}, f32[2,16]{1,0:T(2,128)S(1)}, u32[]{:S(2)}, u32[]{:S(2)}) collective-permute-start(f32[2,16]{1,0:T(2,128)S(1)} %broadcast_multiply_fusion.1), channel_id=1, source_target_pairs={{448,0},{0,64},{64,128},{128,192},{192,256},{256,320},{320,384},{3... | collective-permute-start | bytes 392 | tf_op jit(solution)/shard_map/ppermute | solution.py:26

commit v8 on v6

--- a/solution.py
+++ b/solution.py
@@ -195,15 +195,19 @@
     patch_index = lax.axis_index("patch")
     patches = lax.axis_size("patch")
     layers_d = reduced.shape[0]
-    out_index = jnp.where(orient[patch_index, 0] == 1, 0, layers_d - 1).astype(jnp.int32)
-    in_index = jnp.where(orient[patch_index, 1] == 1, layers_d - 1, 0).astype(jnp.int32)
-    layer_ids = jnp.arange(layers_d)
-    out_mask = (layer_ids == out_index).astype(jnp.float32)[:, None, None]
-    in_mask = (layer_ids == in_index).astype(jnp.float32)[:, None, None]
+    ids = jnp.arange(patches)[:, None]
+    here = (ids == patch_index).astype(jnp.float32)
+    before = (ids == (patch_index + patches - 1) % patches).astype(jnp.float32)
+    layer_ids = jnp.arange(layers_d)[None, :]
+    out_at = jnp.where(orient[:, 0:1] == 1, 0, layers_d - 1)
+    in_at = jnp.where(orient[:, 1:2] == 1, layers_d - 1, 0)
+    out_mask = jnp.sum(here * (layer_ids == out_at).astype(jnp.float32), axis=0)[:, None, None]
+    in_mask = jnp.sum(here * (layer_ids == in_at).astype(jnp.float32), axis=0)[:, None, None]
     out_face = jnp.sum(out_mask * reduced, axis=0)
     in_face = jnp.sum(in_mask * reduced, axis=0)
-    gate_here = link[patch_index].astype(jnp.float32)
-    gate_before = link[(patch_index + patches - 1) % patches].astype(jnp.float32)
+    links = jnp.broadcast_to(link.astype(jnp.float32)[:, None, None], (patches,) + out_face.shape)
+    gate_here = jnp.sum(here[:, :, None] * links, axis=0)
+    gate_before = jnp.sum(before[:, :, None] * links, axis=0)
     from_before = from_behind(out_face * gate_here, "patch", 1)
     from_after = from_behind(in_face * gate_before, "patch", -1)
     design = reduced + in_mask * from_before[None] + out_mask * from_after[None]

time: 75.2 us -> 76.1 us (1.012)
  waiting for transfers between devices: 11.8 us -> 14.6 us
  between operations: 3.1 us -> 0.54 us
  other arithmetic: 13.1 us -> 15.1 us
  local copies, waits for them, and re-layouts: 9.56 us -> 8.24 us
    ppermute x2, waiting for transfers between devices: 0.01 us -> 2.36 us  [neighbour_rows(): lax.ppermute(with_rider(lax.slice_in_dim(stacked, 0, width, axis=dim), co...]
    dynamic_slice x2 -> x0, local copies, waits for them, and re-layouts: 1.31 us -> none  [the longest x1 0.66 us: shards(): gate_here = link[patch_index].astype(jnp.float32)]
    reduce_sum x0 -> x2, other arithmetic: none -> 0.78 us  [the longest x1 0.64 us: shards(): gate_here = jnp.sum(here[:, :, None] * links, axis=0)]
  transfers between devices with their start and end apart: 10 -> 10, of which waited for: 4 -> 5; matrix products, arithmetic and copies ran while one was open for 11% -> 11% of each run, Pallas kernels for 0% -> 0%
where the time goes in v8:
time: 76.1 us; the launch traced here: 75.6 us
  starting transfers between devices  36.4 us (48%)
  other arithmetic  15.1 us (20%)
  waiting for transfers between devices  14.6 us (19%)
  local copies, waits for them, and re-layouts  8.24 us (11%)
    ppermute x2, starting transfers between devices, neighbour_rows(): lax.ppermute(with_rider(lax.slice_in_dim(stacked, length - width, None, a...  13.6 us
    ppermute x2, starting transfers between devices, with_halo(): lax.ppermute(lax.slice_in_dim(block, block.shape[dim] - width, None, axis...  8.85 us
    ppermute x2, waiting for transfers between devices, with_halo(): lax.ppermute(lax.slice_in_dim(block, 0, width, axis=dim), axis, backward)  8.33 us
    ppermute x2, starting transfers between devices, neighbour_rows(): lax.ppermute(with_rider(lax.slice_in_dim(stacked, 0, width, axis=dim), co...  7.1 us
    ppermute x2, starting transfers between devices, with_halo(): lax.ppermute(lax.slice_in_dim(block, 0, width, axis=dim), axis, backward)  6.31 us
    div x1, other arithmetic, slopes_along(): (8.0 * (shifted(1) - shifted(-1)) - (shifted(2) - shifted(-2))) / 12.0  6.02 us
    ppermute x2, waiting for transfers between devices, from_behind(): return lax.ppermute(block, axis, route)  3.87 us
    ppermute x2, waiting for transfers between devices, neighbour_rows(): lax.ppermute(with_rider(lax.slice_in_dim(stacked, 0, width, axis=dim), co...  2.36 us
  transfers between devices with their start and end apart: 10, of which 5 were waited for; matrix products, arithmetic and copies ran while one was open for 11% of the time, Pallas kernels for 0%

profile of v8, /device:TPU:6, one launch (start us, length us, event | category | flops | bytes accessed | tf_op | source)
XLA Modules:
  0.0 75.6 jit_solution(14633501907181132245)
XLA Ops:
  0.0 1.0 %slice_reduce_fusion.2 = (f32[3]{0:T(128)S(1)}, f32[3]{0:T(128)S(1)}) fusion(f32[3,16]{1,0:T(4,128)} %param.29), kind=kLoop, calls=%fused_computation.150 | loop fusion | bytes 48 | tf_op jit(solution)/shard_map/slice | solution.py:127
  1.0 1.3 %slice_bitcast_fusion = (bf16[3,32,16,128]{3,2,1,0:T(8,128)(2,1)S(1)}, bf16[3,32,16,128]{3,2,1,0:T(8,128)(2,1)S(1)}) fusion(bf16[1,8,32,16,128]{4,3,2,1,0:T(8,128)(2,1)} %param.27), kind=kLoop, calls=%fused_computation.48 | loop fusion | bytes 1572864 | tf_op jit(solution)/shard_map/slice | solution.py:164
  2.2 0.2 fusion.36
  2.5 0.2 pad_maximum_fusion.5
  2.7 9.1 %collective-permute-start = (bf16[7,32,2,128]{3,2,1,0:T(2,128)(2,1)S(1)}, bf16[7,32,2,128]{3,2,1,0:T(2,128)(2,1)}, u32[]{:S(2)}, u32[]{:S(2)}) collective-permute-start(bf16[7,32,2,128]{3,2,1,0:T(2,128)(2,1)S(1)} %pad_maximum_fusion.5), channel_id=1, source_target_pairs={{0,1},{1,2},{2,3},{3,4},{4,5},{5,6},{6,7},{7,8},{8,9},{9,10},{10,1... | collective-permute-start | bytes 344072 | tf_op jit(solution)/shard_map/ppermute | solution.py:124
  11.8 0.8 %pad_maximum_fusion.6 = bf16[7,32,2,128]{3,2,1,0:T(2,128)(2,1)} fusion(bf16[1,32,2,128]{3,2,1,0:T(2,128)(2,1)S(1)} %broadcast_in_dim.141, bf16[6,32,2,128]{3,2,1,0:T(2,128)(2,1)S(1)} %get-tuple-element.84), kind=kLoop, calls=%fused_computation.72 | loop fusion | flops 57344 | bytes 229376 | tf_op jit(solution)/shard_map/concatenate | solution.py:116
  12.6 5.8 %collective-permute-start.1 = (bf16[7,32,2,128]{3,2,1,0:T(2,128)(2,1)}, bf16[7,32,2,128]{3,2,1,0:T(2,128)(2,1)}, u32[]{:S(2)}, u32[]{:S(2)}) collective-permute-start(bf16[7,32,2,128]{3,2,1,0:T(2,128)(2,1)} %pad_maximum_fusion.6), channel_id=1, source_target_pairs={{1,0},{2,1},{3,2},{4,3},{5,4},{6,5},{7,6},{8,7},{9,8},{10,9},{11,1... | collective-permute-start | bytes 344072 | tf_op jit(solution)/shard_map/ppermute | solution.py:127
  18.4 0.3 fusion.20
  18.8 0.2 slice_reduce_fusion
  19.0 0.1 copy.114
  19.1 0.8 %copy.103 = bf16[6,32,16,2]{1,2,3,0:T(8,128)(2,1)S(1)} copy(bf16[6,32,16,2]{3,2,1,0:T(8,128)(2,1)S(1)} %get-tuple-element.87) | data formatting | bytes 24576 | tf_op jit(solution)/shard_map/slice | solution.py:127
  19.9 1.3 %collective-permute-start.2 = (bf16[7,32,16,2]{1,2,3,0:T(8,128)(2,1)S(1)}, bf16[7,32,16,2]{1,2,3,0:T(8,128)(2,1)S(1)}, u32[]{:S(2)}, u32[]{:S(2)}) collective-permute-start(bf16[7,32,16,2]{1,2,3,0:T(8,128)(2,1)S(1)} %pad_maximum_fusion.7), channel_id=1, source_target_pairs={{16,0},{32,16},{48,32},{17,1},{33,17},{49,33},{18,2},{34,18},{50,3... | collective-permute-start | bytes 43016 | tf_op jit(solution)/shard_map/ppermute | solution.py:127
  21.2 0.1 copy.115
  21.4 0.8 %copy.106 = bf16[6,32,16,2]{1,2,3,0:T(8,128)(2,1)S(1)} copy(bf16[6,32,16,2]{3,2,1,0:T(8,128)(2,1)S(1)} %get-tuple-element.86) | data formatting | bytes 24576 | tf_op jit(solution)/shard_map/slice | solution.py:125
  22.2 4.5 %collective-permute-start.3 = (bf16[7,32,16,2]{1,2,3,0:T(8,128)(2,1)S(1)}, bf16[7,32,16,2]{1,2,3,0:T(8,128)(2,1)S(1)}, u32[]{:S(2)}, u32[]{:S(2)}) collective-permute-start(bf16[7,32,16,2]{1,2,3,0:T(8,128)(2,1)S(1)} %pad_maximum_fusion.8), channel_id=1, source_target_pairs={{0,16},{16,32},{32,48},{1,17},{17,33},{33,49},{2,18},{18,34},{34,5... | collective-permute-start | bytes 43016 | tf_op jit(solution)/shard_map/ppermute | solution.py:124
  26.7 0.1 fusion.21
  27.0 0.1 select_reduce_fusion
  27.2 0.6 fusion.90
  27.8 2.4 %collective-permute-done.2 = bf16[7,32,16,2]{1,2,3,0:T(8,128)(2,1)S(1)} collective-permute-done((bf16[7,32,16,2]{1,2,3,0:T(8,128)(2,1)S(1)}, bf16[7,32,16,2]{1,2,3,0:T(8,128)(2,1)S(1)}, u32[]{:S(2)}, u32[]{:S(2)}) %collective-permute-start.2) | collective-permute-done | bytes 14368 | tf_op jit(solution)/shard_map/ppermute | solution.py:127
  30.4 0.8 copy.107
  31.1 1.8 %copy.104 = f32[6,32,16,2]{3,2,1,0:T(8,128)} copy(f32[6,32,16,2]{1,2,3,0:T(8,128)S(1)} %slice_convert_fusion.3) | data formatting | bytes 49152 | tf_op jit(solution)/shard_map/convert_element_type | solution.py:137
  32.9 0.1 pad_maximum_fusion.14
  33.0 0.7 slice_convert_fusion.5
  33.7 0.1 copy.100
  33.8 0.7 slice_convert_fusion.4
  34.5 0.1 copy.101
  34.7 1.0 %slice_convert_fusion = f32[6,32,2,128]{3,2,1,0:T(2,128)S(1)} fusion(bf16[7,32,2,128]{3,2,1,0:T(2,128)(2,1)} %collective-permute-done), kind=kLoop, calls=%fused_computation.75 | loop fusion | flops 49152 | bytes 294912 | tf_op jit(solution)/shard_map/convert_element_type | solution.py:137
  35.6 1.0 %slice_convert_fusion.1 = f32[6,32,2,128]{3,2,1,0:T(2,128)S(1)} fusion(bf16[7,32,2,128]{3,2,1,0:T(2,128)(2,1)} %collective-permute-done.1), kind=kLoop, calls=%fused_computation.76 | loop fusion | flops 49152 | bytes 294912 | tf_op jit(solution)/shard_map/convert_element_type | solution.py:137
  36.6 6.0 %fusion.3 = (f32[6,32,16,128]{3,2,1,0:T(8,128)S(1)}, f32[6,32,16,128]{3,2,1,0:T(8,128)S(1)}, f32[6,32,16,128]{3,2,1,0:T(8,128)S(1)}) fusion(f32[6,32,16,128]{3,2,1,0:T(8,128)S(1)} %fusion.21, f32[6,32,16,2]{3,2,1,0:T(8,128)S(1)} %copy.107, f32[6,32,16,2]{3,2,1,0:T(8,128)} %copy.104, f32[6,32,2,128]{3,2,1,0:T(2,128)S(1)} %slice_convert_fusion, ...), kind=kLoop, calls=%fused_computation.15 | loop fusion | flops 9043968 | bytes 6733824 | tf_op jit(solution)/shard_map/div | solution.py:143
  42.7 1.3 %fusion.25 = f32[32,16,128]{2,1,0:T(8,128)S(1)} fusion(f32[6,32,16,128]{3,2,1,0:T(8,128)S(1)} %get-tuple-element.80, f32[6,32,16,128]{3,2,1,0:T(8,128)S(1)} %get-tuple-element.81, f32[6,32,16,128]{3,2,1,0:T(8,128)S(1)} %get-tuple-element.79, bf16[1,8,32,16,128]{4,3,2,1,0:T(8,128)(2,1)} %param.27), kind=kLoop, calls=%fused_computation.54 | loop fusion | flops 1769472 | bytes 5242880 | tf_op jit(solution)/shard_map/sub | solution.py:184
  44.0 0.3 fusion.33
  44.4 0.2 convolution_bitcast_fusion
  44.6 5.6 %collective-permute-start.4 = (f32[4,2,128]{2,1,0:T(2,128)S(1)}, f32[4,2,128]{2,1,0:T(2,128)S(1)}, u32[]{:S(2)}, u32[]{:S(2)}) collective-permute-start(f32[4,2,128]{2,1,0:T(2,128)S(1)} %get-tuple-element.88), channel_id=1, source_target_pairs={{0,1},{1,2},{2,3},{3,4},{4,5},{5,6},{6,7},{7,8},{8,9},{9,10},{10,1... | collective-permute-start | bytes 12296 | tf_op jit(solution)/shard_map/ppermute | solution.py:15
  50.3 5.0 %collective-permute-start.5 = (f32[4,2,128]{2,1,0:T(2,128)S(1)}, f32[4,2,128]{2,1,0:T(2,128)S(1)}, u32[]{:S(2)}, u32[]{:S(2)}) collective-permute-start(f32[4,2,128]{2,1,0:T(2,128)S(1)} %get-tuple-element.89), channel_id=1, source_target_pairs={{1,0},{2,1},{3,2},{4,3},{5,4},{6,5},{7,6},{8,7},{9,8},{10,9},{11,1... | collective-permute-start | bytes 12296 | tf_op jit(solution)/shard_map/ppermute | solution.py:18
  55.3 4.3 %collective-permute-done.5 = f32[4,2,128]{2,1,0:T(2,128)S(1)} collective-permute-done((f32[4,2,128]{2,1,0:T(2,128)S(1)}, f32[4,2,128]{2,1,0:T(2,128)S(1)}, u32[]{:S(2)}, u32[]{:S(2)}) %collective-permute-start.5) | collective-permute-done | bytes 4128 | tf_op jit(solution)/shard_map/ppermute | solution.py:18
  59.7 0.2 fusion.47
  60.1 3.2 %collective-permute-start.6 = (f32[4,2,2]{2,0,1:T(4,128)S(1)}, f32[4,2,2]{2,0,1:T(4,128)S(1)}, u32[]{:S(2)}, u32[]{:S(2)}) collective-permute-start(f32[4,2,2]{2,0,1:T(4,128)S(1)} %get-tuple-element.94), channel_id=1, source_target_pairs={{0,16},{16,32},{32,48},{1,17},{17,33},{33,49},{2,18},{18,34},{34,5... | collective-permute-start | bytes 200 | tf_op jit(solution)/shard_map/ppermute | solution.py:15
  63.3 1.3 %collective-permute-start.7 = (f32[4,2,2]{2,0,1:T(4,128)S(1)}, f32[4,2,2]{2,0,1:T(4,128)S(1)}, u32[]{:S(2)}, u32[]{:S(2)}) collective-permute-start(f32[4,2,2]{2,0,1:T(4,128)S(1)} %get-tuple-element.93), channel_id=1, source_target_pairs={{16,0},{32,16},{48,32},{17,1},{33,17},{49,33},{18,2},{34,18},{50,3... | collective-permute-start | bytes 200 | tf_op jit(solution)/shard_map/ppermute | solution.py:18
  64.7 0.1 scatter-add.6
  64.8 4.0 %collective-permute-done.7 = f32[4,2,2]{2,0,1:T(4,128)S(1)} collective-permute-done((f32[4,2,2]{2,0,1:T(4,128)S(1)}, f32[4,2,2]{2,0,1:T(4,128)S(1)}, u32[]{:S(2)}, u32[]{:S(2)}) %collective-permute-start.7) | collective-permute-done | bytes 96 | tf_op jit(solution)/shard_map/ppermute | solution.py:18
  68.9 0.3 scatter-add.9
  69.2 0.1 multiply_reduce_fusion.1
  69.3 0.6 broadcast_multiply_fusion
  69.9 0.7 broadcast_multiply_fusion.1
  70.6 0.5 collective-permute-start.8
  71.1 0.1 collective-permute-done.9
  71.2 3.7 %collective-permute-done.8 = f32[2,16]{1,0:T(2,128)S(1)} collective-permute-done((f32[2,16]{1,0:T(2,128)S(1)}, f32[2,16]{1,0:T(2,128)S(1)}, u32[]{:S(2)}, u32[]{:S(2)}) %collective-permute-start.8) | collective-permute-done | bytes 160 | tf_op jit(solution)/shard_map/ppermute | solution.py:26
  75.0 0.6 copy.123
  (73 shorter events, 1.1 us)
Async XLA Ops:
  2.5 16.3 %copy-start = (f32[3,128]{1,0:T(4,128)S(1)}, f32[3,128]{1,0:T(4,128)}, u32[]{:S(2)}) copy-start(f32[3,128]{1,0:T(4,128)} %param.28) | copy-start | bytes 4612
  2.7 30.3 %collective-permute-start = (bf16[7,32,2,128]{3,2,1,0:T(2,128)(2,1)S(1)}, bf16[7,32,2,128]{3,2,1,0:T(2,128)(2,1)}, u32[]{:S(2)}, u32[]{:S(2)}) collective-permute-start(bf16[7,32,2,128]{3,2,1,0:T(2,128)(2,1)S(1)} %pad_maximum_fusion.5), channel_id=1, source_target_pairs={{0,1},{1,2},{2,3},{3,4},{4,5},{5,6},{6,7},{7,8},{8,9},{9,10},{10,1... | collective-permute-start | bytes 344072 | tf_op jit(solution)/shard_map/ppermute | solution.py:124
  12.6 21.2 %collective-permute-start.1 = (bf16[7,32,2,128]{3,2,1,0:T(2,128)(2,1)}, bf16[7,32,2,128]{3,2,1,0:T(2,128)(2,1)}, u32[]{:S(2)}, u32[]{:S(2)}) collective-permute-start(bf16[7,32,2,128]{3,2,1,0:T(2,128)(2,1)} %pad_maximum_fusion.6), channel_id=1, source_target_pairs={{1,0},{2,1},{3,2},{4,3},{5,4},{6,5},{7,6},{8,7},{9,8},{10,9},{11,1... | collective-permute-start | bytes 344072 | tf_op jit(solution)/shard_map/ppermute | solution.py:127
  19.9 10.3 %collective-permute-start.2 = (bf16[7,32,16,2]{1,2,3,0:T(8,128)(2,1)S(1)}, bf16[7,32,16,2]{1,2,3,0:T(8,128)(2,1)S(1)}, u32[]{:S(2)}, u32[]{:S(2)}) collective-permute-start(bf16[7,32,16,2]{1,2,3,0:T(8,128)(2,1)S(1)} %pad_maximum_fusion.7), channel_id=1, source_target_pairs={{16,0},{32,16},{48,32},{17,1},{33,17},{49,33},{18,2},{34,18},{50,3... | collective-permute-start | bytes 43016 | tf_op jit(solution)/shard_map/ppermute | solution.py:127
  21.3 5.6 %copy-start.9 = (s32[8,2]{0,1:T(2,128)S(1)}, s32[8,2]{0,1:T(2,128)}, u32[]{:S(2)}) copy-start(s32[8,2]{0,1:T(2,128)} %param.31) | copy-start | bytes 196
  21.3 5.6 %copy-start.5 = (f32[3,32]{1,0:T(4,128)S(1)}, f32[3,32]{1,0:T(4,128)}, u32[]{:S(2)}) copy-start(f32[3,32]{1,0:T(4,128)} %param.30) | copy-start | bytes 1156
  21.3 5.8 %copy-start.11 = (pred[34,4]{0,1:T(4,128)(4,1)S(1)}, pred[34,4]{0,1:T(4,128)(4,1)}, u32[]{:S(2)}) copy-start(pred[34,4]{0,1:T(4,128)(4,1)} %constant.195.clone) | copy-start | bytes 412
  21.3 5.8 %copy-start.12 = (pred[34,4]{0,1:T(4,128)(4,1)S(1)}, pred[34,4]{0,1:T(4,128)(4,1)}, u32[]{:S(2)}) copy-start(pred[34,4]{0,1:T(4,128)(4,1)} %constant.194.clone) | copy-start | bytes 412
  21.3 5.8 %copy-start.13 = (pred[34,4]{0,1:T(4,128)(4,1)S(1)}, pred[34,4]{0,1:T(4,128)(4,1)}, u32[]{:S(2)}) copy-start(pred[34,4]{0,1:T(4,128)(4,1)} %constant.193.clone) | copy-start | bytes 412
  21.4 5.8 %copy-start.10 = (s32[8]{0:T(128)S(1)}, s32[8]{0:T(128)}, u32[]{:S(2)}) copy-start(s32[8]{0:T(128)} %param.32) | copy-start | bytes 100
  22.2 8.1 %collective-permute-start.3 = (bf16[7,32,16,2]{1,2,3,0:T(8,128)(2,1)S(1)}, bf16[7,32,16,2]{1,2,3,0:T(8,128)(2,1)S(1)}, u32[]{:S(2)}, u32[]{:S(2)}) collective-permute-start(bf16[7,32,16,2]{1,2,3,0:T(8,128)(2,1)S(1)} %pad_maximum_fusion.8), channel_id=1, source_target_pairs={{0,16},{16,32},{32,48},{1,17},{17,33},{33,49},{2,18},{18,34},{34,5... | collective-permute-start | bytes 43016 | tf_op jit(solution)/shard_map/ppermute | solution.py:124
  30.4 4.2 %copy-start.1 = (f32[3,16]{1,0:T(4,128)S(1)}, f32[3,16]{1,0:T(4,128)}, u32[]{:S(2)}) copy-start(f32[3,16]{1,0:T(4,128)} %param.29) | copy-start | bytes 580
  42.6 1.7 %copy-start.6 = (pred[18,6]{0,1:T(8,128)(4,1)S(1)}, pred[18,6]{0,1:T(8,128)(4,1)}, u32[]{:S(2)}) copy-start(pred[18,6]{0,1:T(8,128)(4,1)} %constant.198.clone) | copy-start | bytes 328
  42.6 1.7 %copy-start.7 = (pred[18,6]{0,1:T(8,128)(4,1)S(1)}, pred[18,6]{0,1:T(8,128)(4,1)}, u32[]{:S(2)}) copy-start(pred[18,6]{0,1:T(8,128)(4,1)} %constant.197.clone) | copy-start | bytes 328
  42.7 1.7 %copy-start.8 = (pred[18,6]{0,1:T(8,128)(4,1)S(1)}, pred[18,6]{0,1:T(8,128)(4,1)}, u32[]{:S(2)}) copy-start(pred[18,6]{0,1:T(8,128)(4,1)} %constant.196.clone) | copy-start | bytes 328
  42.7 12.6 %copy-start.2 = (pred[130,20]{0,1:T(8,128)(4,1)S(1)}, pred[130,20]{0,1:T(8,128)(4,1)}, u32[]{:S(2)}) copy-start(pred[130,20]{0,1:T(8,128)(4,1)} %constant.201.clone) | copy-start | bytes 7804
  42.7 12.6 %copy-start.3 = (pred[130,20]{0,1:T(8,128)(4,1)S(1)}, pred[130,20]{0,1:T(8,128)(4,1)}, u32[]{:S(2)}) copy-start(pred[130,20]{0,1:T(8,128)(4,1)} %constant.200.clone) | copy-start | bytes 7804
  42.7 12.6 %copy-start.4 = (pred[130,20]{0,1:T(8,128)(4,1)S(1)}, pred[130,20]{0,1:T(8,128)(4,1)}, u32[]{:S(2)}) copy-start(pred[130,20]{0,1:T(8,128)(4,1)} %constant.199.clone) | copy-start | bytes 7804
  44.6 10.7 %collective-permute-start.4 = (f32[4,2,128]{2,1,0:T(2,128)S(1)}, f32[4,2,128]{2,1,0:T(2,128)S(1)}, u32[]{:S(2)}, u32[]{:S(2)}) collective-permute-start(f32[4,2,128]{2,1,0:T(2,128)S(1)} %get-tuple-element.88), channel_id=1, source_target_pairs={{0,1},{1,2},{2,3},{3,4},{4,5},{5,6},{6,7},{7,8},{8,9},{9,10},{10,1... | collective-permute-start | bytes 12296 | tf_op jit(solution)/shard_map/ppermute | solution.py:15
  50.3 9.4 %collective-permute-start.5 = (f32[4,2,128]{2,1,0:T(2,128)S(1)}, f32[4,2,128]{2,1,0:T(2,128)S(1)}, u32[]{:S(2)}, u32[]{:S(2)}) collective-permute-start(f32[4,2,128]{2,1,0:T(2,128)S(1)} %get-tuple-element.89), channel_id=1, source_target_pairs={{1,0},{2,1},{3,2},{4,3},{5,4},{6,5},{7,6},{8,7},{9,8},{10,9},{11,1... | collective-permute-start | bytes 12296 | tf_op jit(solution)/shard_map/ppermute | solution.py:18
  60.1 4.5 %collective-permute-start.6 = (f32[4,2,2]{2,0,1:T(4,128)S(1)}, f32[4,2,2]{2,0,1:T(4,128)S(1)}, u32[]{:S(2)}, u32[]{:S(2)}) collective-permute-start(f32[4,2,2]{2,0,1:T(4,128)S(1)} %get-tuple-element.94), channel_id=1, source_target_pairs={{0,16},{16,32},{32,48},{1,17},{17,33},{33,49},{2,18},{18,34},{34,5... | collective-permute-start | bytes 200 | tf_op jit(solution)/shard_map/ppermute | solution.py:15
  63.3 5.5 %collective-permute-start.7 = (f32[4,2,2]{2,0,1:T(4,128)S(1)}, f32[4,2,2]{2,0,1:T(4,128)S(1)}, u32[]{:S(2)}, u32[]{:S(2)}) collective-permute-start(f32[4,2,2]{2,0,1:T(4,128)S(1)} %get-tuple-element.93), channel_id=1, source_target_pairs={{16,0},{32,16},{48,32},{17,1},{33,17},{49,33},{18,2},{34,18},{50,3... | collective-permute-start | bytes 200 | tf_op jit(solution)/shard_map/ppermute | solution.py:18
  69.9 1.3 %collective-permute-start.9 = (f32[2,16]{1,0:T(2,128)S(1)}, f32[2,16]{1,0:T(2,128)S(1)}, u32[]{:S(2)}, u32[]{:S(2)}) collective-permute-start(f32[2,16]{1,0:T(2,128)S(1)} %broadcast_multiply_fusion), channel_id=1, source_target_pairs={{64,0},{128,64},{192,128},{256,192},{320,256},{384,320},{448,384},... | collective-permute-start | bytes 392 | tf_op jit(solution)/shard_map/ppermute | solution.py:26
  70.6 4.4 %collective-permute-start.8 = (f32[2,16]{1,0:T(2,128)S(1)}, f32[2,16]{1,0:T(2,128)S(1)}, u32[]{:S(2)}, u32[]{:S(2)}) collective-permute-start(f32[2,16]{1,0:T(2,128)S(1)} %broadcast_multiply_fusion.1), channel_id=1, source_target_pairs={{448,0},{0,64},{64,128},{128,192},{192,256},{256,320},{320,384},{3... | collective-permute-start | bytes 392 | tf_op jit(solution)/shard_map/ppermute | solution.py:26

commit v9 on v6

--- a/solution.py
+++ b/solution.py
@@ -72,18 +72,25 @@
     return result
 
 
+def fold_along(partial_value, axis, dim):
+    widened = with_halo(partial_value, ((axis, dim),), 2)
+    length = widened.shape[dim]
+    interior = lax.slice_in_dim(widened, 4, length - 4, axis=dim)
+    inner = interior.shape[dim]
+    widths = [(0, 0)] * widened.ndim
+    widths[dim] = (0, inner - 2)
+    from_low = jnp.pad(lax.slice_in_dim(widened, 0, 2, axis=dim), widths)
+    widths[dim] = (inner - 2, 0)
+    from_high = jnp.pad(lax.slice_in_dim(widened, length - 2, length, axis=dim), widths)
+    return interior + from_low + from_high
+
+
 def fold_vert(partial_value):
-    widened = with_halo(partial_value, (("vert", 1),), 2)
-    interior = widened[:, 4:-4]
-    interior = interior.at[:, :2].add(widened[:, :2])
-    return interior.at[:, -2:].add(widened[:, -2:])
+    return fold_along(partial_value, "vert", 1)
 
 
 def fold_first(partial_value):
-    widened = with_halo(partial_value, (("au", 2),), 2)
-    interior = widened[:, :, 4:-4]
-    interior = interior.at[:, :, :2].add(widened[:, :, :2])
-    return interior.at[:, :, -2:].add(widened[:, :, -2:])
+    return fold_along(partial_value, "au", 2)
 
 
 def split_exact(vector):

time: 75.2 us -> 74.6 us (level)
  no operation moved by 1% of the time
where the time goes in v9:
time: 74.6 us; the launch traced here: 73.9 us
  starting transfers between devices  36.2 us (49%)
  other arithmetic  12.9 us (17%)
  waiting for transfers between devices  12 us (16%)
  local copies, waits for them, and re-layouts  8.99 us (12%)
  between operations  3.11 us (4%)
    ppermute x2, starting transfers between devices, neighbour_rows(): lax.ppermute(with_rider(lax.slice_in_dim(stacked, length - width, None, a...  13.6 us
    ppermute x2, starting transfers between devices, with_halo(): lax.ppermute(lax.slice_in_dim(block, block.shape[dim] - width, None, axis...  8.15 us
    ppermute x2, waiting for transfers between devices, with_halo(): lax.ppermute(lax.slice_in_dim(block, 0, width, axis=dim), axis, backward)  8.07 us
    ppermute x2, starting transfers between devices, neighbour_rows(): lax.ppermute(with_rider(lax.slice_in_dim(stacked, 0, width, axis=dim), co...  7.1 us
    ppermute x2, starting transfers between devices, with_halo(): lax.ppermute(lax.slice_in_dim(block, 0, width, axis=dim), axis, backward)  6.75 us
    div x1, other arithmetic, slopes_along(): (8.0 * (shifted(1) - shifted(-1)) - (shifted(2) - shifted(-2))) / 12.0  6.02 us
    ppermute x2, waiting for transfers between devices, from_behind(): return lax.ppermute(block, axis, route)  3.87 us
    convert_element_type x1, local copies, waits for them, and re-layouts, slopes_along(): high.astype(jnp.float32)  1.82 us
  transfers between devices with their start and end apart: 10, of which 4 were waited for; matrix products, arithmetic and copies ran while one was open for 11% of the time, Pallas kernels for 0%

profile of v9, /device:TPU:6, one launch (start us, length us, event | category | flops | bytes accessed | tf_op | source)
XLA Modules:
  0.0 73.9 jit_solution(9517887832888942603)
XLA Ops:
  0.0 1.0 %slice_reduce_fusion.2 = (f32[3]{0:T(128)S(1)}, f32[3]{0:T(128)S(1)}) fusion(f32[3,16]{1,0:T(4,128)} %param.17), kind=kLoop, calls=%fused_computation.146 | loop fusion | bytes 48 | tf_op jit(solution)/shard_map/slice | solution.py:134
  1.0 1.3 %slice_bitcast_fusion = (bf16[3,32,16,128]{3,2,1,0:T(8,128)(2,1)S(1)}, bf16[3,32,16,128]{3,2,1,0:T(8,128)(2,1)S(1)}) fusion(bf16[1,8,32,16,128]{4,3,2,1,0:T(8,128)(2,1)} %param.15), kind=kLoop, calls=%fused_computation.48 | loop fusion | bytes 1572864 | tf_op jit(solution)/shard_map/slice | solution.py:171
  2.2 0.2 fusion.36
  2.5 0.2 pad_maximum_fusion.5
  2.7 9.1 %collective-permute-start = (bf16[7,32,2,128]{3,2,1,0:T(2,128)(2,1)S(1)}, bf16[7,32,2,128]{3,2,1,0:T(2,128)(2,1)}, u32[]{:S(2)}, u32[]{:S(2)}) collective-permute-start(bf16[7,32,2,128]{3,2,1,0:T(2,128)(2,1)S(1)} %pad_maximum_fusion.5), channel_id=1, source_target_pairs={{0,1},{1,2},{2,3},{3,4},{4,5},{5,6},{6,7},{7,8},{8,9},{9,10},{10,1... | collective-permute-start | bytes 344072 | tf_op jit(solution)/shard_map/ppermute | solution.py:131
  11.8 0.8 %pad_maximum_fusion.6 = bf16[7,32,2,128]{3,2,1,0:T(2,128)(2,1)} fusion(bf16[1,32,2,128]{3,2,1,0:T(2,128)(2,1)S(1)} %broadcast_in_dim.123, bf16[6,32,2,128]{3,2,1,0:T(2,128)(2,1)S(1)} %get-tuple-element.17), kind=kLoop, calls=%fused_computation.72 | loop fusion | flops 57344 | bytes 229376 | tf_op jit(solution)/shard_map/concatenate | solution.py:123
  12.6 5.8 %collective-permute-start.1 = (bf16[7,32,2,128]{3,2,1,0:T(2,128)(2,1)}, bf16[7,32,2,128]{3,2,1,0:T(2,128)(2,1)}, u32[]{:S(2)}, u32[]{:S(2)}) collective-permute-start(bf16[7,32,2,128]{3,2,1,0:T(2,128)(2,1)} %pad_maximum_fusion.6), channel_id=1, source_target_pairs={{1,0},{2,1},{3,2},{4,3},{5,4},{6,5},{7,6},{8,7},{9,8},{10,9},{11,1... | collective-permute-start | bytes 344072 | tf_op jit(solution)/shard_map/ppermute | solution.py:134
  18.4 0.3 fusion.20
  18.8 0.2 slice_reduce_fusion
  19.0 0.1 copy.114
  19.1 0.8 %copy.103 = bf16[6,32,16,2]{1,2,3,0:T(8,128)(2,1)S(1)} copy(bf16[6,32,16,2]{3,2,1,0:T(8,128)(2,1)S(1)} %get-tuple-element.20) | data formatting | bytes 24576 | tf_op jit(solution)/shard_map/slice | solution.py:134
  19.9 1.3 %collective-permute-start.2 = (bf16[7,32,16,2]{1,2,3,0:T(8,128)(2,1)S(1)}, bf16[7,32,16,2]{1,2,3,0:T(8,128)(2,1)S(1)}, u32[]{:S(2)}, u32[]{:S(2)}) collective-permute-start(bf16[7,32,16,2]{1,2,3,0:T(8,128)(2,1)S(1)} %pad_maximum_fusion.7), channel_id=1, source_target_pairs={{16,0},{32,16},{48,32},{17,1},{33,17},{49,33},{18,2},{34,18},{50,3... | collective-permute-start | bytes 43016 | tf_op jit(solution)/shard_map/ppermute | solution.py:134
  21.2 0.1 copy.115
  21.4 0.8 %copy.106 = bf16[6,32,16,2]{1,2,3,0:T(8,128)(2,1)S(1)} copy(bf16[6,32,16,2]{3,2,1,0:T(8,128)(2,1)S(1)} %get-tuple-element.19) | data formatting | bytes 24576 | tf_op jit(solution)/shard_map/slice | solution.py:132
  22.2 4.5 %collective-permute-start.3 = (bf16[7,32,16,2]{1,2,3,0:T(8,128)(2,1)S(1)}, bf16[7,32,16,2]{1,2,3,0:T(8,128)(2,1)S(1)}, u32[]{:S(2)}, u32[]{:S(2)}) collective-permute-start(bf16[7,32,16,2]{1,2,3,0:T(8,128)(2,1)S(1)} %pad_maximum_fusion.8), channel_id=1, source_target_pairs={{0,16},{16,32},{32,48},{1,17},{17,33},{33,49},{2,18},{18,34},{34,5... | collective-permute-start | bytes 43016 | tf_op jit(solution)/shard_map/ppermute | solution.py:131
  26.7 0.1 fusion.21
  26.8 0.6 constant_dynamic-slice_fusion
  28.8 0.1 pad_maximum_fusion.10
  29.0 0.6 fusion.104
  30.9 0.1 add_bitcast_fusion
  31.1 0.8 %copy.107 = f32[6,32,16,2]{3,2,1,0:T(8,128)S(1)} copy(f32[6,32,16,2]{1,2,3,0:T(8,128)S(1)} %slice_convert_fusion.2) | data formatting | bytes 49152 | tf_op jit(solution)/shard_map/convert_element_type | solution.py:144
  31.8 1.8 %copy.104 = f32[6,32,16,2]{3,2,1,0:T(8,128)} copy(f32[6,32,16,2]{1,2,3,0:T(8,128)S(1)} %slice_convert_fusion.3) | data formatting | bytes 49152 | tf_op jit(solution)/shard_map/convert_element_type | solution.py:144
  33.6 0.1 pad_maximum_fusion.14
  33.7 0.7 slice_convert_fusion.5
  34.4 0.1 copy.100
  34.5 0.7 slice_convert_fusion.4
  35.2 0.1 copy.101
  35.3 0.1 pad_maximum_fusion.9
  35.4 1.0 %slice_convert_fusion = f32[6,32,2,128]{3,2,1,0:T(2,128)S(1)} fusion(bf16[7,32,2,128]{3,2,1,0:T(2,128)(2,1)} %collective-permute-done), kind=kLoop, calls=%fused_computation.75 | loop fusion | flops 49152 | bytes 294912 | tf_op jit(solution)/shard_map/convert_element_type | solution.py:144
  36.3 1.0 %slice_convert_fusion.1 = f32[6,32,2,128]{3,2,1,0:T(2,128)S(1)} fusion(bf16[7,32,2,128]{3,2,1,0:T(2,128)(2,1)} %collective-permute-done.1), kind=kLoop, calls=%fused_computation.76 | loop fusion | flops 49152 | bytes 294912 | tf_op jit(solution)/shard_map/convert_element_type | solution.py:144
  37.3 6.0 %fusion.3 = (f32[6,32,16,128]{3,2,1,0:T(8,128)S(1)}, f32[6,32,16,128]{3,2,1,0:T(8,128)S(1)}, f32[6,32,16,128]{3,2,1,0:T(8,128)S(1)}) fusion(f32[6,32,16,128]{3,2,1,0:T(8,128)S(1)} %fusion.21, f32[6,32,16,2]{3,2,1,0:T(8,128)S(1)} %copy.107, f32[6,32,16,2]{3,2,1,0:T(8,128)} %copy.104, f32[6,32,2,128]{3,2,1,0:T(2,128)S(1)} %slice_convert_fusion, ...), kind=kLoop, calls=%fused_computation.15 | loop fusion | flops 9043968 | bytes 6733824 | tf_op jit(solution)/shard_map/div | solution.py:150
  43.4 1.3 %fusion.25 = f32[32,16,128]{2,1,0:T(8,128)S(1)} fusion(f32[6,32,16,128]{3,2,1,0:T(8,128)S(1)} %get-tuple-element.13, f32[6,32,16,128]{3,2,1,0:T(8,128)S(1)} %get-tuple-element.14, f32[6,32,16,128]{3,2,1,0:T(8,128)S(1)} %get-tuple-element.12, bf16[1,8,32,16,128]{4,3,2,1,0:T(8,128)(2,1)} %param.15), kind=kLoop, calls=%fused_computation.54 | loop fusion | flops 1769472 | bytes 5242880 | tf_op jit(solution)/shard_map/sub | solution.py:191
  44.7 0.3 fusion.33
  45.1 0.2 convolution_bitcast_fusion
  45.3 5.2 %collective-permute-start.4 = (f32[4,2,128]{2,1,0:T(2,128)S(1)}, f32[4,2,128]{2,1,0:T(2,128)S(1)}, u32[]{:S(2)}, u32[]{:S(2)}) collective-permute-start(f32[4,2,128]{2,1,0:T(2,128)S(1)} %get-tuple-element.21), channel_id=1, source_target_pairs={{0,1},{1,2},{2,3},{3,4},{4,5},{5,6},{6,7},{7,8},{8,9},{9,10},{10,1... | collective-permute-start | bytes 12296 | tf_op jit(solution)/shard_map/ppermute | solution.py:15
  50.5 5.5 %collective-permute-start.5 = (f32[4,2,128]{2,1,0:T(2,128)S(1)}, f32[4,2,128]{2,1,0:T(2,128)S(1)}, u32[]{:S(2)}, u32[]{:S(2)}) collective-permute-start(f32[4,2,128]{2,1,0:T(2,128)S(1)} %get-tuple-element.22), channel_id=1, source_target_pairs={{1,0},{2,1},{3,2},{4,3},{5,4},{6,5},{7,6},{8,7},{9,8},{10,9},{11,1... | collective-permute-start | bytes 12296 | tf_op jit(solution)/shard_map/ppermute | solution.py:18
  56.0 3.9 %collective-permute-done.5 = f32[4,2,128]{2,1,0:T(2,128)S(1)} collective-permute-done((f32[4,2,128]{2,1,0:T(2,128)S(1)}, f32[4,2,128]{2,1,0:T(2,128)S(1)}, u32[]{:S(2)}, u32[]{:S(2)}) %collective-permute-start.5) | collective-permute-done | bytes 4128 | tf_op jit(solution)/shard_map/ppermute | solution.py:18
  59.9 0.2 fusion.47
  60.2 0.1 fusion.103
  60.2 3.0 %collective-permute-start.6 = (f32[4,2,2]{2,0,1:T(4,128)S(1)}, f32[4,2,2]{2,0,1:T(4,128)S(1)}, u32[]{:S(2)}, u32[]{:S(2)}) collective-permute-start(f32[4,2,2]{2,0,1:T(4,128)S(1)} %get-tuple-element.26), channel_id=1, source_target_pairs={{0,16},{16,32},{32,48},{1,17},{17,33},{33,49},{2,18},{18,34},{34,5... | collective-permute-start | bytes 200 | tf_op jit(solution)/shard_map/ppermute | solution.py:15
  63.2 1.3 %collective-permute-start.7 = (f32[4,2,2]{2,0,1:T(4,128)S(1)}, f32[4,2,2]{2,0,1:T(4,128)S(1)}, u32[]{:S(2)}, u32[]{:S(2)}) collective-permute-start(f32[4,2,2]{2,0,1:T(4,128)S(1)} %get-tuple-element.27), channel_id=1, source_target_pairs={{16,0},{32,16},{48,32},{17,1},{33,17},{49,33},{18,2},{34,18},{50,3... | collective-permute-start | bytes 200 | tf_op jit(solution)/shard_map/ppermute | solution.py:18
  64.5 4.2 %collective-permute-done.7 = f32[4,2,2]{2,0,1:T(4,128)S(1)} collective-permute-done((f32[4,2,2]{2,0,1:T(4,128)S(1)}, f32[4,2,2]{2,0,1:T(4,128)S(1)}, u32[]{:S(2)}, u32[]{:S(2)}) %collective-permute-start.7) | collective-permute-done | bytes 96 | tf_op jit(solution)/shard_map/ppermute | solution.py:18
  68.7 0.1 multiply_reduce_fusion.1
  68.9 0.5 collective-permute-start.8
  69.3 0.8 %collective-permute-done.9 = f32[2,16]{1,0:T(2,128)S(1)} collective-permute-done((f32[2,16]{1,0:T(2,128)S(1)}, f32[2,16]{1,0:T(2,128)S(1)}, u32[]{:S(2)}, u32[]{:S(2)}) %collective-permute-start.9) | collective-permute-done | bytes 160 | tf_op jit(solution)/shard_map/ppermute | solution.py:26
  70.1 3.1 %collective-permute-done.8 = f32[2,16]{1,0:T(2,128)S(1)} collective-permute-done((f32[2,16]{1,0:T(2,128)S(1)}, f32[2,16]{1,0:T(2,128)S(1)}, u32[]{:S(2)}, u32[]{:S(2)}) %collective-permute-start.8) | collective-permute-done | bytes 160 | tf_op jit(solution)/shard_map/ppermute | solution.py:26
  73.2 0.1 multiply_add_fusion
  73.3 0.6 copy.123
  (68 shorter events, 0.5 us)
Async XLA Ops:
  2.5 16.3 %copy-start = (f32[3,128]{1,0:T(4,128)S(1)}, f32[3,128]{1,0:T(4,128)}, u32[]{:S(2)}) copy-start(f32[3,128]{1,0:T(4,128)} %param.16) | copy-start | bytes 4612
  2.7 31.0 %collective-permute-start = (bf16[7,32,2,128]{3,2,1,0:T(2,128)(2,1)S(1)}, bf16[7,32,2,128]{3,2,1,0:T(2,128)(2,1)}, u32[]{:S(2)}, u32[]{:S(2)}) collective-permute-start(bf16[7,32,2,128]{3,2,1,0:T(2,128)(2,1)S(1)} %pad_maximum_fusion.5), channel_id=1, source_target_pairs={{0,1},{1,2},{2,3},{3,4},{4,5},{5,6},{6,7},{7,8},{8,9},{9,10},{10,1... | collective-permute-start | bytes 344072 | tf_op jit(solution)/shard_map/ppermute | solution.py:131
  12.6 21.9 %collective-permute-start.1 = (bf16[7,32,2,128]{3,2,1,0:T(2,128)(2,1)}, bf16[7,32,2,128]{3,2,1,0:T(2,128)(2,1)}, u32[]{:S(2)}, u32[]{:S(2)}) collective-permute-start(bf16[7,32,2,128]{3,2,1,0:T(2,128)(2,1)} %pad_maximum_fusion.6), channel_id=1, source_target_pairs={{1,0},{2,1},{3,2},{4,3},{5,4},{6,5},{7,6},{8,7},{9,8},{10,9},{11,1... | collective-permute-start | bytes 344072 | tf_op jit(solution)/shard_map/ppermute | solution.py:134
  19.9 11.0 %collective-permute-start.2 = (bf16[7,32,16,2]{1,2,3,0:T(8,128)(2,1)S(1)}, bf16[7,32,16,2]{1,2,3,0:T(8,128)(2,1)S(1)}, u32[]{:S(2)}, u32[]{:S(2)}) collective-permute-start(bf16[7,32,16,2]{1,2,3,0:T(8,128)(2,1)S(1)} %pad_maximum_fusion.7), channel_id=1, source_target_pairs={{16,0},{32,16},{48,32},{17,1},{33,17},{49,33},{18,2},{34,18},{50,3... | collective-permute-start | bytes 43016 | tf_op jit(solution)/shard_map/ppermute | solution.py:134
  21.3 5.5 %copy-start.10 = (s32[8,2]{0,1:T(2,128)S(1)}, s32[8,2]{0,1:T(2,128)}, u32[]{:S(2)}) copy-start(s32[8,2]{0,1:T(2,128)} %param.19) | copy-start | bytes 196
  21.3 7.5 %copy-start.5 = (f32[3,32]{1,0:T(4,128)S(1)}, f32[3,32]{1,0:T(4,128)}, u32[]{:S(2)}) copy-start(f32[3,32]{1,0:T(4,128)} %param.18) | copy-start | bytes 1156
  21.3 7.6 %copy-start.11 = (pred[34,4]{0,1:T(4,128)(4,1)S(1)}, pred[34,4]{0,1:T(4,128)(4,1)}, u32[]{:S(2)}) copy-start(pred[34,4]{0,1:T(4,128)(4,1)} %constant.79.clone) | copy-start | bytes 412
  21.3 7.6 %copy-start.12 = (pred[34,4]{0,1:T(4,128)(4,1)S(1)}, pred[34,4]{0,1:T(4,128)(4,1)}, u32[]{:S(2)}) copy-start(pred[34,4]{0,1:T(4,128)(4,1)} %constant.78.clone) | copy-start | bytes 412
  21.3 7.5 %copy-start.13 = (pred[34,4]{0,1:T(4,128)(4,1)S(1)}, pred[34,4]{0,1:T(4,128)(4,1)}, u32[]{:S(2)}) copy-start(pred[34,4]{0,1:T(4,128)(4,1)} %constant.77.clone) | copy-start | bytes 412
  21.4 7.6 %copy-start.6 = (s32[8]{0:T(128)S(1)}, s32[8]{0:T(128)}, u32[]{:S(2)}) copy-start(s32[8]{0:T(128)} %param.20) | copy-start | bytes 100
  22.2 8.8 %collective-permute-start.3 = (bf16[7,32,16,2]{1,2,3,0:T(8,128)(2,1)S(1)}, bf16[7,32,16,2]{1,2,3,0:T(8,128)(2,1)S(1)}, u32[]{:S(2)}, u32[]{:S(2)}) collective-permute-start(bf16[7,32,16,2]{1,2,3,0:T(8,128)(2,1)S(1)} %pad_maximum_fusion.8), channel_id=1, source_target_pairs={{0,16},{16,32},{32,48},{1,17},{17,33},{33,49},{2,18},{18,34},{34,5... | collective-permute-start | bytes 43016 | tf_op jit(solution)/shard_map/ppermute | solution.py:131
  31.1 4.2 %copy-start.1 = (f32[3,16]{1,0:T(4,128)S(1)}, f32[3,16]{1,0:T(4,128)}, u32[]{:S(2)}) copy-start(f32[3,16]{1,0:T(4,128)} %param.17) | copy-start | bytes 580
  43.3 1.7 %copy-start.7 = (pred[18,6]{0,1:T(8,128)(4,1)S(1)}, pred[18,6]{0,1:T(8,128)(4,1)}, u32[]{:S(2)}) copy-start(pred[18,6]{0,1:T(8,128)(4,1)} %constant.82.clone) | copy-start | bytes 328
  43.3 1.7 %copy-start.8 = (pred[18,6]{0,1:T(8,128)(4,1)S(1)}, pred[18,6]{0,1:T(8,128)(4,1)}, u32[]{:S(2)}) copy-start(pred[18,6]{0,1:T(8,128)(4,1)} %constant.81.clone) | copy-start | bytes 328
  43.4 1.7 %copy-start.9 = (pred[18,6]{0,1:T(8,128)(4,1)S(1)}, pred[18,6]{0,1:T(8,128)(4,1)}, u32[]{:S(2)}) copy-start(pred[18,6]{0,1:T(8,128)(4,1)} %constant.80.clone) | copy-start | bytes 328
  43.4 12.6 %copy-start.2 = (pred[130,20]{0,1:T(8,128)(4,1)S(1)}, pred[130,20]{0,1:T(8,128)(4,1)}, u32[]{:S(2)}) copy-start(pred[130,20]{0,1:T(8,128)(4,1)} %constant.85.clone) | copy-start | bytes 7804
  43.4 12.6 %copy-start.3 = (pred[130,20]{0,1:T(8,128)(4,1)S(1)}, pred[130,20]{0,1:T(8,128)(4,1)}, u32[]{:S(2)}) copy-start(pred[130,20]{0,1:T(8,128)(4,1)} %constant.84.clone) | copy-start | bytes 7804
  43.4 12.6 %copy-start.4 = (pred[130,20]{0,1:T(8,128)(4,1)S(1)}, pred[130,20]{0,1:T(8,128)(4,1)}, u32[]{:S(2)}) copy-start(pred[130,20]{0,1:T(8,128)(4,1)} %constant.83.clone) | copy-start | bytes 7804
  45.3 10.7 %collective-permute-start.4 = (f32[4,2,128]{2,1,0:T(2,128)S(1)}, f32[4,2,128]{2,1,0:T(2,128)S(1)}, u32[]{:S(2)}, u32[]{:S(2)}) collective-permute-start(f32[4,2,128]{2,1,0:T(2,128)S(1)} %get-tuple-element.21), channel_id=1, source_target_pairs={{0,1},{1,2},{2,3},{3,4},{4,5},{5,6},{6,7},{7,8},{8,9},{9,10},{10,1... | collective-permute-start | bytes 12296 | tf_op jit(solution)/shard_map/ppermute | solution.py:15
  50.5 9.4 %collective-permute-start.5 = (f32[4,2,128]{2,1,0:T(2,128)S(1)}, f32[4,2,128]{2,1,0:T(2,128)S(1)}, u32[]{:S(2)}, u32[]{:S(2)}) collective-permute-start(f32[4,2,128]{2,1,0:T(2,128)S(1)} %get-tuple-element.22), channel_id=1, source_target_pairs={{1,0},{2,1},{3,2},{4,3},{5,4},{6,5},{7,6},{8,7},{9,8},{10,9},{11,1... | collective-permute-start | bytes 12296 | tf_op jit(solution)/shard_map/ppermute | solution.py:18
  60.2 4.3 %collective-permute-start.6 = (f32[4,2,2]{2,0,1:T(4,128)S(1)}, f32[4,2,2]{2,0,1:T(4,128)S(1)}, u32[]{:S(2)}, u32[]{:S(2)}) collective-permute-start(f32[4,2,2]{2,0,1:T(4,128)S(1)} %get-tuple-element.26), channel_id=1, source_target_pairs={{0,16},{16,32},{32,48},{1,17},{17,33},{33,49},{2,18},{18,34},{34,5... | collective-permute-start | bytes 200 | tf_op jit(solution)/shard_map/ppermute | solution.py:15
  63.2 5.5 %collective-permute-start.7 = (f32[4,2,2]{2,0,1:T(4,128)S(1)}, f32[4,2,2]{2,0,1:T(4,128)S(1)}, u32[]{:S(2)}, u32[]{:S(2)}) collective-permute-start(f32[4,2,2]{2,0,1:T(4,128)S(1)} %get-tuple-element.27), channel_id=1, source_target_pairs={{16,0},{32,16},{48,32},{17,1},{33,17},{49,33},{18,2},{34,18},{50,3... | collective-permute-start | bytes 200 | tf_op jit(solution)/shard_map/ppermute | solution.py:18
  68.8 1.3 %collective-permute-start.9 = (f32[2,16]{1,0:T(2,128)S(1)}, f32[2,16]{1,0:T(2,128)S(1)}, u32[]{:S(2)}, u32[]{:S(2)}) collective-permute-start(f32[2,16]{1,0:T(2,128)S(1)} %broadcast_multiply_fusion), channel_id=1, source_target_pairs={{64,0},{128,64},{192,128},{256,192},{320,256},{384,320},{448,384},... | collective-permute-start | bytes 392 | tf_op jit(solution)/shard_map/ppermute | solution.py:26
  68.9 4.4 %collective-permute-start.8 = (f32[2,16]{1,0:T(2,128)S(1)}, f32[2,16]{1,0:T(2,128)S(1)}, u32[]{:S(2)}, u32[]{:S(2)}) collective-permute-start(f32[2,16]{1,0:T(2,128)S(1)} %broadcast_multiply_fusion.1), channel_id=1, source_target_pairs={{448,0},{0,64},{64,128},{128,192},{192,256},{256,320},{320,384},{3... | collective-permute-start | bytes 392 | tf_op jit(solution)/shard_map/ppermute | solution.py:26

commit v10 on v9

--- a/solution.py
+++ b/solution.py
@@ -213,8 +213,11 @@
     gate_before = link[(patch_index + patches - 1) % patches].astype(jnp.float32)
     from_before = from_behind(out_face * gate_here, "patch", 1)
     from_after = from_behind(in_face * gate_before, "patch", -1)
-    design = reduced + in_mask * from_before[None] + out_mask * from_after[None]
-    return design[None]
+    rows = [
+        reduced[layer] + in_mask[layer] * from_before + out_mask[layer] * from_after
+        for layer in range(layers_d)
+    ]
+    return jnp.stack(rows)[None]
 
 
 def solution(mesh):

time: 74.6 us -> 81.1 us (1.087)
  other arithmetic: 12.9 us -> 18.5 us
    another operation x2 -> x3, other arithmetic: 0.02 us -> 5 us  [the longest x1 4.98 us: shards(): return jnp.stack(rows)[None]]
    slice x0 -> x3, local copies, waits for them, and re-layouts: none -> 1.32 us  [the longest x1 0.67 us: shards(): out_mask[layer] * from_after]
  transfers between devices with their start and end apart: 10 -> 10, of which waited for: 4 -> 4; matrix products, arithmetic and copies ran while one was open for 11% -> 12% of each run, Pallas kernels for 0% -> 0%
where the time goes in v10:
time: 81.1 us; the launch traced here: 80.3 us
  starting transfers between devices  36.1 us (45%)
  other arithmetic  18.5 us (23%)
  waiting for transfers between devices  12 us (15%)
  local copies, waits for them, and re-layouts  9.78 us (12%)
  between operations  3.16 us (4%)
    ppermute x2, starting transfers between devices, neighbour_rows(): lax.ppermute(with_rider(lax.slice_in_dim(stacked, length - width, None, a...  13.6 us
    ppermute x2, starting transfers between devices, with_halo(): lax.ppermute(lax.slice_in_dim(block, block.shape[dim] - width, None, axis...  8.12 us
    ppermute x2, waiting for transfers between devices, with_halo(): lax.ppermute(lax.slice_in_dim(block, 0, width, axis=dim), axis, backward)  8.07 us
    ppermute x2, starting transfers between devices, neighbour_rows(): lax.ppermute(with_rider(lax.slice_in_dim(stacked, 0, width, axis=dim), co...  7.1 us
    ppermute x2, starting transfers between devices, with_halo(): lax.ppermute(lax.slice_in_dim(block, 0, width, axis=dim), axis, backward)  6.75 us
    div x1, other arithmetic, slopes_along(): (8.0 * (shifted(1) - shifted(-1)) - (shifted(2) - shifted(-2))) / 12.0  6.06 us
    another operation x1, other arithmetic, shards(): return jnp.stack(rows)[None]  4.98 us
    ppermute x2, waiting for transfers between devices, from_behind(): return lax.ppermute(block, axis, route)  3.86 us
  transfers between devices with their start and end apart: 10, of which 4 were waited for; matrix products, arithmetic and copies ran while one was open for 12% of the time, Pallas kernels for 0%

profile of v10, /device:TPU:6, one launch (start us, length us, event | category | flops | bytes accessed | tf_op | source)
XLA Modules:
  0.0 80.3 jit_solution(16063926866333565976)
XLA Ops:
  0.0 1.0 %slice_reduce_fusion.2 = (f32[3]{0:T(128)S(1)}, f32[3]{0:T(128)S(1)}) fusion(f32[3,16]{1,0:T(4,128)} %param.17), kind=kLoop, calls=%fused_computation.145 | loop fusion | bytes 48 | tf_op jit(solution)/shard_map/slice | solution.py:134
  1.0 1.3 %slice_bitcast_fusion = (bf16[3,32,16,128]{3,2,1,0:T(8,128)(2,1)S(1)}, bf16[3,32,16,128]{3,2,1,0:T(8,128)(2,1)S(1)}) fusion(bf16[1,8,32,16,128]{4,3,2,1,0:T(8,128)(2,1)} %param.15), kind=kLoop, calls=%fused_computation.48 | loop fusion | bytes 1572864 | tf_op jit(solution)/shard_map/slice | solution.py:171
  2.2 0.2 fusion.36
  2.5 0.2 pad_maximum_fusion.5
  2.7 9.1 %collective-permute-start = (bf16[7,32,2,128]{3,2,1,0:T(2,128)(2,1)S(1)}, bf16[7,32,2,128]{3,2,1,0:T(2,128)(2,1)}, u32[]{:S(2)}, u32[]{:S(2)}) collective-permute-start(bf16[7,32,2,128]{3,2,1,0:T(2,128)(2,1)S(1)} %pad_maximum_fusion.5), channel_id=1, source_target_pairs={{0,1},{1,2},{2,3},{3,4},{4,5},{5,6},{6,7},{7,8},{8,9},{9,10},{10,1... | collective-permute-start | bytes 344072 | tf_op jit(solution)/shard_map/ppermute | solution.py:131
  11.8 0.8 %pad_maximum_fusion.6 = bf16[7,32,2,128]{3,2,1,0:T(2,128)(2,1)} fusion(bf16[1,32,2,128]{3,2,1,0:T(2,128)(2,1)S(1)} %broadcast_in_dim.121, bf16[6,32,2,128]{3,2,1,0:T(2,128)(2,1)S(1)} %get-tuple-element.17), kind=kLoop, calls=%fused_computation.72 | loop fusion | flops 57344 | bytes 229376 | tf_op jit(solution)/shard_map/concatenate | solution.py:123
  12.6 5.8 %collective-permute-start.1 = (bf16[7,32,2,128]{3,2,1,0:T(2,128)(2,1)}, bf16[7,32,2,128]{3,2,1,0:T(2,128)(2,1)}, u32[]{:S(2)}, u32[]{:S(2)}) collective-permute-start(bf16[7,32,2,128]{3,2,1,0:T(2,128)(2,1)} %pad_maximum_fusion.6), channel_id=1, source_target_pairs={{1,0},{2,1},{3,2},{4,3},{5,4},{6,5},{7,6},{8,7},{9,8},{10,9},{11,1... | collective-permute-start | bytes 344072 | tf_op jit(solution)/shard_map/ppermute | solution.py:134
  18.5 0.3 fusion.20
  18.8 0.2 slice_reduce_fusion
  19.0 0.1 copy.107
  19.1 0.8 copy.97
  19.9 1.3 %collective-permute-start.2 = (bf16[7,32,16,2]{1,2,3,0:T(8,128)(2,1)S(1)}, bf16[7,32,16,2]{1,2,3,0:T(8,128)(2,1)S(1)}, u32[]{:S(2)}, u32[]{:S(2)}) collective-permute-start(bf16[7,32,16,2]{1,2,3,0:T(8,128)(2,1)S(1)} %pad_maximum_fusion.7), channel_id=1, source_target_pairs={{16,0},{32,16},{48,32},{17,1},{33,17},{49,33},{18,2},{34,18},{50,3... | collective-permute-start | bytes 43016 | tf_op jit(solution)/shard_map/ppermute | solution.py:134
  21.2 0.1 copy.108
  21.4 0.8 copy.100
  22.2 4.5 %collective-permute-start.3 = (bf16[7,32,16,2]{1,2,3,0:T(8,128)(2,1)S(1)}, bf16[7,32,16,2]{1,2,3,0:T(8,128)(2,1)S(1)}, u32[]{:S(2)}, u32[]{:S(2)}) collective-permute-start(bf16[7,32,16,2]{1,2,3,0:T(8,128)(2,1)S(1)} %pad_maximum_fusion.8), channel_id=1, source_target_pairs={{0,16},{16,32},{32,48},{1,17},{17,33},{33,49},{2,18},{18,34},{34,5... | collective-permute-start | bytes 43016 | tf_op jit(solution)/shard_map/ppermute | solution.py:131
  26.7 0.1 fusion.21
  26.9 0.7 constant_dynamic-slice_fusion
  28.9 0.1 pad_maximum_fusion.10
  29.0 0.7 fusion.106
  29.7 0.6 fusion.105
  30.3 0.7 fusion.107
  32.5 0.8 copy.101
  33.3 1.8 %copy.98 = f32[6,32,16,2]{3,2,1,0:T(8,128)} copy(f32[6,32,16,2]{1,2,3,0:T(8,128)S(1)} %slice_convert_fusion.3) | data formatting | bytes 49152 | tf_op jit(solution)/shard_map/convert_element_type | solution.py:144
  35.1 0.1 pad_maximum_fusion.14
  35.2 0.7 slice_convert_fusion.5
  35.9 0.1 copy.94
  36.0 0.7 slice_convert_fusion.4
  36.6 0.1 copy.95
  36.8 1.0 %slice_convert_fusion = f32[6,32,2,128]{3,2,1,0:T(2,128)S(1)} fusion(bf16[7,32,2,128]{3,2,1,0:T(2,128)(2,1)} %collective-permute-done), kind=kLoop, calls=%fused_computation.75 | loop fusion | flops 49152 | bytes 294912 | tf_op jit(solution)/shard_map/convert_element_type | solution.py:144
  37.8 1.0 %slice_convert_fusion.1 = f32[6,32,2,128]{3,2,1,0:T(2,128)S(1)} fusion(bf16[7,32,2,128]{3,2,1,0:T(2,128)(2,1)} %collective-permute-done.1), kind=kLoop, calls=%fused_computation.76 | loop fusion | flops 49152 | bytes 294912 | tf_op jit(solution)/shard_map/convert_element_type | solution.py:144
  38.8 6.1 %fusion.3 = (f32[6,32,16,128]{3,2,1,0:T(8,128)S(1)}, f32[6,32,16,128]{3,2,1,0:T(8,128)S(1)}, f32[6,32,16,128]{3,2,1,0:T(8,128)S(1)}) fusion(f32[6,32,16,128]{3,2,1,0:T(8,128)S(1)} %fusion.21, f32[6,32,16,2]{3,2,1,0:T(8,128)S(1)} %copy.101, f32[6,32,16,2]{3,2,1,0:T(8,128)} %copy.98, f32[6,32,2,128]{3,2,1,0:T(2,128)S(1)} %slice_convert_fusion, ...), kind=kLoop, calls=%fused_computation.15 | loop fusion | flops 9043968 | bytes 6733824 | tf_op jit(solution)/shard_map/div | solution.py:150
  44.9 1.3 %fusion.25 = f32[32,16,128]{2,1,0:T(8,128)S(1)} fusion(f32[6,32,16,128]{3,2,1,0:T(8,128)S(1)} %get-tuple-element.13, f32[6,32,16,128]{3,2,1,0:T(8,128)S(1)} %get-tuple-element.14, f32[6,32,16,128]{3,2,1,0:T(8,128)S(1)} %get-tuple-element.12, bf16[1,8,32,16,128]{4,3,2,1,0:T(8,128)(2,1)} %param.15), kind=kLoop, calls=%fused_computation.54 | loop fusion | flops 1769472 | bytes 5242880 | tf_op jit(solution)/shard_map/sub | solution.py:191
  46.2 0.3 fusion.33
  46.6 0.2 convolution_bitcast_fusion
  46.8 5.2 %collective-permute-start.4 = (f32[4,2,128]{2,1,0:T(2,128)S(1)}, f32[4,2,128]{2,1,0:T(2,128)S(1)}, u32[]{:S(2)}, u32[]{:S(2)}) collective-permute-start(f32[4,2,128]{2,1,0:T(2,128)S(1)} %get-tuple-element.21), channel_id=1, source_target_pairs={{0,1},{1,2},{2,3},{3,4},{4,5},{5,6},{6,7},{7,8},{8,9},{9,10},{10,1... | collective-permute-start | bytes 12296 | tf_op jit(solution)/shard_map/ppermute | solution.py:15
  52.0 5.5 %collective-permute-start.5 = (f32[4,2,128]{2,1,0:T(2,128)S(1)}, f32[4,2,128]{2,1,0:T(2,128)S(1)}, u32[]{:S(2)}, u32[]{:S(2)}) collective-permute-start(f32[4,2,128]{2,1,0:T(2,128)S(1)} %get-tuple-element.22), channel_id=1, source_target_pairs={{1,0},{2,1},{3,2},{4,3},{5,4},{6,5},{7,6},{8,7},{9,8},{10,9},{11,1... | collective-permute-start | bytes 12296 | tf_op jit(solution)/shard_map/ppermute | solution.py:18
  57.5 3.9 %collective-permute-done.5 = f32[4,2,128]{2,1,0:T(2,128)S(1)} collective-permute-done((f32[4,2,128]{2,1,0:T(2,128)S(1)}, f32[4,2,128]{2,1,0:T(2,128)S(1)}, u32[]{:S(2)}, u32[]{:S(2)}) %collective-permute-start.5) | collective-permute-done | bytes 4128 | tf_op jit(solution)/shard_map/ppermute | solution.py:18
  61.4 0.2 fusion.47
  61.7 0.1 fusion.104
  61.7 2.9 %collective-permute-start.6 = (f32[4,2,2]{2,0,1:T(4,128)S(1)}, f32[4,2,2]{2,0,1:T(4,128)S(1)}, u32[]{:S(2)}, u32[]{:S(2)}) collective-permute-start(f32[4,2,2]{2,0,1:T(4,128)S(1)} %get-tuple-element.30), channel_id=1, source_target_pairs={{0,16},{16,32},{32,48},{1,17},{17,33},{33,49},{2,18},{18,34},{34,5... | collective-permute-start | bytes 200 | tf_op jit(solution)/shard_map/ppermute | solution.py:15
  64.7 1.3 %collective-permute-start.7 = (f32[4,2,2]{2,0,1:T(4,128)S(1)}, f32[4,2,2]{2,0,1:T(4,128)S(1)}, u32[]{:S(2)}, u32[]{:S(2)}) collective-permute-start(f32[4,2,2]{2,0,1:T(4,128)S(1)} %get-tuple-element.31), channel_id=1, source_target_pairs={{16,0},{32,16},{48,32},{17,1},{33,17},{49,33},{18,2},{34,18},{50,3... | collective-permute-start | bytes 200 | tf_op jit(solution)/shard_map/ppermute | solution.py:18
  66.0 4.2 %collective-permute-done.7 = f32[4,2,2]{2,0,1:T(4,128)S(1)} collective-permute-done((f32[4,2,2]{2,0,1:T(4,128)S(1)}, f32[4,2,2]{2,0,1:T(4,128)S(1)}, u32[]{:S(2)}, u32[]{:S(2)}) %collective-permute-start.7) | collective-permute-done | bytes 96 | tf_op jit(solution)/shard_map/ppermute | solution.py:18
  70.2 0.1 multiply_reduce_fusion.1
  70.3 0.5 collective-permute-start.8
  70.8 0.8 collective-permute-done.9
  71.6 3.1 %collective-permute-done.8 = f32[2,16]{1,0:T(2,128)S(1)} collective-permute-done((f32[2,16]{1,0:T(2,128)S(1)}, f32[2,16]{1,0:T(2,128)S(1)}, u32[]{:S(2)}, u32[]{:S(2)}) %collective-permute-start.8) | collective-permute-done | bytes 160 | tf_op jit(solution)/shard_map/ppermute | solution.py:26
  74.7 5.0 %add_bitcast_fusion.5 = (f32[1,2,16]{2,1,0:T(2,128)S(1)}, f32[1,2,16]{2,1,0:T(2,128)S(1)}, f32[1,2,16]{2,1,0:T(2,128)S(1)}, f32[1,2,16]{2,1,0:T(2,128)S(1)}) fusion(f32[2,16]{1,0:T(2,128)S(1)} %collective-permute-done.9, f32[2,16]{1,0:T(2,128)S(1)} %bitcast.111, f32[2,16]{1,0:T(2,128)S(1)} %collective-permute-done.8, f32[]{:T(128)} %bitcast.29, ...), kind=kLoop, calls=%fused_computation.162 | loop fusion | flops 512 | bytes 1312 | tf_op jit(solution)/shard_map/stack | solution.py:220
  79.7 0.6 maximum_bitcast_fusion
  (70 shorter events, 0.6 us)
Async XLA Ops:
  2.5 16.3 %copy-start = (f32[3,128]{1,0:T(4,128)S(1)}, f32[3,128]{1,0:T(4,128)}, u32[]{:S(2)}) copy-start(f32[3,128]{1,0:T(4,128)} %param.16) | copy-start | bytes 4612
  2.7 32.5 %collective-permute-start = (bf16[7,32,2,128]{3,2,1,0:T(2,128)(2,1)S(1)}, bf16[7,32,2,128]{3,2,1,0:T(2,128)(2,1)}, u32[]{:S(2)}, u32[]{:S(2)}) collective-permute-start(bf16[7,32,2,128]{3,2,1,0:T(2,128)(2,1)S(1)} %pad_maximum_fusion.5), channel_id=1, source_target_pairs={{0,1},{1,2},{2,3},{3,4},{4,5},{5,6},{6,7},{7,8},{8,9},{9,10},{10,1... | collective-permute-start | bytes 344072 | tf_op jit(solution)/shard_map/ppermute | solution.py:131
  12.6 23.3 %collective-permute-start.1 = (bf16[7,32,2,128]{3,2,1,0:T(2,128)(2,1)}, bf16[7,32,2,128]{3,2,1,0:T(2,128)(2,1)}, u32[]{:S(2)}, u32[]{:S(2)}) collective-permute-start(bf16[7,32,2,128]{3,2,1,0:T(2,128)(2,1)} %pad_maximum_fusion.6), channel_id=1, source_target_pairs={{1,0},{2,1},{3,2},{4,3},{5,4},{6,5},{7,6},{8,7},{9,8},{10,9},{11,1... | collective-permute-start | bytes 344072 | tf_op jit(solution)/shard_map/ppermute | solution.py:134
  19.9 12.4 %collective-permute-start.2 = (bf16[7,32,16,2]{1,2,3,0:T(8,128)(2,1)S(1)}, bf16[7,32,16,2]{1,2,3,0:T(8,128)(2,1)S(1)}, u32[]{:S(2)}, u32[]{:S(2)}) collective-permute-start(bf16[7,32,16,2]{1,2,3,0:T(8,128)(2,1)S(1)} %pad_maximum_fusion.7), channel_id=1, source_target_pairs={{16,0},{32,16},{48,32},{17,1},{33,17},{49,33},{18,2},{34,18},{50,3... | collective-permute-start | bytes 43016 | tf_op jit(solution)/shard_map/ppermute | solution.py:134
  21.3 5.5 %copy-start.10 = (s32[8,2]{0,1:T(2,128)S(1)}, s32[8,2]{0,1:T(2,128)}, u32[]{:S(2)}) copy-start(s32[8,2]{0,1:T(2,128)} %param.19) | copy-start | bytes 196
  21.3 7.5 %copy-start.5 = (f32[3,32]{1,0:T(4,128)S(1)}, f32[3,32]{1,0:T(4,128)}, u32[]{:S(2)}) copy-start(f32[3,32]{1,0:T(4,128)} %param.18) | copy-start | bytes 1156
  21.3 8.3 %copy-start.11 = (pred[34,4]{0,1:T(4,128)(4,1)S(1)}, pred[34,4]{0,1:T(4,128)(4,1)}, u32[]{:S(2)}) copy-start(pred[34,4]{0,1:T(4,128)(4,1)} %constant.79.clone) | copy-start | bytes 412
  21.3 8.3 %copy-start.12 = (pred[34,4]{0,1:T(4,128)(4,1)S(1)}, pred[34,4]{0,1:T(4,128)(4,1)}, u32[]{:S(2)}) copy-start(pred[34,4]{0,1:T(4,128)(4,1)} %constant.78.clone) | copy-start | bytes 412
  21.4 8.3 %copy-start.13 = (pred[34,4]{0,1:T(4,128)(4,1)S(1)}, pred[34,4]{0,1:T(4,128)(4,1)}, u32[]{:S(2)}) copy-start(pred[34,4]{0,1:T(4,128)(4,1)} %constant.77.clone) | copy-start | bytes 412
  21.4 8.9 %copy-start.6 = (s32[8]{0:T(128)S(1)}, s32[8]{0:T(128)}, u32[]{:S(2)}) copy-start(s32[8]{0:T(128)} %param.20) | copy-start | bytes 100
  22.2 10.2 %collective-permute-start.3 = (bf16[7,32,16,2]{1,2,3,0:T(8,128)(2,1)S(1)}, bf16[7,32,16,2]{1,2,3,0:T(8,128)(2,1)S(1)}, u32[]{:S(2)}, u32[]{:S(2)}) collective-permute-start(bf16[7,32,16,2]{1,2,3,0:T(8,128)(2,1)S(1)} %pad_maximum_fusion.8), channel_id=1, source_target_pairs={{0,16},{16,32},{32,48},{1,17},{17,33},{33,49},{2,18},{18,34},{34,5... | collective-permute-start | bytes 43016 | tf_op jit(solution)/shard_map/ppermute | solution.py:131
  32.5 4.3 %copy-start.1 = (f32[3,16]{1,0:T(4,128)S(1)}, f32[3,16]{1,0:T(4,128)}, u32[]{:S(2)}) copy-start(f32[3,16]{1,0:T(4,128)} %param.17) | copy-start | bytes 580
  44.8 1.7 %copy-start.7 = (pred[18,6]{0,1:T(8,128)(4,1)S(1)}, pred[18,6]{0,1:T(8,128)(4,1)}, u32[]{:S(2)}) copy-start(pred[18,6]{0,1:T(8,128)(4,1)} %constant.82.clone) | copy-start | bytes 328
  44.8 1.7 %copy-start.8 = (pred[18,6]{0,1:T(8,128)(4,1)S(1)}, pred[18,6]{0,1:T(8,128)(4,1)}, u32[]{:S(2)}) copy-start(pred[18,6]{0,1:T(8,128)(4,1)} %constant.81.clone) | copy-start | bytes 328
  44.8 1.7 %copy-start.9 = (pred[18,6]{0,1:T(8,128)(4,1)S(1)}, pred[18,6]{0,1:T(8,128)(4,1)}, u32[]{:S(2)}) copy-start(pred[18,6]{0,1:T(8,128)(4,1)} %constant.80.clone) | copy-start | bytes 328
  44.9 12.6 %copy-start.2 = (pred[130,20]{0,1:T(8,128)(4,1)S(1)}, pred[130,20]{0,1:T(8,128)(4,1)}, u32[]{:S(2)}) copy-start(pred[130,20]{0,1:T(8,128)(4,1)} %constant.85.clone) | copy-start | bytes 7804
  44.9 12.6 %copy-start.3 = (pred[130,20]{0,1:T(8,128)(4,1)S(1)}, pred[130,20]{0,1:T(8,128)(4,1)}, u32[]{:S(2)}) copy-start(pred[130,20]{0,1:T(8,128)(4,1)} %constant.84.clone) | copy-start | bytes 7804
  44.9 12.6 %copy-start.4 = (pred[130,20]{0,1:T(8,128)(4,1)S(1)}, pred[130,20]{0,1:T(8,128)(4,1)}, u32[]{:S(2)}) copy-start(pred[130,20]{0,1:T(8,128)(4,1)} %constant.83.clone) | copy-start | bytes 7804
  46.8 10.7 %collective-permute-start.4 = (f32[4,2,128]{2,1,0:T(2,128)S(1)}, f32[4,2,128]{2,1,0:T(2,128)S(1)}, u32[]{:S(2)}, u32[]{:S(2)}) collective-permute-start(f32[4,2,128]{2,1,0:T(2,128)S(1)} %get-tuple-element.21), channel_id=1, source_target_pairs={{0,1},{1,2},{2,3},{3,4},{4,5},{5,6},{6,7},{7,8},{8,9},{9,10},{10,1... | collective-permute-start | bytes 12296 | tf_op jit(solution)/shard_map/ppermute | solution.py:15
  52.0 9.4 %collective-permute-start.5 = (f32[4,2,128]{2,1,0:T(2,128)S(1)}, f32[4,2,128]{2,1,0:T(2,128)S(1)}, u32[]{:S(2)}, u32[]{:S(2)}) collective-permute-start(f32[4,2,128]{2,1,0:T(2,128)S(1)} %get-tuple-element.22), channel_id=1, source_target_pairs={{1,0},{2,1},{3,2},{4,3},{5,4},{6,5},{7,6},{8,7},{9,8},{10,9},{11,1... | collective-permute-start | bytes 12296 | tf_op jit(solution)/shard_map/ppermute | solution.py:18
  61.7 4.2 %collective-permute-start.6 = (f32[4,2,2]{2,0,1:T(4,128)S(1)}, f32[4,2,2]{2,0,1:T(4,128)S(1)}, u32[]{:S(2)}, u32[]{:S(2)}) collective-permute-start(f32[4,2,2]{2,0,1:T(4,128)S(1)} %get-tuple-element.30), channel_id=1, source_target_pairs={{0,16},{16,32},{32,48},{1,17},{17,33},{33,49},{2,18},{18,34},{34,5... | collective-permute-start | bytes 200 | tf_op jit(solution)/shard_map/ppermute | solution.py:15
  64.7 5.5 %collective-permute-start.7 = (f32[4,2,2]{2,0,1:T(4,128)S(1)}, f32[4,2,2]{2,0,1:T(4,128)S(1)}, u32[]{:S(2)}, u32[]{:S(2)}) collective-permute-start(f32[4,2,2]{2,0,1:T(4,128)S(1)} %get-tuple-element.31), channel_id=1, source_target_pairs={{16,0},{32,16},{48,32},{17,1},{33,17},{49,33},{18,2},{34,18},{50,3... | collective-permute-start | bytes 200 | tf_op jit(solution)/shard_map/ppermute | solution.py:18
  70.3 1.3 %collective-permute-start.9 = (f32[2,16]{1,0:T(2,128)S(1)}, f32[2,16]{1,0:T(2,128)S(1)}, u32[]{:S(2)}, u32[]{:S(2)}) collective-permute-start(f32[2,16]{1,0:T(2,128)S(1)} %broadcast_multiply_fusion), channel_id=1, source_target_pairs={{64,0},{128,64},{192,128},{256,192},{320,256},{384,320},{448,384},... | collective-permute-start | bytes 392 | tf_op jit(solution)/shard_map/ppermute | solution.py:26
  70.3 4.4 %collective-permute-start.8 = (f32[2,16]{1,0:T(2,128)S(1)}, f32[2,16]{1,0:T(2,128)S(1)}, u32[]{:S(2)}, u32[]{:S(2)}) collective-permute-start(f32[2,16]{1,0:T(2,128)S(1)} %broadcast_multiply_fusion.1), channel_id=1, source_target_pairs={{448,0},{0,64},{64,128},{128,192},{192,256},{256,320},{320,384},{3... | collective-permute-start | bytes 392 | tf_op jit(solution)/shard_map/ppermute | solution.py:26

commit v11 on v9

--- a/solution.py
+++ b/solution.py
@@ -197,8 +197,9 @@
     mat_v = smoothed_band(jnp.concatenate([coef_low_v, coef_v, coef_high_v], axis=1), columns_v, 2)
     mat_u = smoothed_band(jnp.concatenate([coef_low_u, coef_u, coef_high_u], axis=1), columns_u, 2)
     reduced = jnp.einsum("wvu,wa->avu", density, mat_w, precision=highest)
-    reduced = fold_vert(jnp.einsum("avu,vb->abu", reduced, mat_v, precision=highest))
-    reduced = fold_first(jnp.einsum("abu,uc->abc", reduced, mat_u, precision=highest))
+    reduced = jnp.einsum("avu,uc->avc", reduced, mat_u, precision=highest)
+    reduced = fold_vert(jnp.einsum("avc,vb->abc", reduced, mat_v, precision=highest))
+    reduced = fold_first(reduced)
     patch_index = lax.axis_index("patch")
     patches = lax.axis_size("patch")
     layers_d = reduced.shape[0]

time: 74.6 us -> 77.3 us (1.036)
  waiting for transfers between devices: 12 us -> 15.2 us
  starting transfers between devices: 36.2 us -> 34.5 us
  other arithmetic: 12.9 us -> 14.1 us
    ppermute x2, waiting for transfers between devices: 0.01 us -> 2.41 us  [neighbour_rows(): lax.ppermute(with_rider(lax.slice_in_dim(stacked, 0, width, axis=dim), co...]
    ppermute x2, starting transfers between devices: 13.6 us -> 12 us  [neighbour_rows(): lax.ppermute(with_rider(lax.slice_in_dim(stacked, length - width, None, a...]
    convert_element_type x1, local copies, waits for them, and re-layouts: 0.75 us -> 1.82 us  [slopes_along(): low.astype(jnp.float32)]
    convert_element_type x1, local copies, waits for them, and re-layouts: 1.82 us -> 0.75 us  [slopes_along(): high.astype(jnp.float32)]
    ppermute x2, waiting for transfers between devices: 8.07 us -> 8.9 us  [with_halo(): lax.ppermute(lax.slice_in_dim(block, 0, width, axis=dim), axis, backward)]
  transfers between devices with their start and end apart: 10 -> 10, of which waited for: 4 -> 5; matrix products, arithmetic and copies ran while one was open for 11% -> 12% of each run, Pallas kernels for 0% -> 0%
where the time goes in v11:
time: 77.3 us; the launch traced here: 76 us
  starting transfers between devices  34.5 us (45%)
  waiting for transfers between devices  15.2 us (20%)
  other arithmetic  14.1 us (18%)
  local copies, waits for them, and re-layouts  8.38 us (11%)
  between operations  3.05 us (4%)
    ppermute x2, starting transfers between devices, neighbour_rows(): lax.ppermute(with_rider(lax.slice_in_dim(stacked, length - width, None, a...  12 us
    ppermute x2, waiting for transfers between devices, with_halo(): lax.ppermute(lax.slice_in_dim(block, 0, width, axis=dim), axis, backward)  8.9 us
    ppermute x2, starting transfers between devices, with_halo(): lax.ppermute(lax.slice_in_dim(block, block.shape[dim] - width, None, axis...  8.1 us
    ppermute x2, starting transfers between devices, neighbour_rows(): lax.ppermute(with_rider(lax.slice_in_dim(stacked, 0, width, axis=dim), co...  7.12 us
    ppermute x2, starting transfers between devices, with_halo(): lax.ppermute(lax.slice_in_dim(block, 0, width, axis=dim), axis, backward)  6.7 us
    div x1, other arithmetic, slopes_along(): (8.0 * (shifted(1) - shifted(-1)) - (shifted(2) - shifted(-2))) / 12.0  6.06 us
    ppermute x2, waiting for transfers between devices, from_behind(): return lax.ppermute(block, axis, route)  3.87 us
    ppermute x2, waiting for transfers between devices, neighbour_rows(): lax.ppermute(with_rider(lax.slice_in_dim(stacked, 0, width, axis=dim), co...  2.41 us
  transfers between devices with their start and end apart: 10, of which 5 were waited for; matrix products, arithmetic and copies ran while one was open for 12% of the time, Pallas kernels for 0%

profile of v11, /device:TPU:6, one launch (start us, length us, event | category | flops | bytes accessed | tf_op | source)
XLA Modules:
  0.0 76.0 jit_solution(7272623199228890042)
XLA Ops:
  0.0 1.0 %slice_reduce_fusion.2 = (f32[3]{0:T(128)S(1)}, f32[3]{0:T(128)S(1)}) fusion(f32[3,16]{1,0:T(4,128)} %param.17), kind=kLoop, calls=%fused_computation.144 | loop fusion | bytes 48 | tf_op jit(solution)/shard_map/slice | solution.py:134
  1.0 1.3 %slice_bitcast_fusion = (bf16[3,32,16,128]{3,2,1,0:T(8,128)(2,1)S(1)}, bf16[3,32,16,128]{3,2,1,0:T(8,128)(2,1)S(1)}) fusion(bf16[1,8,32,16,128]{4,3,2,1,0:T(8,128)(2,1)} %param.15), kind=kLoop, calls=%fused_computation.48 | loop fusion | bytes 1572864 | tf_op jit(solution)/shard_map/slice | solution.py:171
  2.2 0.2 fusion.36
  2.5 0.2 pad_maximum_fusion.5
  2.7 9.1 %collective-permute-start = (bf16[7,32,2,128]{3,2,1,0:T(2,128)(2,1)S(1)}, bf16[7,32,2,128]{3,2,1,0:T(2,128)(2,1)}, u32[]{:S(2)}, u32[]{:S(2)}) collective-permute-start(bf16[7,32,2,128]{3,2,1,0:T(2,128)(2,1)S(1)} %pad_maximum_fusion.5), channel_id=1, source_target_pairs={{0,1},{1,2},{2,3},{3,4},{4,5},{5,6},{6,7},{7,8},{8,9},{9,10},{10,1... | collective-permute-start | bytes 344072 | tf_op jit(solution)/shard_map/ppermute | solution.py:131
  11.8 0.2 pad_maximum_fusion.6
  12.0 5.8 %collective-permute-start.1 = (bf16[7,32,2,128]{3,2,1,0:T(2,128)(2,1)S(1)}, bf16[7,32,2,128]{3,2,1,0:T(2,128)(2,1)}, u32[]{:S(2)}, u32[]{:S(2)}) collective-permute-start(bf16[7,32,2,128]{3,2,1,0:T(2,128)(2,1)S(1)} %pad_maximum_fusion.6), channel_id=1, source_target_pairs={{1,0},{2,1},{3,2},{4,3},{5,4},{6,5},{7,6},{8,7},{9,8},{10,9},{11,1... | collective-permute-start | bytes 344072 | tf_op jit(solution)/shard_map/ppermute | solution.py:134
  17.8 0.3 fusion.19
  18.1 0.2 slice_reduce_fusion.1
  18.3 0.1 copy.101
  18.5 0.8 %copy.94 = bf16[6,32,16,2]{1,2,3,0:T(8,128)(2,1)S(1)} copy(bf16[6,32,16,2]{3,2,1,0:T(8,128)(2,1)S(1)} %get-tuple-element.20) | data formatting | bytes 24576 | tf_op jit(solution)/shard_map/slice | solution.py:132
  19.3 2.9 %collective-permute-start.3 = (bf16[7,32,16,2]{1,2,3,0:T(8,128)(2,1)S(1)}, bf16[7,32,16,2]{1,2,3,0:T(8,128)(2,1)S(1)}, u32[]{:S(2)}, u32[]{:S(2)}) collective-permute-start(bf16[7,32,16,2]{1,2,3,0:T(8,128)(2,1)S(1)} %pad_maximum_fusion.8), channel_id=1, source_target_pairs={{0,16},{16,32},{32,48},{1,17},{17,33},{33,49},{2,18},{18,34},{34,5... | collective-permute-start | bytes 43016 | tf_op jit(solution)/shard_map/ppermute | solution.py:131
  22.2 0.1 copy.100
  22.4 0.8 %copy.91 = bf16[6,32,16,2]{1,2,3,0:T(8,128)(2,1)S(1)} copy(bf16[6,32,16,2]{3,2,1,0:T(8,128)(2,1)S(1)} %get-tuple-element.19) | data formatting | bytes 24576 | tf_op jit(solution)/shard_map/slice | solution.py:134
  23.2 1.3 %collective-permute-start.2 = (bf16[7,32,16,2]{1,2,3,0:T(8,128)(2,1)S(1)}, bf16[7,32,16,2]{1,2,3,0:T(8,128)(2,1)S(1)}, u32[]{:S(2)}, u32[]{:S(2)}) collective-permute-start(bf16[7,32,16,2]{1,2,3,0:T(8,128)(2,1)S(1)} %pad_maximum_fusion.7), channel_id=1, source_target_pairs={{16,0},{32,16},{48,32},{17,1},{33,17},{49,33},{18,2},{34,18},{50,3... | collective-permute-start | bytes 43016 | tf_op jit(solution)/shard_map/ppermute | solution.py:134
  24.5 0.1 fusion.21
  24.6 0.6 constant_dynamic-slice_fusion
  26.5 0.1 pad_maximum_fusion.10
  26.7 0.6 compare_convert_fusion
  27.2 0.1 add_bitcast_fusion.2
  27.3 2.4 %collective-permute-done.2 = bf16[7,32,16,2]{1,2,3,0:T(8,128)(2,1)S(1)} collective-permute-done((bf16[7,32,16,2]{1,2,3,0:T(8,128)(2,1)S(1)}, bf16[7,32,16,2]{1,2,3,0:T(8,128)(2,1)S(1)}, u32[]{:S(2)}, u32[]{:S(2)}) %collective-permute-start.2) | collective-permute-done | bytes 14368 | tf_op jit(solution)/shard_map/ppermute | solution.py:134
  29.8 0.8 copy.92
  30.6 1.8 %copy.95 = f32[6,32,16,2]{3,2,1,0:T(8,128)} copy(f32[6,32,16,2]{1,2,3,0:T(8,128)S(1)} %slice_convert_fusion.2) | data formatting | bytes 49152 | tf_op jit(solution)/shard_map/convert_element_type | solution.py:144
  32.4 0.1 pad_maximum_fusion.14
  32.5 0.7 select_add_fusion
  33.3 0.7 slice_convert_fusion.5
  33.9 0.1 copy.88
  34.0 0.6 slice_convert_fusion.4
  34.7 0.1 copy.89
  34.8 1.0 %slice_convert_fusion = f32[6,32,2,128]{3,2,1,0:T(2,128)S(1)} fusion(bf16[7,32,2,128]{3,2,1,0:T(2,128)(2,1)} %collective-permute-done), kind=kLoop, calls=%fused_computation.75 | loop fusion | flops 49152 | bytes 294912 | tf_op jit(solution)/shard_map/convert_element_type | solution.py:144
  35.8 1.0 %slice_convert_fusion.1 = f32[6,32,2,128]{3,2,1,0:T(2,128)S(1)} fusion(bf16[7,32,2,128]{3,2,1,0:T(2,128)(2,1)} %collective-permute-done.1), kind=kLoop, calls=%fused_computation.76 | loop fusion | flops 49152 | bytes 294912 | tf_op jit(solution)/shard_map/convert_element_type | solution.py:144
  36.8 6.1 %fusion.3 = (f32[6,32,16,128]{3,2,1,0:T(8,128)S(1)}, f32[6,32,16,128]{3,2,1,0:T(8,128)S(1)}, f32[6,32,16,128]{3,2,1,0:T(8,128)S(1)}) fusion(f32[6,32,16,128]{3,2,1,0:T(8,128)S(1)} %fusion.21, f32[6,32,16,2]{3,2,1,0:T(8,128)} %copy.95, f32[6,32,16,2]{3,2,1,0:T(8,128)S(1)} %copy.92, f32[6,32,2,128]{3,2,1,0:T(2,128)S(1)} %slice_convert_fusion, ...), kind=kLoop, calls=%fused_computation.15 | loop fusion | flops 9043968 | bytes 6733824 | tf_op jit(solution)/shard_map/div | solution.py:150
  42.9 1.3 %fusion.25 = f32[32,16,128]{2,1,0:T(8,128)S(1)} fusion(f32[6,32,16,128]{3,2,1,0:T(8,128)S(1)} %get-tuple-element.13, f32[6,32,16,128]{3,2,1,0:T(8,128)S(1)} %get-tuple-element.14, f32[6,32,16,128]{3,2,1,0:T(8,128)S(1)} %get-tuple-element.12, bf16[1,8,32,16,128]{4,3,2,1,0:T(8,128)(2,1)} %param.15), kind=kLoop, calls=%fused_computation.54 | loop fusion | flops 1769472 | bytes 5242880 | tf_op jit(solution)/shard_map/sub | solution.py:191
  44.2 0.3 fusion.33
  44.5 0.2 fusion.37
  44.8 0.2 convolution_bitcast_fusion
  45.0 5.2 %collective-permute-start.4 = (f32[4,2,20]{2,1,0:T(2,128)S(1)}, f32[4,2,20]{2,1,0:T(2,128)S(1)}, u32[]{:S(2)}, u32[]{:S(2)}) collective-permute-start(f32[4,2,20]{2,1,0:T(2,128)S(1)} %get-tuple-element.21), channel_id=1, source_target_pairs={{0,1},{1,2},{2,3},{3,4},{4,5},{5,6},{6,7},{7,8},{8,9},{9,10},{10,1... | collective-permute-start | bytes 1928 | tf_op jit(solution)/shard_map/ppermute | solution.py:15
  50.3 5.4 %collective-permute-start.5 = (f32[4,2,20]{2,1,0:T(2,128)S(1)}, f32[4,2,20]{2,1,0:T(2,128)S(1)}, u32[]{:S(2)}, u32[]{:S(2)}) collective-permute-start(f32[4,2,20]{2,1,0:T(2,128)S(1)} %get-tuple-element.22), channel_id=1, source_target_pairs={{1,0},{2,1},{3,2},{4,3},{5,4},{6,5},{7,6},{8,7},{9,8},{10,9},{11,1... | collective-permute-start | bytes 1928 | tf_op jit(solution)/shard_map/ppermute | solution.py:18
  55.7 0.6 fusion.103
  57.7 2.9 %collective-permute-done.5 = f32[4,2,20]{2,1,0:T(2,128)S(1)} collective-permute-done((f32[4,2,20]{2,1,0:T(2,128)S(1)}, f32[4,2,20]{2,1,0:T(2,128)S(1)}, u32[]{:S(2)}, u32[]{:S(2)}) %collective-permute-start.5) | collective-permute-done | bytes 672 | tf_op jit(solution)/shard_map/ppermute | solution.py:18
  60.7 2.9 %collective-permute-start.6 = (f32[4,2,2]{2,1,0:T(2,128)S(1)}, f32[4,2,2]{2,1,0:T(2,128)S(1)}, u32[]{:S(2)}, u32[]{:S(2)}) collective-permute-start(f32[4,2,2]{2,1,0:T(2,128)S(1)} %get-tuple-element.26), channel_id=1, source_target_pairs={{0,16},{16,32},{32,48},{1,17},{17,33},{33,49},{2,18},{18,34},{34,5... | collective-permute-start | bytes 200 | tf_op jit(solution)/shard_map/ppermute | solution.py:15
  63.5 1.3 %collective-permute-start.7 = (f32[4,2,2]{2,1,0:T(2,128)S(1)}, f32[4,2,2]{2,1,0:T(2,128)S(1)}, u32[]{:S(2)}, u32[]{:S(2)}) collective-permute-start(f32[4,2,2]{2,1,0:T(2,128)S(1)} %get-tuple-element.27), channel_id=1, source_target_pairs={{16,0},{32,16},{48,32},{17,1},{33,17},{49,33},{18,2},{34,18},{50,3... | collective-permute-start | bytes 200 | tf_op jit(solution)/shard_map/ppermute | solution.py:18
  64.9 6.0 %collective-permute-done.7 = f32[4,2,2]{2,1,0:T(2,128)S(1)} collective-permute-done((f32[4,2,2]{2,1,0:T(2,128)S(1)}, f32[4,2,2]{2,1,0:T(2,128)S(1)}, u32[]{:S(2)}, u32[]{:S(2)}) %collective-permute-start.7) | collective-permute-done | bytes 96 | tf_op jit(solution)/shard_map/ppermute | solution.py:18
  70.8 0.1 multiply_reduce_fusion.1
  71.0 0.5 collective-permute-start.8
  71.5 0.8 %collective-permute-done.9 = f32[2,16]{1,0:T(2,128)S(1)} collective-permute-done((f32[2,16]{1,0:T(2,128)S(1)}, f32[2,16]{1,0:T(2,128)S(1)}, u32[]{:S(2)}, u32[]{:S(2)}) %collective-permute-start.9) | collective-permute-done | bytes 160 | tf_op jit(solution)/shard_map/ppermute | solution.py:26
  72.3 3.0 %collective-permute-done.8 = f32[2,16]{1,0:T(2,128)S(1)} collective-permute-done((f32[2,16]{1,0:T(2,128)S(1)}, f32[2,16]{1,0:T(2,128)S(1)}, u32[]{:S(2)}, u32[]{:S(2)}) %collective-permute-start.8) | collective-permute-done | bytes 160 | tf_op jit(solution)/shard_map/ppermute | solution.py:26
  75.3 0.7 add_bitcast_fusion
  (62 shorter events, 0.6 us)
Async XLA Ops:
  2.5 15.7 %copy-start = (f32[3,128]{1,0:T(4,128)S(1)}, f32[3,128]{1,0:T(4,128)}, u32[]{:S(2)}) copy-start(f32[3,128]{1,0:T(4,128)} %param.16) | copy-start | bytes 4612
  2.7 30.6 %collective-permute-start = (bf16[7,32,2,128]{3,2,1,0:T(2,128)(2,1)S(1)}, bf16[7,32,2,128]{3,2,1,0:T(2,128)(2,1)}, u32[]{:S(2)}, u32[]{:S(2)}) collective-permute-start(bf16[7,32,2,128]{3,2,1,0:T(2,128)(2,1)S(1)} %pad_maximum_fusion.5), channel_id=1, source_target_pairs={{0,1},{1,2},{2,3},{3,4},{4,5},{5,6},{6,7},{7,8},{8,9},{9,10},{10,1... | collective-permute-start | bytes 344072 | tf_op jit(solution)/shard_map/ppermute | solution.py:131
  12.0 22.0 %collective-permute-start.1 = (bf16[7,32,2,128]{3,2,1,0:T(2,128)(2,1)S(1)}, bf16[7,32,2,128]{3,2,1,0:T(2,128)(2,1)}, u32[]{:S(2)}, u32[]{:S(2)}) collective-permute-start(bf16[7,32,2,128]{3,2,1,0:T(2,128)(2,1)S(1)} %pad_maximum_fusion.6), channel_id=1, source_target_pairs={{1,0},{2,1},{3,2},{4,3},{5,4},{6,5},{7,6},{8,7},{9,8},{10,9},{11,1... | collective-permute-start | bytes 344072 | tf_op jit(solution)/shard_map/ppermute | solution.py:134
  19.3 8.0 %collective-permute-start.3 = (bf16[7,32,16,2]{1,2,3,0:T(8,128)(2,1)S(1)}, bf16[7,32,16,2]{1,2,3,0:T(8,128)(2,1)S(1)}, u32[]{:S(2)}, u32[]{:S(2)}) collective-permute-start(bf16[7,32,16,2]{1,2,3,0:T(8,128)(2,1)S(1)} %pad_maximum_fusion.8), channel_id=1, source_target_pairs={{0,16},{16,32},{32,48},{1,17},{17,33},{33,49},{2,18},{18,34},{34,5... | collective-permute-start | bytes 43016 | tf_op jit(solution)/shard_map/ppermute | solution.py:131
  22.3 2.3 %copy-start.8 = (s32[8,2]{0,1:T(2,128)S(1)}, s32[8,2]{0,1:T(2,128)}, u32[]{:S(2)}) copy-start(s32[8,2]{0,1:T(2,128)} %param.19) | copy-start | bytes 196
  22.3 4.2 %copy-start.3 = (f32[3,32]{1,0:T(4,128)S(1)}, f32[3,32]{1,0:T(4,128)}, u32[]{:S(2)}) copy-start(f32[3,32]{1,0:T(4,128)} %param.18) | copy-start | bytes 1156
  22.4 4.3 %copy-start.9 = (pred[34,4]{0,1:T(4,128)(4,1)S(1)}, pred[34,4]{0,1:T(4,128)(4,1)}, u32[]{:S(2)}) copy-start(pred[34,4]{0,1:T(4,128)(4,1)} %constant.79.clone) | copy-start | bytes 412
  22.4 4.3 %copy-start.10 = (pred[34,4]{0,1:T(4,128)(4,1)S(1)}, pred[34,4]{0,1:T(4,128)(4,1)}, u32[]{:S(2)}) copy-start(pred[34,4]{0,1:T(4,128)(4,1)} %constant.78.clone) | copy-start | bytes 412
  22.4 4.3 %copy-start.11 = (pred[34,4]{0,1:T(4,128)(4,1)S(1)}, pred[34,4]{0,1:T(4,128)(4,1)}, u32[]{:S(2)}) copy-start(pred[34,4]{0,1:T(4,128)(4,1)} %constant.77.clone) | copy-start | bytes 412
  23.2 6.5 %collective-permute-start.2 = (bf16[7,32,16,2]{1,2,3,0:T(8,128)(2,1)S(1)}, bf16[7,32,16,2]{1,2,3,0:T(8,128)(2,1)S(1)}, u32[]{:S(2)}, u32[]{:S(2)}) collective-permute-start(bf16[7,32,16,2]{1,2,3,0:T(8,128)(2,1)S(1)} %pad_maximum_fusion.7), channel_id=1, source_target_pairs={{16,0},{32,16},{48,32},{17,1},{33,17},{49,33},{18,2},{34,18},{50,3... | collective-permute-start | bytes 43016 | tf_op jit(solution)/shard_map/ppermute | solution.py:134
  29.8 4.9 %copy-start.1 = (f32[3,16]{1,0:T(4,128)S(1)}, f32[3,16]{1,0:T(4,128)}, u32[]{:S(2)}) copy-start(f32[3,16]{1,0:T(4,128)} %param.17) | copy-start | bytes 580
  42.8 1.9 %copy-start.5 = (pred[18,6]{0,1:T(8,128)(4,1)S(1)}, pred[18,6]{0,1:T(8,128)(4,1)}, u32[]{:S(2)}) copy-start(pred[18,6]{0,1:T(8,128)(4,1)} %constant.82.clone) | copy-start | bytes 328
  42.9 1.9 %copy-start.6 = (pred[18,6]{0,1:T(8,128)(4,1)S(1)}, pred[18,6]{0,1:T(8,128)(4,1)}, u32[]{:S(2)}) copy-start(pred[18,6]{0,1:T(8,128)(4,1)} %constant.81.clone) | copy-start | bytes 328
  42.9 1.9 %copy-start.7 = (pred[18,6]{0,1:T(8,128)(4,1)S(1)}, pred[18,6]{0,1:T(8,128)(4,1)}, u32[]{:S(2)}) copy-start(pred[18,6]{0,1:T(8,128)(4,1)} %constant.80.clone) | copy-start | bytes 328
  42.9 12.8 %copy-start.4 = (s32[8]{0:T(128)S(1)}, s32[8]{0:T(128)}, u32[]{:S(2)}) copy-start(s32[8]{0:T(128)} %param.20) | copy-start | bytes 100
  42.9 27.9 %copy-start.2 = (f32[4]{0:T(128)S(1)}, f32[4]{0:T(128)}, u32[]{:S(2)}) copy-start(f32[4]{0:T(128)} %get-tuple-element.57) | copy-start | bytes 52
  45.0 12.6 %collective-permute-start.4 = (f32[4,2,20]{2,1,0:T(2,128)S(1)}, f32[4,2,20]{2,1,0:T(2,128)S(1)}, u32[]{:S(2)}, u32[]{:S(2)}) collective-permute-start(f32[4,2,20]{2,1,0:T(2,128)S(1)} %get-tuple-element.21), channel_id=1, source_target_pairs={{0,1},{1,2},{2,3},{3,4},{4,5},{5,6},{6,7},{7,8},{8,9},{9,10},{10,1... | collective-permute-start | bytes 1928 | tf_op jit(solution)/shard_map/ppermute | solution.py:15
  50.3 10.3 %collective-permute-start.5 = (f32[4,2,20]{2,1,0:T(2,128)S(1)}, f32[4,2,20]{2,1,0:T(2,128)S(1)}, u32[]{:S(2)}, u32[]{:S(2)}) collective-permute-start(f32[4,2,20]{2,1,0:T(2,128)S(1)} %get-tuple-element.22), channel_id=1, source_target_pairs={{1,0},{2,1},{3,2},{4,3},{5,4},{6,5},{7,6},{8,7},{9,8},{10,9},{11,1... | collective-permute-start | bytes 1928 | tf_op jit(solution)/shard_map/ppermute | solution.py:18
  60.7 4.2 %collective-permute-start.6 = (f32[4,2,2]{2,1,0:T(2,128)S(1)}, f32[4,2,2]{2,1,0:T(2,128)S(1)}, u32[]{:S(2)}, u32[]{:S(2)}) collective-permute-start(f32[4,2,2]{2,1,0:T(2,128)S(1)} %get-tuple-element.26), channel_id=1, source_target_pairs={{0,16},{16,32},{32,48},{1,17},{17,33},{33,49},{2,18},{18,34},{34,5... | collective-permute-start | bytes 200 | tf_op jit(solution)/shard_map/ppermute | solution.py:15
  63.5 7.3 %collective-permute-start.7 = (f32[4,2,2]{2,1,0:T(2,128)S(1)}, f32[4,2,2]{2,1,0:T(2,128)S(1)}, u32[]{:S(2)}, u32[]{:S(2)}) collective-permute-start(f32[4,2,2]{2,1,0:T(2,128)S(1)} %get-tuple-element.27), channel_id=1, source_target_pairs={{16,0},{32,16},{48,32},{17,1},{33,17},{49,33},{18,2},{34,18},{50,3... | collective-permute-start | bytes 200 | tf_op jit(solution)/shard_map/ppermute | solution.py:18
  70.9 1.4 %collective-permute-start.9 = (f32[2,16]{1,0:T(2,128)S(1)}, f32[2,16]{1,0:T(2,128)S(1)}, u32[]{:S(2)}, u32[]{:S(2)}) collective-permute-start(f32[2,16]{1,0:T(2,128)S(1)} %broadcast_multiply_fusion), channel_id=1, source_target_pairs={{64,0},{128,64},{192,128},{256,192},{320,256},{384,320},{448,384},... | collective-permute-start | bytes 392 | tf_op jit(solution)/shard_map/ppermute | solution.py:26
  71.0 4.3 %collective-permute-start.8 = (f32[2,16]{1,0:T(2,128)S(1)}, f32[2,16]{1,0:T(2,128)S(1)}, u32[]{:S(2)}, u32[]{:S(2)}) collective-permute-start(f32[2,16]{1,0:T(2,128)S(1)} %broadcast_multiply_fusion.1), channel_id=1, source_target_pairs={{448,0},{0,64},{64,128},{128,192},{192,256},{256,320},{320,384},{3... | collective-permute-start | bytes 392 | tf_op jit(solution)/shard_map/ppermute | solution.py:26
